TPU v7x, 128 devices: a whole 4x4x4 slice. The times are simulated.
128 devices in a mesh: section: 4 (over z), expert: 32 (over y, x, core).
Axes of the slice: x: 4, y: 4, z: 4, core: 2. Of those that a mesh axis runs over, the one named last changes fastest.
Arguments:
- hidden_in: bfloat16 [4, 6144, 2048], P('section', 'expert'), may hold values from -6 to 6
- out_grad: bfloat16 [4, 6144, 2048], P('section', 'expert'), may hold values from -1.5 to 1.5
- routes: int32 [4, 6144, 2], P('section', 'expert'), may hold values from 0 to 31, all different within a row; in each aligned block of 192 rows (0 to 191, 192 to 383, ..., all dimensions but the last counted through in order) at most 24 rows name the same one
- mixing: bfloat16 [4, 6144, 2], P('section', 'expert'), may hold values from 0.099609375 to 0.8984375
- w_gate: bfloat16 [4, 32, 2048, 768], P('section', 'expert'), may hold values from -0.125 to 0.125
- w_up: bfloat16 [4, 32, 2048, 768], P('section', 'expert'), may hold values from -0.125 to 0.125
- w_down: bfloat16 [4, 32, 768, 2048], P('section', 'expert'), may hold values from -0.21875 to 0.21875
Outputs:
- grad_gate: bfloat16 [4, 32, 2048, 768], P('section', 'expert')
- grad_up: bfloat16 [4, 32, 2048, 768], P('section', 'expert')
- grad_down: bfloat16 [4, 32, 768, 2048], P('section', 'expert')
- handed: bfloat16 [4, 6144, 2048], P('section', 'expert')
- prob_grad: bfloat16 [4, 6144, 2], P('section', 'expert')
Inputs may be any that keep to these rules, and one draw needn't show every extreme that they name: `routes`: the two experts of a token differ. Among the 192 tokens of one device (aligned blocks of the token dimension), no expert is named more than 24 times, and in some block some expert is named exactly 24 times; every expert is named by some token of each section.
All inputs are finite; a program needn't handle non-finite values.
Results may differ from a plain program's by a relative error of at most 0.012.
Values may be sent and summed in bfloat16 or wider, within the bound.
No kernel may reach another device: no remote copies, remote signals or barrier semaphores. Data moves between devices by JAX's collectives and lax.ppermute only.
A program may use at most 128 MiB of HBM per device.

v0:
```python
import jax
import jax.numpy as jnp
from jax import lax
from jax.sharding import PartitionSpec as P


def shifted(block, axis, distance):
    devices = range(lax.axis_size(axis))
    route = [(i - distance, i) for i in devices if i - distance in devices]
    return lax.ppermute(block, axis, route)


def contract_rows(left, right):
    return lax.dot_general(
        left, right, (((0,), (0,)), ((), ())), preferred_element_type=jnp.float32
    )


def contract_cols(left, right):
    return lax.dot_general(
        left, right, (((1,), (1,)), ((), ())), preferred_element_type=jnp.float32
    )


def exchange(block, groups):
    lead = block.shape[0]
    parted = block.reshape((groups, lead // groups) + block.shape[1:])
    moved = lax.all_to_all(parted, "expert", split_axis=0, concat_axis=0, tiled=True)
    return moved.reshape(block.shape)


def per_device(hidden_in, out_grad, routes, mixing, w_gate, w_up, w_down):
    tokens_in = hidden_in[0]
    grads_in = out_grad[0]
    groups = lax.axis_size("expert")
    tok_rows = tokens_in.shape[0]
    capacity = 4 * tok_rows // groups
    slot_total = groups * capacity
    gate_mat = w_gate[0, 0]
    up_mat = w_up[0, 0]
    down_mat = w_down[0, 0]

    chosen = routes[0].reshape(-1)
    onehot = (chosen[:, None] == jnp.arange(groups, dtype=jnp.int32)[None, :]).astype(jnp.int32)
    slot_rank = jnp.sum(onehot * (jnp.cumsum(onehot, axis=0) - 1), axis=1)
    slot_index = (chosen * capacity + slot_rank).reshape(tok_rows, 2)
    slot_ids = jnp.arange(slot_total, dtype=jnp.int32)
    hit = slot_index[None, :, :] == slot_ids[:, None, None]
    pick = jnp.any(hit, axis=2).astype(jnp.bfloat16)
    slot_weight = jnp.sum(
        jnp.where(hit, mixing[0][None, :, :].astype(jnp.float32), 0.0), axis=(1, 2)
    ).astype(jnp.bfloat16)

    send_rows = jnp.dot(pick, tokens_in, preferred_element_type=jnp.float32).astype(jnp.bfloat16)
    send_grads = jnp.dot(pick, grads_in, preferred_element_type=jnp.float32).astype(jnp.bfloat16)

    rows_in = exchange(send_rows, groups)
    weight_in = exchange(slot_weight, groups)
    grad_rows = exchange(send_grads, groups)

    pre_gate = jnp.dot(rows_in, gate_mat, preferred_element_type=jnp.float32)
    pre_up = jnp.dot(rows_in, up_mat, preferred_element_type=jnp.float32)
    sigmoid_g = jax.nn.sigmoid(pre_gate)
    silu_g = pre_gate * sigmoid_g
    act_rows = (silu_g * pre_up).astype(jnp.bfloat16)
    expert_out = jnp.dot(act_rows, down_mat, preferred_element_type=jnp.float32).astype(
        jnp.bfloat16
    )
    prob_part = jnp.sum(
        grad_rows.astype(jnp.float32) * expert_out.astype(jnp.float32), axis=1
    ).astype(jnp.bfloat16)
    scaled = (weight_in.astype(jnp.float32)[:, None] * grad_rows.astype(jnp.float32)).astype(
        jnp.bfloat16
    )
    act_grad = contract_cols(scaled, down_mat)
    gate_pre = (act_grad * pre_up * sigmoid_g * (1.0 + pre_gate * (1.0 - sigmoid_g))).astype(
        jnp.bfloat16
    )
    up_pre = (act_grad * silu_g).astype(jnp.bfloat16)
    in_grad = (contract_cols(gate_pre, gate_mat) + contract_cols(up_pre, up_mat)).astype(
        jnp.bfloat16
    )

    back_grad = exchange(in_grad, groups)
    back_prob = exchange(prob_part, groups)

    grad_down = contract_rows(act_rows, scaled).astype(jnp.bfloat16)
    grad_gate = contract_rows(rows_in, gate_pre).astype(jnp.bfloat16)
    grad_up = contract_rows(rows_in, up_pre).astype(jnp.bfloat16)

    input_grad = (
        grads_in.astype(jnp.float32) + contract_rows(pick, back_grad)
    ).astype(jnp.bfloat16)
    prob_grad = jnp.sum(
        jnp.where(hit, back_prob.astype(jnp.float32)[:, None, None], 0.0), axis=0
    ).astype(jnp.bfloat16)
    handed = shifted(input_grad, "section", -1)
    return (
        grad_gate[None, None],
        grad_up[None, None],
        grad_down[None, None],
        handed[None],
        prob_grad[None],
    )


def solution(mesh):
    placed = (
        P("section", "expert", None),
        P("section", "expert", None),
        P("section", "expert", None),
        P("section", "expert", None),
        P("section", "expert", None, None),
        P("section", "expert", None, None),
        P("section", "expert", None, None),
    )
    return jax.shard_map(
        per_device,
        mesh=mesh,
        in_specs=placed,
        out_specs=(
            P("section", "expert", None, None),
            P("section", "expert", None, None),
            P("section", "expert", None, None),
            P("section", "expert", None),
            P("section", "expert", None),
        ),
        check_vma=False,
    )
```

profile of v0, /device:TPU:0, one launch (start us, length us, event | category | flops | bytes accessed | tf_op | source)
XLA Modules:
  0.0 219.9 jit_solution(5798829784457830035)
XLA Ops:
  4.2 3.8 %convolution_convert_fusion.5 = bf16[768,2048]{1,0:T(8,128)(2,1)} fusion(pred[768,192]{0,1:T(8,128)(4,1)S(1)} %fusion.20, bf16[1,192,2048]{2,1,0:T(8,128)(2,1)} %param.7), kind=kOutput, calls=%fused_computation.12 | convolution fusion | flops 605552640 | bytes 4079616 | tf_op jit(solution)/shard_map/dot_general | solution.py:54
  8.1 7.5 %all-to-all-start = ((bf16[32,24,2048]{2,1,0:T(8,128)(2,1)}), bf16[32,24,2048]{2,1,0:T(8,128)(2,1)}, u32[]{:S(2)}, u32[]{:S(2)}) async-start(bf16[32,24,2048]{2,1,0:T(8,128)(2,1)} %bitcast.90), calls=%async_computation | async-start | bytes 6291456 | tf_op jit(solution)/shard_map/all_to_all | solution.py:28
  15.6 3.8 %convolution_convert_fusion.4 = bf16[768,2048]{1,0:T(8,128)(2,1)} fusion(pred[768,192]{0,1:T(8,128)(4,1)S(1)} %fusion.20, bf16[1,192,2048]{2,1,0:T(8,128)(2,1)} %param.8), kind=kOutput, calls=%fused_computation.11 | convolution fusion | flops 605552640 | bytes 4079616 | tf_op jit(solution)/shard_map/dot_general | solution.py:55
  19.5 38.2 %all-to-all-done = bf16[32,24,2048]{2,1,0:T(8,128)(2,1)} async-done(((bf16[32,24,2048]{2,1,0:T(8,128)(2,1)}), bf16[32,24,2048]{2,1,0:T(8,128)(2,1)}, u32[]{:S(2)}, u32[]{:S(2)}) %all-to-all-start) | async-done | bytes 3145760 | tf_op jit(solution)/shard_map/all_to_all | solution.py:28
  57.6 4.8 %all-to-all-start.2 = ((bf16[32,24,2048]{2,1,0:T(8,128)(2,1)}), bf16[32,24,2048]{2,1,0:T(8,128)(2,1)}, u32[]{:S(2)}, u32[]{:S(2)}) async-start(bf16[32,24,2048]{2,1,0:T(8,128)(2,1)} %bitcast.89), calls=%async_computation.2 | async-start | bytes 6291456 | tf_op jit(solution)/shard_map/all_to_all | solution.py:28
  62.5 5.4 %fusion.5 = f32[768,768]{1,0:T(8,128)S(1)} fusion(bf16[768,2048]{1,0:T(8,128)(2,1)} %bitcast.4, bf16[1,1,2048,768]{3,2,1,0:T(8,128)(2,1)} %param.11), kind=kOutput, calls=%fused_computation.15 | convolution fusion | flops 2415919104 | bytes 8650752 | tf_op jit(solution)/shard_map/dot_general | solution.py:61
  69.3 6.4 %multiply_convert_fusion = (bf16[768,768]{1,0:T(8,128)(2,1)}, f32[768,768]{1,0:T(8,128)}) fusion(f32[768,768]{1,0:T(8,128)S(1)} %fusion.5, bf16[768,2048]{1,0:T(8,128)(2,1)} %bitcast.4, bf16[1,1,2048,768]{3,2,1,0:T(8,128)(2,1)S(1)} %copy-done), kind=kOutput, calls=%fused_computation.28 | convolution fusion | flops 2419458048 | bytes 12189696 | tf_op jit(solution)/shard_map/dot_general | solution.py:62
  75.7 28.8 %all-to-all-done.2 = bf16[32,24,2048]{2,1,0:T(8,128)(2,1)} async-done(((bf16[32,24,2048]{2,1,0:T(8,128)(2,1)}), bf16[32,24,2048]{2,1,0:T(8,128)(2,1)}, u32[]{:S(2)}, u32[]{:S(2)}) %all-to-all-start.2) | async-done | bytes 3145760 | tf_op jit(solution)/shard_map/all_to_all | solution.py:28
  104.5 5.9 %fusion.2 = bf16[768]{0:T(1024)(128)(2,1)S(1)} fusion(bf16[32,24,2048]{2,1,0:T(8,128)(2,1)} %all-to-all-done.2, bf16[768,768]{1,0:T(8,128)(2,1)} %get-tuple-element.9, bf16[1,1,768,2048]{3,2,1,0:T(8,128)(2,1)} %param.13), kind=kOutput, calls=%fused_computation.5 | convolution fusion | flops 2423782656 | bytes 7472640 | tf_op jit(solution)/shard_map/dot_general | solution.py:66
  111.1 3.8 %all-to-all-start.4 = ((bf16[32,1,24]{2,1,0:T(2,128)(2,1)}), bf16[32,1,24]{2,1,0:T(2,128)(2,1)S(1)}, u32[]{:S(2)}, u32[]{:S(2)}) async-start(bf16[32,1,24]{2,1,0:T(2,128)(2,1)} %convert_element_type.168), calls=%async_computation.4 | async-start | bytes 32768 | tf_op jit(solution)/shard_map/all_to_all | solution.py:28
  114.9 7.3 %all-to-all-done.4 = bf16[32,1,24]{2,1,0:T(2,128)(2,1)S(1)} async-done(((bf16[32,1,24]{2,1,0:T(2,128)(2,1)}), bf16[32,1,24]{2,1,0:T(2,128)(2,1)S(1)}, u32[]{:S(2)}, u32[]{:S(2)}) %all-to-all-start.4) | async-done | bytes 1568 | tf_op jit(solution)/shard_map/all_to_all | solution.py:28
  123.4 10.7 %all_to_all.27 = bf16[32,1,24]{2,1,0:T(2,128)(2,1)S(1)} all-to-all(bf16[32,1,24]{2,1,0:T(2,128)(2,1)S(1)} %convert_element_type.167), channel_id=1, replica_groups=mesh['section'=4,'expert'=32] {'expert'}, dimensions={0} | all-to-all | bytes 3072 | tf_op jit(solution)/shard_map/all_to_all | solution.py:28
  134.2 2.6 %fusion = bf16[32,24,2048]{2,1,0:T(8,128)(2,1)S(1)} fusion(bf16[32,24,2048]{2,1,0:T(8,128)(2,1)} %all-to-all-done.2, f32[32,24]{1,0:T(8,128)S(1)} %bitcast.94), kind=kLoop, calls=%fused_computation.3 | loop fusion | flops 4718592 | bytes 6294528 | tf_op jit(solution)/shard_map/convert_element_type | solution.py:72
  137.7 4.9 %multiply_convert_fusion.1 = (bf16[768,768]{1,0:T(8,128)(2,1)S(1)}, bf16[768,768]{1,0:T(8,128)(2,1)S(1)}) fusion(f32[768,768]{1,0:T(8,128)S(1)} %copy-done.8, f32[768,768]{1,0:T(8,128)} %get-tuple-element.10, bf16[768,2048]{1,0:T(8,128)(2,1)S(1)} %bitcast.92, bf16[1,1,768,2048]{3,2,1,0:T(8,128)(2,1)S(1)} %copy-done.3), kind=kOutput, calls=%fused_computation.29 | convolution fusion | flops 2423586816 | bytes 13369344 | tf_op jit(solution)/shard_map/dot_general | solution.py:20
  142.7 2.6 %fusion.3 = f32[768,2048]{1,0:T(8,128)S(1)} fusion(bf16[768,768]{1,0:T(8,128)(2,1)S(1)} %get-tuple-element.8, bf16[1,1,2048,768]{3,2,1,0:T(8,128)(2,1)S(1)} %copy-done.4), kind=kOutput, calls=%fused_computation.13 | convolution fusion | flops 2415919104 | bytes 10616832 | tf_op jit(solution)/shard_map/dot_general | solution.py:20
  145.3 4.0 %add_convert_fusion = bf16[768,2048]{1,0:T(8,128)(2,1)} fusion(f32[768,2048]{1,0:T(8,128)S(1)} %fusion.3, bf16[768,768]{1,0:T(8,128)(2,1)S(1)} %get-tuple-element.7, bf16[1,1,2048,768]{3,2,1,0:T(8,128)(2,1)S(1)} %copy-done), kind=kOutput, calls=%fused_computation.6 | convolution fusion | flops 2419064832 | bytes 13762560 | tf_op jit(solution)/shard_map/dot_general | solution.py:20
  149.4 4.8 %all-to-all-start.3 = ((bf16[32,24,2048]{2,1,0:T(8,128)(2,1)}), bf16[32,24,2048]{2,1,0:T(8,128)(2,1)}, u32[]{:S(2)}, u32[]{:S(2)}) async-start(bf16[32,24,2048]{2,1,0:T(8,128)(2,1)} %bitcast.91), calls=%async_computation.3 | async-start | bytes 6291456 | tf_op jit(solution)/shard_map/all_to_all | solution.py:28
  154.3 6.6 %fusion.14 = bf16[1,1,2048,768]{3,2,1,0:T(8,128)(2,1)} fusion(bf16[768,2048]{1,0:T(8,128)(2,1)} %bitcast.4, bf16[768,768]{1,0:T(8,128)(2,1)} %copy-done.10), kind=kOutput, calls=%fused_computation.24 | convolution fusion | flops 2417491968 | bytes 7471104 | tf_op jit(solution)/shard_map/dot_general | solution.py:14
  160.9 4.1 %fusion.1 = bf16[768,2048]{1,0:T(8,128)(2,1)} fusion(bf16[32,24,2048]{2,1,0:T(8,128)(2,1)} %all-to-all-done.2, f32[768]{0:T(1024)S(1)} %reshape.121), kind=kLoop, calls=%fused_computation.4 | loop fusion | flops 4718592 | bytes 6294528 | tf_op jit(solution)/shard_map/convert_element_type | solution.py:72
  165.0 31.2 %all-to-all-done.3 = bf16[32,24,2048]{2,1,0:T(8,128)(2,1)} async-done(((bf16[32,24,2048]{2,1,0:T(8,128)(2,1)}), bf16[32,24,2048]{2,1,0:T(8,128)(2,1)}, u32[]{:S(2)}, u32[]{:S(2)}) %all-to-all-start.3) | async-done | bytes 3145760 | tf_op jit(solution)/shard_map/all_to_all | solution.py:28
  196.2 3.0 %fusion.16 = bf16[192,2048]{1,0:T(8,128)(2,1)S(1)} fusion(pred[768,192]{0,1:T(8,128)(4,1)S(1)} %fusion.20, bf16[768,2048]{1,0:T(8,128)(2,1)} %bitcast.18, bf16[1,192,2048]{2,1,0:T(8,128)(2,1)} %param.8), kind=kOutput, calls=%fused_computation.27 | convolution fusion | flops 605159424 | bytes 4866048 | tf_op jit(solution)/shard_map/dot_general | solution.py:14
  201.0 6.2 %fusion.13 = bf16[1,1,2048,768]{3,2,1,0:T(8,128)(2,1)} fusion(bf16[768,2048]{1,0:T(8,128)(2,1)} %bitcast.4, bf16[768,768]{1,0:T(8,128)(2,1)S(1)} %copy-done.6), kind=kOutput, calls=%fused_computation.23 | convolution fusion | flops 2417491968 | bytes 7471104 | tf_op jit(solution)/shard_map/dot_general | solution.py:14
  207.2 4.0 %fusion.15 = bf16[1,1,768,2048]{3,2,1,0:T(8,128)(2,1)} fusion(bf16[768,768]{1,0:T(8,128)(2,1)S(1)} %copy-done.9, bf16[768,2048]{1,0:T(8,128)(2,1)S(1)} %copy-done.1), kind=kOutput, calls=%fused_computation.25 | convolution fusion | flops 2417491968 | bytes 7471104 | tf_op jit(solution)/shard_map/dot_general | solution.py:14
  211.2 7.7 %collective-permute-done = bf16[192,2048]{1,0:T(8,128)(2,1)S(1)} collective-permute-done((bf16[192,2048]{1,0:T(8,128)(2,1)S(1)}, bf16[192,2048]{1,0:T(8,128)(2,1)S(1)}, u32[]{:S(2)}, u32[]{:S(2)}) %collective-permute-start) | collective-permute-done | bytes 786464 | tf_op jit(solution)/shard_map/ppermute | solution.py:10
  (45 shorter events, 10.7 us)
Async XLA Ops:
  0.6 68.7 %copy-start = (bf16[1,1,2048,768]{3,2,1,0:T(8,128)(2,1)S(1)}, bf16[1,1,2048,768]{3,2,1,0:T(8,128)(2,1)}, u32[]{:S(2)}) copy-start(bf16[1,1,2048,768]{3,2,1,0:T(8,128)(2,1)} %param.12) | copy-start | bytes 9437188
  8.1 49.5 %all-to-all-start = ((bf16[32,24,2048]{2,1,0:T(8,128)(2,1)}), bf16[32,24,2048]{2,1,0:T(8,128)(2,1)}, u32[]{:S(2)}, u32[]{:S(2)}) async-start(bf16[32,24,2048]{2,1,0:T(8,128)(2,1)} %bitcast.90), calls=%async_computation | async-start | bytes 6291456 | tf_op jit(solution)/shard_map/all_to_all | solution.py:28
  57.6 46.8 %all-to-all-start.2 = ((bf16[32,24,2048]{2,1,0:T(8,128)(2,1)}), bf16[32,24,2048]{2,1,0:T(8,128)(2,1)}, u32[]{:S(2)}, u32[]{:S(2)}) async-start(bf16[32,24,2048]{2,1,0:T(8,128)(2,1)} %bitcast.89), calls=%async_computation.2 | async-start | bytes 6291456 | tf_op jit(solution)/shard_map/all_to_all | solution.py:28
  67.9 1.4 copy-start.7
  104.5 10.5 %copy-start.2 = (bf16[1,192,2]{1,2,0:T(2,128)(2,1)S(1)}, bf16[1,192,2]{1,2,0:T(2,128)(2,1)}, u32[]{:S(2)}) copy-start(bf16[1,192,2]{1,2,0:T(2,128)(2,1)} %param.10) | copy-start | bytes 2308
  111.1 11.1 %all-to-all-start.4 = ((bf16[32,1,24]{2,1,0:T(2,128)(2,1)}), bf16[32,1,24]{2,1,0:T(2,128)(2,1)S(1)}, u32[]{:S(2)}, u32[]{:S(2)}) async-start(bf16[32,1,24]{2,1,0:T(2,128)(2,1)} %convert_element_type.168), calls=%async_computation.4 | async-start | bytes 32768 | tf_op jit(solution)/shard_map/all_to_all | solution.py:28
  134.2 2.8 %copy-start.3 = (bf16[1,1,768,2048]{3,2,1,0:T(8,128)(2,1)S(1)}, bf16[1,1,768,2048]{3,2,1,0:T(8,128)(2,1)}, u32[]{:S(2)}) copy-start(bf16[1,1,768,2048]{3,2,1,0:T(8,128)(2,1)} %param.13) | copy-start | bytes 9437188
  134.2 3.6 %copy-start.8 = (f32[768,768]{1,0:T(8,128)S(1)}, f32[768,768]{1,0:T(8,128)}, u32[]{:S(2)}) copy-start(f32[768,768]{1,0:T(8,128)} %copy-done.7) | copy-start | bytes 7077892
  137.7 5.0 %copy-start.4 = (bf16[1,1,2048,768]{3,2,1,0:T(8,128)(2,1)S(1)}, bf16[1,1,2048,768]{3,2,1,0:T(8,128)(2,1)}, u32[]{:S(2)}) copy-start(bf16[1,1,2048,768]{3,2,1,0:T(8,128)(2,1)} %param.11) | copy-start | bytes 9437188
  142.7 2.7 %copy-start.5 = (bf16[768,768]{1,0:T(8,128)(2,1)}, bf16[768,768]{1,0:T(8,128)(2,1)S(1)}, u32[]{:S(2)}) copy-start(bf16[768,768]{1,0:T(8,128)(2,1)S(1)} %get-tuple-element.8) | copy-start | bytes 3538948
  142.7 2.7 %copy-start.10 = (bf16[768,768]{1,0:T(8,128)(2,1)}, bf16[768,768]{1,0:T(8,128)(2,1)S(1)}, u32[]{:S(2)}) copy-start(bf16[768,768]{1,0:T(8,128)(2,1)S(1)} %get-tuple-element.7) | copy-start | bytes 3538948
  149.4 46.8 %all-to-all-start.3 = ((bf16[32,24,2048]{2,1,0:T(8,128)(2,1)}), bf16[32,24,2048]{2,1,0:T(8,128)(2,1)}, u32[]{:S(2)}, u32[]{:S(2)}) async-start(bf16[32,24,2048]{2,1,0:T(8,128)(2,1)} %bitcast.91), calls=%async_computation.3 | async-start | bytes 6291456 | tf_op jit(solution)/shard_map/all_to_all | solution.py:28
  196.2 4.8 %copy-start.6 = (bf16[768,768]{1,0:T(8,128)(2,1)S(1)}, bf16[768,768]{1,0:T(8,128)(2,1)}, u32[]{:S(2)}) copy-start(bf16[768,768]{1,0:T(8,128)(2,1)} %copy-done.5) | copy-start | bytes 3538948
  199.2 8.1 %copy-start.1 = (bf16[768,2048]{1,0:T(8,128)(2,1)S(1)}, bf16[768,2048]{1,0:T(8,128)(2,1)}, u32[]{:S(2)}) copy-start(bf16[768,2048]{1,0:T(8,128)(2,1)} %fusion.1) | copy-start | bytes 9437188
  199.2 8.1 %copy-start.9 = (bf16[768,768]{1,0:T(8,128)(2,1)S(1)}, bf16[768,768]{1,0:T(8,128)(2,1)}, u32[]{:S(2)}) copy-start(bf16[768,768]{1,0:T(8,128)(2,1)} %get-tuple-element.9) | copy-start | bytes 3538948
  199.2 19.8 %collective-permute-start = (bf16[192,2048]{1,0:T(8,128)(2,1)S(1)}, bf16[192,2048]{1,0:T(8,128)(2,1)S(1)}, u32[]{:S(2)}, u32[]{:S(2)}) collective-permute-start(bf16[192,2048]{1,0:T(8,128)(2,1)S(1)} %fusion.16), channel_id=1, source_target_pairs={{32,0},{64,32},{96,64},{33,1},{65,33},{97,65},{34,2},{66,34},{98,6... | collective-permute-start | bytes 2359304 | tf_op jit(solution)/shard_map/ppermute | solution.py:10
where the time goes:
time: 220 us
  waiting for transfers between devices  113 us (51%)
  matrix products  56.7 us (26%)
  starting transfers between devices  22.8 us (10%)
  blocking collectives  10.7 us (5%)
  other arithmetic  9.76 us (4%)
  local copies, waits for them, and re-layouts  5.88 us (3%)
    all_to_all x4, waiting for transfers between devices, exchange(): lax.all_to_all(parted, 'expert', split_axis=0, concat_axis=0, tiled=True)  105 us
    all_to_all x4, starting transfers between devices, exchange(): lax.all_to_all(parted, 'expert', split_axis=0, concat_axis=0, tiled=True)  21 us
    dot_general x4, matrix products, contract_rows(): lax.dot_general(left, right, (((0,), (0,)), ((), ())), preferred_element_...  19.8 us
    dot_general x3, matrix products, contract_cols(): lax.dot_general(left, right, (((1,), (1,)), ((), ())), preferred_element_...  11.6 us
    all_to_all x1, blocking collectives, exchange(): lax.all_to_all(parted, 'expert', split_axis=0, concat_axis=0, tiled=True)  10.7 us
    ppermute x1, waiting for transfers between devices, shifted(): return lax.ppermute(block, axis, route)  7.75 us
    convert_element_type x2, other arithmetic, per_device(): (weight_in.astype(jnp.float32)[:, None] * grad_rows.astype(jnp.float32))....  6.74 us
    dot_general x1, matrix products, per_device(): pre_up = jnp.dot(rows_in, up_mat, preferred_element_type=jnp.float32)  6.38 us
  transfers between devices with their start and end apart: 5, of which 5 were waited for; matrix products, arithmetic and copies ran while one was open for 17% of the time, Pallas kernels for 0%

commit v1 on v0

--- a/solution.py
+++ b/solution.py
@@ -29,11 +29,17 @@
     return moved.reshape(block.shape)
 
 
+def side_block(values):
+    lanes = jnp.arange(128, dtype=jnp.int32)[None, :]
+    return jnp.where(lanes == 0, values[:, None], jnp.zeros((), values.dtype))
+
+
 def per_device(hidden_in, out_grad, routes, mixing, w_gate, w_up, w_down):
     tokens_in = hidden_in[0]
     grads_in = out_grad[0]
     groups = lax.axis_size("expert")
     tok_rows = tokens_in.shape[0]
+    model_width = tokens_in.shape[1]
     capacity = 4 * tok_rows // groups
     slot_total = groups * capacity
     gate_mat = w_gate[0, 0]
@@ -47,16 +53,18 @@
     slot_ids = jnp.arange(slot_total, dtype=jnp.int32)
     hit = slot_index[None, :, :] == slot_ids[:, None, None]
     pick = jnp.any(hit, axis=2).astype(jnp.bfloat16)
+
+    send_rows = jnp.dot(pick, tokens_in, preferred_element_type=jnp.float32).astype(jnp.bfloat16)
+    send_grads = jnp.dot(pick, grads_in, preferred_element_type=jnp.float32).astype(jnp.bfloat16)
     slot_weight = jnp.sum(
         jnp.where(hit, mixing[0][None, :, :].astype(jnp.float32), 0.0), axis=(1, 2)
     ).astype(jnp.bfloat16)
-
-    send_rows = jnp.dot(pick, tokens_in, preferred_element_type=jnp.float32).astype(jnp.bfloat16)
-    send_grads = jnp.dot(pick, grads_in, preferred_element_type=jnp.float32).astype(jnp.bfloat16)
+    send_grads = jnp.concatenate([send_grads, side_block(slot_weight)], axis=1)
 
     rows_in = exchange(send_rows, groups)
-    weight_in = exchange(slot_weight, groups)
-    grad_rows = exchange(send_grads, groups)
+    grad_ext = exchange(send_grads, groups)
+    grad_rows = grad_ext[:, :model_width]
+    weight_in = grad_ext[:, model_width]
 
     pre_gate = jnp.dot(rows_in, gate_mat, preferred_element_type=jnp.float32)
     pre_up = jnp.dot(rows_in, up_mat, preferred_element_type=jnp.float32)
@@ -81,8 +89,9 @@
         jnp.bfloat16
     )
 
-    back_grad = exchange(in_grad, groups)
-    back_prob = exchange(prob_part, groups)
+    back_ext = exchange(jnp.concatenate([in_grad, side_block(prob_part)], axis=1), groups)
+    back_grad = back_ext[:, :model_width]
+    back_prob = back_ext[:, model_width]
 
     grad_down = contract_rows(act_rows, scaled).astype(jnp.bfloat16)
     grad_gate = contract_rows(rows_in, gate_pre).astype(jnp.bfloat16)

time: 220 us -> 204 us (0.927)
  blocking collectives: 10.7 us -> 0 us
  starting transfers between devices: 22.8 us -> 19 us
  local copies, waits for them, and re-layouts: 5.88 us -> 3.07 us
    all_to_all x1 -> x0, blocking collectives: 10.7 us -> none  [exchange(): lax.all_to_all(parted, 'expert', split_axis=0, concat_axis=0, tiled=True)]
    convert_element_type x4 -> x0, other arithmetic: 6.81 us -> none  [the longest x2 6.74 us: per_device(): (weight_in.astype(jnp.float32)[:, None] * grad_rows.astype(jnp.float32))....]
    concatenate x0 -> x2, other arithmetic: none -> 4.12 us  [the longest x1 2.09 us: per_device(): jnp.concatenate([in_grad, side_block(prob_part)], axis=1)]
    all_to_all x4 -> x3, starting transfers between devices: 21 us -> 17.7 us  [exchange(): lax.all_to_all(parted, 'expert', split_axis=0, concat_axis=0, tiled=True)]
    all_to_all x4 -> x3, waiting for transfers between devices: 105 us -> 106 us  [exchange(): lax.all_to_all(parted, 'expert', split_axis=0, concat_axis=0, tiled=True)]
  transfers between devices with their start and end apart: 5 -> 4, of which waited for: 5 -> 4; matrix products, arithmetic and copies ran while one was open for 17% -> 16% of each run, Pallas kernels for 0% -> 0%
where the time goes in v1:
time: 204 us; the launch traced here: 203 us
  waiting for transfers between devices  115 us (56%)
  matrix products  55.6 us (27%)
  starting transfers between devices  19 us (9%)
  other arithmetic  9.55 us (5%)
  local copies, waits for them, and re-layouts  3.07 us (2%)
    all_to_all x3, waiting for transfers between devices, exchange(): lax.all_to_all(parted, 'expert', split_axis=0, concat_axis=0, tiled=True)  106 us
    dot_general x4, matrix products, contract_rows(): lax.dot_general(left, right, (((0,), (0,)), ((), ())), preferred_element_...  22 us
    all_to_all x3, starting transfers between devices, exchange(): lax.all_to_all(parted, 'expert', split_axis=0, concat_axis=0, tiled=True)  17.7 us
    dot_general x3, matrix products, contract_cols(): lax.dot_general(left, right, (((1,), (1,)), ((), ())), preferred_element_...  11.1 us
    ppermute x1, waiting for transfers between devices, shifted(): return lax.ppermute(block, axis, route)  9.58 us
    dot_general x1, matrix products, per_device(): pre_gate = jnp.dot(rows_in, gate_mat, preferred_element_type=jnp.float32)  6.85 us
    dot_general x1, matrix products, per_device(): pre_up = jnp.dot(rows_in, up_mat, preferred_element_type=jnp.float32)  5.28 us
    dot_general x1, matrix products, per_device(): jnp.dot(act_rows, down_mat, preferred_element_type=jnp.float32)  4.35 us
  transfers between devices with their start and end apart: 4, of which 4 were waited for; matrix products, arithmetic and copies ran while one was open for 16% of the time, Pallas kernels for 0%

profile of v1, /device:TPU:0, one launch (start us, length us, event | category | flops | bytes accessed | tf_op | source)
XLA Modules:
  0.0 203.5 jit_solution(6276458681824501485)
XLA Ops:
  4.2 3.8 %convolution_convert_fusion.5 = bf16[768,2048]{1,0:T(8,128)(2,1)} fusion(pred[768,192]{0,1:T(8,128)(4,1)S(1)} %fusion.26, bf16[1,192,2048]{2,1,0:T(8,128)(2,1)} %param.7), kind=kOutput, calls=%fused_computation.10 | convolution fusion | flops 605552640 | bytes 4079616 | tf_op jit(solution)/shard_map/dot_general | solution.py:57
  8.1 7.7 %all-to-all-start = ((bf16[32,24,2048]{2,1,0:T(8,128)(2,1)}), bf16[32,24,2048]{2,1,0:T(8,128)(2,1)}, u32[]{:S(2)}, u32[]{:S(2)}) async-start(bf16[32,24,2048]{2,1,0:T(8,128)(2,1)} %bitcast.78), calls=%async_computation | async-start | bytes 6291456 | tf_op jit(solution)/shard_map/all_to_all | solution.py:28
  16.2 2.2 %convolution_convert_fusion.4 = bf16[768,2048]{1,0:T(8,128)(2,1)S(1)} fusion(pred[768,192]{0,1:T(8,128)(4,1)S(1)} %fusion.26, bf16[1,192,2048]{2,1,0:T(8,128)(2,1)} %param.8), kind=kOutput, calls=%fused_computation.9 | convolution fusion | flops 605552640 | bytes 4079616 | tf_op jit(solution)/shard_map/dot_general | solution.py:58
  18.3 2.0 %pad_maximum_fusion = bf16[768,2176]{1,0:T(8,128)(2,1)} fusion(bf16[768,128]{1,0:T(8,128)(2,1)S(1)} %broadcast_select_fusion.1, bf16[768,2048]{1,0:T(8,128)(2,1)S(1)} %convolution_convert_fusion.4), kind=kLoop, calls=%fused_computation.11 | loop fusion | flops 6684672 | bytes 6684672 | tf_op jit(solution)/shard_map/concatenate | solution.py:62
  20.4 37.4 %all-to-all-done = bf16[32,24,2048]{2,1,0:T(8,128)(2,1)} async-done(((bf16[32,24,2048]{2,1,0:T(8,128)(2,1)}), bf16[32,24,2048]{2,1,0:T(8,128)(2,1)}, u32[]{:S(2)}, u32[]{:S(2)}) %all-to-all-start) | async-done | bytes 3145760 | tf_op jit(solution)/shard_map/all_to_all | solution.py:28
  57.8 5.0 %all-to-all-start.1 = ((bf16[32,24,2176]{2,1,0:T(8,128)(2,1)}), bf16[32,24,2176]{2,1,0:T(8,128)(2,1)}, u32[]{:S(2)}, u32[]{:S(2)}) async-start(bf16[32,24,2176]{2,1,0:T(8,128)(2,1)} %bitcast.76), calls=%async_computation.1 | async-start | bytes 6684672 | tf_op jit(solution)/shard_map/all_to_all | solution.py:28
  62.8 6.8 %fusion.6 = f32[768,768]{1,0:T(8,128)} fusion(bf16[768,2048]{1,0:T(8,128)(2,1)} %bitcast.4, bf16[1,1,2048,768]{3,2,1,0:T(8,128)(2,1)} %param.11), kind=kOutput, calls=%fused_computation.17 | convolution fusion | flops 2415919104 | bytes 8650752 | tf_op jit(solution)/shard_map/dot_general | solution.py:69
  69.6 37.2 %all-to-all-done.1 = bf16[32,24,2176]{2,1,0:T(8,128)(2,1)} async-done(((bf16[32,24,2176]{2,1,0:T(8,128)(2,1)}), bf16[32,24,2176]{2,1,0:T(8,128)(2,1)}, u32[]{:S(2)}, u32[]{:S(2)}) %all-to-all-start.1) | async-done | bytes 3342368 | tf_op jit(solution)/shard_map/all_to_all | solution.py:28
  106.8 1.1 convert_reduce_fusion.1
  107.9 5.6 %fusion.12 = f32[768,768]{1,0:T(8,128)S(1)} fusion(bf16[1,1,768,2048]{3,2,1,0:T(8,128)(2,1)} %param.13, f32[768]{0:T(1024)S(1)} %convert_reduce_fusion.1, bf16[768,2176]{1,0:T(8,128)(2,1)} %bitcast.8), kind=kOutput, calls=%fused_computation.23 | convolution fusion | flops 2420637696 | bytes 8653824 | tf_op jit(solution)/shard_map/dot_general | solution.py:20
  113.6 5.3 %multiply_convert_fusion = (bf16[768,768]{1,0:T(8,128)(2,1)S(1)}, bf16[768,768]{1,0:T(8,128)(2,1)S(1)}, bf16[768,768]{1,0:T(8,128)(2,1)S(1)}) fusion(f32[768,768]{1,0:T(8,128)S(1)} %copy-done.6, f32[768,768]{1,0:T(8,128)S(1)} %fusion.12, bf16[768,2048]{1,0:T(8,128)(2,1)} %bitcast.4, bf16[1,1,2048,768]{3,2,1,0:T(8,128)(2,1)S(1)} %copy-done), kind=kOutput, calls=%fused_computation.30 | convolution fusion | flops 2424766464 | bytes 14548992 | tf_op jit(solution)/shard_map/dot_general | solution.py:70
  118.9 2.6 %fusion.4 = f32[768,2048]{1,0:T(8,128)S(1)} fusion(bf16[768,768]{1,0:T(8,128)(2,1)S(1)} %get-tuple-element.6, bf16[1,1,2048,768]{3,2,1,0:T(8,128)(2,1)S(1)} %copy-done.2), kind=kOutput, calls=%fused_computation.15 | convolution fusion | flops 2415919104 | bytes 10616832 | tf_op jit(solution)/shard_map/dot_general | solution.py:20
  122.0 4.3 %fusion.1 = bf16[768]{0:T(1024)(128)(2,1)S(1)} fusion(bf16[768,2176]{1,0:T(8,128)(2,1)} %bitcast.8, bf16[768,768]{1,0:T(8,128)(2,1)S(1)} %get-tuple-element.5, bf16[1,1,768,2048]{3,2,1,0:T(8,128)(2,1)S(1)} %copy-done.3), kind=kOutput, calls=%fused_computation.3 | convolution fusion | flops 2423782656 | bytes 7472640 | tf_op jit(solution)/shard_map/dot_general | solution.py:74
  126.6 2.9 %add_convert_fusion = bf16[768,2048]{1,0:T(8,128)(2,1)S(1)} fusion(f32[768,2048]{1,0:T(8,128)S(1)} %fusion.4, bf16[768,768]{1,0:T(8,128)(2,1)S(1)} %get-tuple-element.7, bf16[1,1,2048,768]{3,2,1,0:T(8,128)(2,1)S(1)} %copy-done), kind=kOutput, calls=%fused_computation.4 | convolution fusion | flops 2419064832 | bytes 13762560 | tf_op jit(solution)/shard_map/dot_general | solution.py:20
  129.5 2.1 %pad_maximum_fusion.1 = bf16[768,2176]{1,0:T(8,128)(2,1)} fusion(bf16[768,128]{1,0:T(8,128)(2,1)S(1)} %broadcast_select_fusion, bf16[768,2048]{1,0:T(8,128)(2,1)S(1)} %add_convert_fusion), kind=kLoop, calls=%fused_computation.12 | loop fusion | flops 6684672 | bytes 6684672 | tf_op jit(solution)/shard_map/concatenate | solution.py:92
  131.5 5.0 %all-to-all-start.2 = ((bf16[32,24,2176]{2,1,0:T(8,128)(2,1)}), bf16[32,24,2176]{2,1,0:T(8,128)(2,1)}, u32[]{:S(2)}, u32[]{:S(2)}) async-start(bf16[32,24,2176]{2,1,0:T(8,128)(2,1)} %bitcast.77), calls=%async_computation.2 | async-start | bytes 6684672 | tf_op jit(solution)/shard_map/all_to_all | solution.py:28
  136.6 6.7 %fusion.15 = bf16[1,1,2048,768]{3,2,1,0:T(8,128)(2,1)} fusion(bf16[768,2048]{1,0:T(8,128)(2,1)} %bitcast.4, bf16[768,768]{1,0:T(8,128)(2,1)} %copy-done.9), kind=kOutput, calls=%fused_computation.26 | convolution fusion | flops 2417491968 | bytes 7471104 | tf_op jit(solution)/shard_map/dot_general | solution.py:14
  143.3 6.1 %fusion.16 = bf16[1,1,768,2048]{3,2,1,0:T(8,128)(2,1)} fusion(bf16[768,768]{1,0:T(8,128)(2,1)S(1)} %copy-done.8, f32[768]{0:T(1024)S(1)} %convert_reduce_fusion.1, bf16[768,2176]{1,0:T(8,128)(2,1)} %bitcast.8), kind=kOutput, calls=%fused_computation.27 | convolution fusion | flops 2422210560 | bytes 7474176 | tf_op jit(solution)/shard_map/dot_general | solution.py:14
  149.4 31.2 %all-to-all-done.2 = bf16[32,24,2176]{2,1,0:T(8,128)(2,1)} async-done(((bf16[32,24,2176]{2,1,0:T(8,128)(2,1)}), bf16[32,24,2176]{2,1,0:T(8,128)(2,1)}, u32[]{:S(2)}, u32[]{:S(2)}) %all-to-all-start.2) | async-done | bytes 3342368 | tf_op jit(solution)/shard_map/all_to_all | solution.py:28
  180.6 3.0 %fusion.20 = bf16[192,2048]{1,0:T(8,128)(2,1)S(1)} fusion(pred[768,192]{0,1:T(8,128)(4,1)S(1)} %fusion.26, bf16[768,2176]{1,0:T(8,128)(2,1)} %bitcast.16, bf16[1,192,2048]{2,1,0:T(8,128)(2,1)} %param.8), kind=kOutput, calls=%fused_computation.29 | convolution fusion | flops 605159424 | bytes 4866048 | tf_op jit(solution)/shard_map/dot_general | solution.py:14
  183.5 1.3 collective-permute-start
  184.9 6.2 %fusion.14 = bf16[1,1,2048,768]{3,2,1,0:T(8,128)(2,1)} fusion(bf16[768,2048]{1,0:T(8,128)(2,1)} %bitcast.4, bf16[768,768]{1,0:T(8,128)(2,1)S(1)} %copy-done.5), kind=kOutput, calls=%fused_computation.25 | convolution fusion | flops 2417491968 | bytes 7471104 | tf_op jit(solution)/shard_map/dot_general | solution.py:14
  191.1 1.1 convert_reduce_fusion
  193.0 9.6 %collective-permute-done = bf16[192,2048]{1,0:T(8,128)(2,1)S(1)} collective-permute-done((bf16[192,2048]{1,0:T(8,128)(2,1)S(1)}, bf16[192,2048]{1,0:T(8,128)(2,1)S(1)}, u32[]{:S(2)}, u32[]{:S(2)}) %collective-permute-start) | collective-permute-done | bytes 786464 | tf_op jit(solution)/shard_map/ppermute | solution.py:10
  (39 shorter events, 6.4 us)
Async XLA Ops:
  0.6 112.9 %copy-start = (bf16[1,1,2048,768]{3,2,1,0:T(8,128)(2,1)S(1)}, bf16[1,1,2048,768]{3,2,1,0:T(8,128)(2,1)}, u32[]{:S(2)}) copy-start(bf16[1,1,2048,768]{3,2,1,0:T(8,128)(2,1)} %param.12) | copy-start | bytes 9437188
  8.1 7.7 %copy-start.1 = (bf16[1,192,2]{1,2,0:T(2,128)(2,1)S(1)}, bf16[1,192,2]{1,2,0:T(2,128)(2,1)}, u32[]{:S(2)}) copy-start(bf16[1,192,2]{1,2,0:T(2,128)(2,1)} %param.10) | copy-start | bytes 2308
  8.1 49.7 %all-to-all-start = ((bf16[32,24,2048]{2,1,0:T(8,128)(2,1)}), bf16[32,24,2048]{2,1,0:T(8,128)(2,1)}, u32[]{:S(2)}, u32[]{:S(2)}) async-start(bf16[32,24,2048]{2,1,0:T(8,128)(2,1)} %bitcast.78), calls=%async_computation | async-start | bytes 6291456 | tf_op jit(solution)/shard_map/all_to_all | solution.py:28
  57.8 49.0 %all-to-all-start.1 = ((bf16[32,24,2176]{2,1,0:T(8,128)(2,1)}), bf16[32,24,2176]{2,1,0:T(8,128)(2,1)}, u32[]{:S(2)}, u32[]{:S(2)}) async-start(bf16[32,24,2176]{2,1,0:T(8,128)(2,1)} %bitcast.76), calls=%async_computation.1 | async-start | bytes 6684672 | tf_op jit(solution)/shard_map/all_to_all | solution.py:28
  107.9 5.7 %copy-start.6 = (f32[768,768]{1,0:T(8,128)S(1)}, f32[768,768]{1,0:T(8,128)}, u32[]{:S(2)}) copy-start(f32[768,768]{1,0:T(8,128)} %fusion.6) | copy-start | bytes 7077892
  113.5 5.3 %copy-start.2 = (bf16[1,1,2048,768]{3,2,1,0:T(8,128)(2,1)S(1)}, bf16[1,1,2048,768]{3,2,1,0:T(8,128)(2,1)}, u32[]{:S(2)}) copy-start(bf16[1,1,2048,768]{3,2,1,0:T(8,128)(2,1)} %param.11) | copy-start | bytes 9437188
  118.8 2.7 %copy-start.4 = (bf16[768,768]{1,0:T(8,128)(2,1)}, bf16[768,768]{1,0:T(8,128)(2,1)S(1)}, u32[]{:S(2)}) copy-start(bf16[768,768]{1,0:T(8,128)(2,1)S(1)} %get-tuple-element.6) | copy-start | bytes 3538948
  118.9 2.7 %copy-start.7 = (bf16[768,768]{1,0:T(8,128)(2,1)}, bf16[768,768]{1,0:T(8,128)(2,1)S(1)}, u32[]{:S(2)}) copy-start(bf16[768,768]{1,0:T(8,128)(2,1)S(1)} %get-tuple-element.5) | copy-start | bytes 3538948
  118.9 7.7 %copy-start.9 = (bf16[768,768]{1,0:T(8,128)(2,1)}, bf16[768,768]{1,0:T(8,128)(2,1)S(1)}, u32[]{:S(2)}) copy-start(bf16[768,768]{1,0:T(8,128)(2,1)S(1)} %get-tuple-element.7) | copy-start | bytes 3538948
  118.9 3.1 %copy-start.3 = (bf16[1,1,768,2048]{3,2,1,0:T(8,128)(2,1)S(1)}, bf16[1,1,768,2048]{3,2,1,0:T(8,128)(2,1)}, u32[]{:S(2)}) copy-start(bf16[1,1,768,2048]{3,2,1,0:T(8,128)(2,1)} %param.13) | copy-start | bytes 9437188
  131.5 49.0 %all-to-all-start.2 = ((bf16[32,24,2176]{2,1,0:T(8,128)(2,1)}), bf16[32,24,2176]{2,1,0:T(8,128)(2,1)}, u32[]{:S(2)}, u32[]{:S(2)}) async-start(bf16[32,24,2176]{2,1,0:T(8,128)(2,1)} %bitcast.77), calls=%async_computation.2 | async-start | bytes 6684672 | tf_op jit(solution)/shard_map/all_to_all | solution.py:28
  136.6 6.7 %copy-start.8 = (bf16[768,768]{1,0:T(8,128)(2,1)S(1)}, bf16[768,768]{1,0:T(8,128)(2,1)}, u32[]{:S(2)}) copy-start(bf16[768,768]{1,0:T(8,128)(2,1)} %copy-done.7) | copy-start | bytes 3538948
  180.6 4.3 %copy-start.5 = (bf16[768,768]{1,0:T(8,128)(2,1)S(1)}, bf16[768,768]{1,0:T(8,128)(2,1)}, u32[]{:S(2)}) copy-start(bf16[768,768]{1,0:T(8,128)(2,1)} %copy-done.4) | copy-start | bytes 3538948
  183.5 19.1 %collective-permute-start = (bf16[192,2048]{1,0:T(8,128)(2,1)S(1)}, bf16[192,2048]{1,0:T(8,128)(2,1)S(1)}, u32[]{:S(2)}, u32[]{:S(2)}) collective-permute-start(bf16[192,2048]{1,0:T(8,128)(2,1)S(1)} %fusion.20), channel_id=1, source_target_pairs={{32,0},{64,32},{96,64},{33,1},{65,33},{97,65},{34,2},{66,34},{98,6... | collective-permute-start | bytes 2359304 | tf_op jit(solution)/shard_map/ppermute | solution.py:10

commit v2 on v1

--- a/solution.py
+++ b/solution.py
@@ -34,38 +34,9 @@
     return jnp.where(lanes == 0, values[:, None], jnp.zeros((), values.dtype))
 
 
-def per_device(hidden_in, out_grad, routes, mixing, w_gate, w_up, w_down):
-    tokens_in = hidden_in[0]
-    grads_in = out_grad[0]
-    groups = lax.axis_size("expert")
-    tok_rows = tokens_in.shape[0]
-    model_width = tokens_in.shape[1]
-    capacity = 4 * tok_rows // groups
-    slot_total = groups * capacity
-    gate_mat = w_gate[0, 0]
-    up_mat = w_up[0, 0]
-    down_mat = w_down[0, 0]
-
-    chosen = routes[0].reshape(-1)
-    onehot = (chosen[:, None] == jnp.arange(groups, dtype=jnp.int32)[None, :]).astype(jnp.int32)
-    slot_rank = jnp.sum(onehot * (jnp.cumsum(onehot, axis=0) - 1), axis=1)
-    slot_index = (chosen * capacity + slot_rank).reshape(tok_rows, 2)
-    slot_ids = jnp.arange(slot_total, dtype=jnp.int32)
-    hit = slot_index[None, :, :] == slot_ids[:, None, None]
-    pick = jnp.any(hit, axis=2).astype(jnp.bfloat16)
-
-    send_rows = jnp.dot(pick, tokens_in, preferred_element_type=jnp.float32).astype(jnp.bfloat16)
-    send_grads = jnp.dot(pick, grads_in, preferred_element_type=jnp.float32).astype(jnp.bfloat16)
-    slot_weight = jnp.sum(
-        jnp.where(hit, mixing[0][None, :, :].astype(jnp.float32), 0.0), axis=(1, 2)
-    ).astype(jnp.bfloat16)
-    send_grads = jnp.concatenate([send_grads, side_block(slot_weight)], axis=1)
-
-    rows_in = exchange(send_rows, groups)
-    grad_ext = exchange(send_grads, groups)
+def expert_chunk(rows_in, grad_ext, gate_mat, up_mat, down_mat, model_width):
     grad_rows = grad_ext[:, :model_width]
     weight_in = grad_ext[:, model_width]
-
     pre_gate = jnp.dot(rows_in, gate_mat, preferred_element_type=jnp.float32)
     pre_up = jnp.dot(rows_in, up_mat, preferred_element_type=jnp.float32)
     sigmoid_g = jax.nn.sigmoid(pre_gate)
@@ -88,18 +59,64 @@
     in_grad = (contract_cols(gate_pre, gate_mat) + contract_cols(up_pre, up_mat)).astype(
         jnp.bfloat16
     )
+    back_ext = jnp.concatenate([in_grad, side_block(prob_part)], axis=1)
+    return back_ext, act_rows, scaled, gate_pre, up_pre
 
-    back_ext = exchange(jnp.concatenate([in_grad, side_block(prob_part)], axis=1), groups)
-    back_grad = back_ext[:, :model_width]
-    back_prob = back_ext[:, model_width]
 
-    grad_down = contract_rows(act_rows, scaled).astype(jnp.bfloat16)
-    grad_gate = contract_rows(rows_in, gate_pre).astype(jnp.bfloat16)
-    grad_up = contract_rows(rows_in, up_pre).astype(jnp.bfloat16)
+def per_device(hidden_in, out_grad, routes, mixing, w_gate, w_up, w_down):
+    tokens_in = hidden_in[0]
+    grads_in = out_grad[0]
+    groups = lax.axis_size("expert")
+    tok_rows = tokens_in.shape[0]
+    model_width = tokens_in.shape[1]
+    capacity = 4 * tok_rows // groups
+    slot_total = groups * capacity
+    chunks = 2 if capacity % 2 == 0 else 1
+    sub = capacity // chunks
+    gate_mat = w_gate[0, 0]
+    up_mat = w_up[0, 0]
+    down_mat = w_down[0, 0]
 
-    input_grad = (
-        grads_in.astype(jnp.float32) + contract_rows(pick, back_grad)
-    ).astype(jnp.bfloat16)
+    chosen = routes[0].reshape(-1)
+    onehot = (chosen[:, None] == jnp.arange(groups, dtype=jnp.int32)[None, :]).astype(jnp.int32)
+    slot_rank = jnp.sum(onehot * (jnp.cumsum(onehot, axis=0) - 1), axis=1)
+    slot_index = (chosen * capacity + slot_rank).reshape(tok_rows, 2)
+    slot_ids = jnp.arange(slot_total, dtype=jnp.int32)
+    hit = slot_index[None, :, :] == slot_ids[:, None, None]
+    pick = jnp.any(hit, axis=2).astype(jnp.bfloat16).reshape(groups, capacity, tok_rows)
+    slot_weight = jnp.sum(
+        jnp.where(hit, mixing[0][None, :, :].astype(jnp.float32), 0.0), axis=(1, 2)
+    ).astype(jnp.bfloat16).reshape(groups, capacity)
+
+    picks, backs, saved = [], [], []
+    for c in range(chunks):
+        pick_c = pick[:, c * sub:(c + 1) * sub, :].reshape(groups * sub, tok_rows)
+        weight_c = slot_weight[:, c * sub:(c + 1) * sub].reshape(groups * sub)
+        send_rows = jnp.dot(pick_c, tokens_in, preferred_element_type=jnp.float32).astype(
+            jnp.bfloat16
+        )
+        send_grads = jnp.dot(pick_c, grads_in, preferred_element_type=jnp.float32).astype(
+            jnp.bfloat16
+        )
+        send_grads = jnp.concatenate([send_grads, side_block(weight_c)], axis=1)
+        rows_in = exchange(send_rows, groups)
+        grad_ext = exchange(send_grads, groups)
+        back_ext, act_rows, scaled, gate_pre, up_pre = expert_chunk(
+            rows_in, grad_ext, gate_mat, up_mat, down_mat, model_width
+        )
+        picks.append(pick_c)
+        backs.append(exchange(back_ext, groups))
+        saved.append((rows_in, act_rows, scaled, gate_pre, up_pre))
+
+    grad_down = sum(contract_rows(a, s) for _, a, s, _, _ in saved).astype(jnp.bfloat16)
+    grad_gate = sum(contract_rows(r, g) for r, _, _, g, _ in saved).astype(jnp.bfloat16)
+    grad_up = sum(contract_rows(r, u) for r, _, _, _, u in saved).astype(jnp.bfloat16)
+
+    combined = sum(contract_rows(p, b[:, :model_width]) for p, b in zip(picks, backs))
+    input_grad = (grads_in.astype(jnp.float32) + combined).astype(jnp.bfloat16)
+    back_prob = jnp.concatenate(
+        [b[:, model_width].reshape(groups, sub) for b in backs], axis=1
+    ).reshape(slot_total)
     prob_grad = jnp.sum(
         jnp.where(hit, back_prob.astype(jnp.float32)[:, None, None], 0.0), axis=0
     ).astype(jnp.bfloat16)

time: 204 us -> 288 us (1.41)
  local copies, waits for them, and re-layouts: 3.07 us -> 54.2 us
  matrix products: 55.6 us -> 82.4 us
  starting transfers between devices: 19 us -> 33.2 us
  waiting for transfers between devices: 115 us -> 104 us
    reshape x0 -> x14, local copies, waits for them, and re-layouts: none -> 44.9 us  [the longest x6 22.1 us: exchange(): return moved.reshape(block.shape)]
    dot_general x4 -> x8, matrix products: 22 us -> 40.2 us  [contract_rows(): lax.dot_general(left, right, (((0,), (0,)), ((), ())), preferred_element_...]
    all_to_all x3 -> x6, starting transfers between devices: 17.7 us -> 31.9 us  [exchange(): lax.all_to_all(parted, 'expert', split_axis=0, concat_axis=0, tiled=True)]
    all_to_all x3 -> x6, waiting for transfers between devices: 106 us -> 94.4 us  [exchange(): lax.all_to_all(parted, 'expert', split_axis=0, concat_axis=0, tiled=True)]
    dot_general x3 -> x6, matrix products: 11.1 us -> 17.3 us  [contract_cols(): lax.dot_general(left, right, (((1,), (1,)), ((), ())), preferred_element_...]
    dot_general x5 -> x10, matrix products: 22.5 us -> 24.8 us  [the longest x2 7.33 us: expert_chunk(): pre_gate = jnp.dot(rows_in, gate_mat, preferred_element_type=jnp.float32)]
  transfers between devices with their start and end apart: 4 -> 7, of which waited for: 4 -> 7; matrix products, arithmetic and copies ran while one was open for 16% -> 35% of each run, Pallas kernels for 0% -> 0%
where the time goes in v2:
time: 288 us; the launch traced here: 286 us
  waiting for transfers between devices  104 us (36%)
  matrix products  82.4 us (29%)
  local copies, waits for them, and re-layouts  54.2 us (19%)
  starting transfers between devices  33.2 us (12%)
  other arithmetic  10.6 us (4%)
    all_to_all x6, waiting for transfers between devices, exchange(): lax.all_to_all(parted, 'expert', split_axis=0, concat_axis=0, tiled=True)  94.4 us
    dot_general x8, matrix products, contract_rows(): lax.dot_general(left, right, (((0,), (0,)), ((), ())), preferred_element_...  40.2 us
    all_to_all x6, starting transfers between devices, exchange(): lax.all_to_all(parted, 'expert', split_axis=0, concat_axis=0, tiled=True)  31.9 us
    reshape x6, local copies, waits for them, and re-layouts, exchange(): return moved.reshape(block.shape)  22.1 us
    reshape x6, local copies, waits for them, and re-layouts, exchange(): parted = block.reshape((groups, lead // groups) + block.shape[1:])  21.7 us
    dot_general x6, matrix products, contract_cols(): lax.dot_general(left, right, (((1,), (1,)), ((), ())), preferred_element_...  17.3 us
    ppermute x1, waiting for transfers between devices, shifted(): return lax.ppermute(block, axis, route)  9.65 us
    dot_general x2, matrix products, expert_chunk(): pre_gate = jnp.dot(rows_in, gate_mat, preferred_element_type=jnp.float32)  7.33 us
  transfers between devices with their start and end apart: 7, of which 7 were waited for; matrix products, arithmetic and copies ran while one was open for 35% of the time, Pallas kernels for 0%

profile of v2, /device:TPU:0, one launch (start us, length us, event | category | flops | bytes accessed | tf_op | source)
XLA Modules:
  0.0 285.6 jit_solution(2024604203209583679)
XLA Ops:
  12.8 7.6 %all-to-all-start = ((bf16[32,12,2048]{2,1,0:T(8,128)(2,1)}), bf16[32,12,2048]{2,1,0:T(8,128)(2,1)}, u32[]{:S(2)}, u32[]{:S(2)}) async-start(bf16[32,12,2048]{2,1,0:T(8,128)(2,1)} %reshape.110), calls=%async_computation | async-start | bytes 4194304 | tf_op jit(solution)/shard_map/all_to_all | solution.py:28
  26.9 23.5 %all-to-all-done = bf16[32,12,2048]{2,1,0:T(8,128)(2,1)} async-done(((bf16[32,12,2048]{2,1,0:T(8,128)(2,1)}), bf16[32,12,2048]{2,1,0:T(8,128)(2,1)}, u32[]{:S(2)}, u32[]{:S(2)}) %all-to-all-start) | async-done | bytes 1572896 | tf_op jit(solution)/shard_map/all_to_all | solution.py:28
  50.4 4.8 %all-to-all-start.2 = ((bf16[32,12,2048]{2,1,0:T(8,128)(2,1)}), bf16[32,12,2048]{2,1,0:T(8,128)(2,1)}, u32[]{:S(2)}, u32[]{:S(2)}) async-start(bf16[32,12,2048]{2,1,0:T(8,128)(2,1)} %reshape.115), calls=%async_computation.2 | async-start | bytes 4194304 | tf_op jit(solution)/shard_map/all_to_all | solution.py:28
  62.7 22.6 %all-to-all-done.2 = bf16[32,12,2048]{2,1,0:T(8,128)(2,1)} async-done(((bf16[32,12,2048]{2,1,0:T(8,128)(2,1)}), bf16[32,12,2048]{2,1,0:T(8,128)(2,1)}, u32[]{:S(2)}, u32[]{:S(2)}) %all-to-all-start.2) | async-done | bytes 1572896 | tf_op jit(solution)/shard_map/all_to_all | solution.py:28
  85.3 4.8 %all-to-all-start.1 = ((bf16[32,12,2176]{2,1,0:T(8,128)(2,1)}), bf16[32,12,2176]{2,1,0:T(8,128)(2,1)}, u32[]{:S(2)}, u32[]{:S(2)}) async-start(bf16[32,12,2176]{2,1,0:T(8,128)(2,1)} %reshape.112), calls=%async_computation.1 | async-start | bytes 4456448 | tf_op jit(solution)/shard_map/all_to_all | solution.py:28
  104.0 4.9 %fusion.10 = f32[384,768]{1,0:T(8,128)} fusion(bf16[384,2048]{1,0:T(8,128)(2,1)} %reshape.111, bf16[1,1,2048,768]{3,2,1,0:T(8,128)(2,1)} %param.11), kind=kOutput, calls=%fused_computation.17 | convolution fusion | flops 1207959552 | bytes 5898240 | tf_op jit(solution)/shard_map/dot_general | solution.py:40
  111.4 10.3 %all-to-all-done.1 = bf16[32,12,2176]{2,1,0:T(8,128)(2,1)} async-done(((bf16[32,12,2176]{2,1,0:T(8,128)(2,1)}), bf16[32,12,2176]{2,1,0:T(8,128)(2,1)}, u32[]{:S(2)}, u32[]{:S(2)}) %all-to-all-start.1) | async-done | bytes 1671200 | tf_op jit(solution)/shard_map/all_to_all | solution.py:28
  121.6 5.0 %all-to-all-start.3 = ((bf16[32,12,2176]{2,1,0:T(8,128)(2,1)}), bf16[32,12,2176]{2,1,0:T(8,128)(2,1)}, u32[]{:S(2)}, u32[]{:S(2)}) async-start(bf16[32,12,2176]{2,1,0:T(8,128)(2,1)} %reshape.117), calls=%async_computation.3 | async-start | bytes 4456448 | tf_op jit(solution)/shard_map/all_to_all | solution.py:28
  126.6 3.7 %reshape.113 = bf16[384,2176]{1,0:T(8,128)(2,1)} reshape(bf16[32,12,2176]{2,1,0:T(8,128)(2,1)} %all-to-all-done.1) | data formatting | bytes 3342336 | tf_op jit(solution)/shard_map/reshape | solution.py:29
  131.4 3.9 %fusion.26 = f32[384,768]{1,0:T(8,128)S(1)} fusion(bf16[1,1,768,2048]{3,2,1,0:T(8,128)(2,1)} %param.13, f32[384]{0:T(512)S(1)} %convert_reduce_fusion.1, bf16[384,2176]{1,0:T(8,128)(2,1)} %reshape.113), kind=kOutput, calls=%fused_computation.33 | convolution fusion | flops 1210318848 | bytes 5899776 | tf_op jit(solution)/shard_map/dot_general | solution.py:20
  140.4 17.6 %all-to-all-done.3 = bf16[32,12,2176]{2,1,0:T(8,128)(2,1)} async-done(((bf16[32,12,2176]{2,1,0:T(8,128)(2,1)}), bf16[32,12,2176]{2,1,0:T(8,128)(2,1)}, u32[]{:S(2)}, u32[]{:S(2)}) %all-to-all-start.3) | async-done | bytes 1671200 | tf_op jit(solution)/shard_map/all_to_all | solution.py:28
  158.0 3.7 %reshape.118 = bf16[384,2176]{1,0:T(8,128)(2,1)} reshape(bf16[32,12,2176]{2,1,0:T(8,128)(2,1)} %all-to-all-done.3) | data formatting | bytes 3342336 | tf_op jit(solution)/shard_map/reshape | solution.py:29
  162.7 3.9 %fusion.24 = f32[384,768]{1,0:T(8,128)S(1)} fusion(bf16[1,1,768,2048]{3,2,1,0:T(8,128)(2,1)} %param.13, f32[384]{0:T(512)S(1)} %convert_reduce_fusion, bf16[384,2176]{1,0:T(8,128)(2,1)} %reshape.118), kind=kOutput, calls=%fused_computation.31 | convolution fusion | flops 1210318848 | bytes 5899776 | tf_op jit(solution)/shard_map/dot_general | solution.py:20
  182.8 5.0 %all-to-all-start.4 = ((bf16[32,12,2176]{2,1,0:T(8,128)(2,1)}), bf16[32,12,2176]{2,1,0:T(8,128)(2,1)}, u32[]{:S(2)}, u32[]{:S(2)}) async-start(bf16[32,12,2176]{2,1,0:T(8,128)(2,1)} %reshape.119), calls=%async_computation.4 | async-start | bytes 4456448 | tf_op jit(solution)/shard_map/all_to_all | solution.py:28
  196.3 6.2 %fusion.68 = f32[2048,768]{1,0:T(8,128)} fusion(bf16[384,2048]{1,0:T(8,128)(2,1)} %reshape.111, bf16[384,768]{1,0:T(8,128)(2,1)} %get-tuple-element.10), kind=kOutput, calls=%fused_computation.99 | convolution fusion | flops 1207959552 | bytes 8454144 | tf_op jit(solution)/shard_map/dot_general | solution.py:14
  202.4 4.5 %fusion.59 = f32[768,2048]{1,0:T(8,128)} fusion(bf16[384,768]{1,0:T(8,128)(2,1)S(1)} %copy-done.16, f32[384]{0:T(512)S(1)} %convert_reduce_fusion.1, bf16[384,2176]{1,0:T(8,128)(2,1)S(1)} %copy-done.9), kind=kOutput, calls=%fused_computation.74 | convolution fusion | flops 1210318848 | bytes 8456192 | tf_op jit(solution)/shard_map/dot_general | solution.py:14
  206.9 12.2 %all-to-all-done.4 = bf16[32,12,2176]{2,1,0:T(8,128)(2,1)} async-done(((bf16[32,12,2176]{2,1,0:T(8,128)(2,1)}), bf16[32,12,2176]{2,1,0:T(8,128)(2,1)}, u32[]{:S(2)}, u32[]{:S(2)}) %all-to-all-start.4) | async-done | bytes 1671200 | tf_op jit(solution)/shard_map/all_to_all | solution.py:28
  219.1 4.8 %all-to-all-start.5 = ((bf16[32,12,2176]{2,1,0:T(8,128)(2,1)}), bf16[32,12,2176]{2,1,0:T(8,128)(2,1)}, u32[]{:S(2)}, u32[]{:S(2)}) async-start(bf16[32,12,2176]{2,1,0:T(8,128)(2,1)} %reshape.121), calls=%async_computation.5 | async-start | bytes 4456448 | tf_op jit(solution)/shard_map/all_to_all | solution.py:28
  224.0 6.2 %fusion.67 = f32[2048,768]{1,0:T(8,128)} fusion(bf16[384,2048]{1,0:T(8,128)(2,1)} %reshape.111, bf16[384,768]{1,0:T(8,128)(2,1)} %get-tuple-element.9), kind=kOutput, calls=%fused_computation.98 | convolution fusion | flops 1207959552 | bytes 8454144 | tf_op jit(solution)/shard_map/dot_general | solution.py:14
  230.2 6.4 %fusion.29 = bf16[1,1,2048,768]{3,2,1,0:T(8,128)(2,1)} fusion(f32[2048,768]{1,0:T(8,128)} %fusion.68, bf16[384,2048]{1,0:T(8,128)(2,1)S(1)} %copy-done.4, bf16[384,768]{1,0:T(8,128)(2,1)S(1)} %copy-done.17), kind=kOutput, calls=%fused_computation.38 | convolution fusion | flops 1211105280 | bytes 11599872 | tf_op jit(solution)/shard_map/dot_general | solution.py:14
  247.3 8.3 %all-to-all-done.5 = bf16[32,12,2176]{2,1,0:T(8,128)(2,1)} async-done(((bf16[32,12,2176]{2,1,0:T(8,128)(2,1)}), bf16[32,12,2176]{2,1,0:T(8,128)(2,1)}, u32[]{:S(2)}, u32[]{:S(2)}) %all-to-all-start.5) | async-done | bytes 1671200 | tf_op jit(solution)/shard_map/all_to_all | solution.py:28
  259.2 3.7 %fusion.42 = bf16[192,2048]{1,0:T(8,128)(2,1)} fusion(f32[192,2048]{1,0:T(8,128)} %fusion.44, pred[384,192]{1,0:T(32,128)(4,1)S(1)} %reshape.114, bf16[384,2176]{1,0:T(8,128)(2,1)} %reshape.122, bf16[1,192,2048]{2,1,0:T(8,128)(2,1)} %param.8), kind=kOutput, calls=%fused_computation.48 | convolution fusion | flops 303562752 | bytes 4792320 | tf_op jit(solution)/shard_map/dot_general | solution.py:14
  264.3 6.3 %fusion.28 = bf16[1,1,2048,768]{3,2,1,0:T(8,128)(2,1)} fusion(f32[2048,768]{1,0:T(8,128)} %fusion.67, bf16[384,2048]{1,0:T(8,128)(2,1)S(1)} %copy-done.5, bf16[384,768]{1,0:T(8,128)(2,1)S(1)} %copy-done.11), kind=kOutput, calls=%fused_computation.37 | convolution fusion | flops 1211105280 | bytes 11599872 | tf_op jit(solution)/shard_map/dot_general | solution.py:14
  273.9 9.7 %collective-permute-done = bf16[192,2048]{1,0:T(8,128)(2,1)} collective-permute-done((bf16[192,2048]{1,0:T(8,128)(2,1)}, bf16[192,2048]{1,0:T(8,128)(2,1)}, u32[]{:S(2)}, u32[]{:S(2)}) %collective-permute-start) | collective-permute-done | bytes 786464 | tf_op jit(solution)/shard_map/ppermute | solution.py:10
  (122 shorter events, 95.0 us)
Async XLA Ops:
  0.6 134.7 %copy-start = (bf16[1,1,2048,768]{3,2,1,0:T(8,128)(2,1)S(1)}, bf16[1,1,2048,768]{3,2,1,0:T(8,128)(2,1)}, u32[]{:S(2)}) copy-start(bf16[1,1,2048,768]{3,2,1,0:T(8,128)(2,1)} %param.12) | copy-start | bytes 9437188
  12.8 37.6 %all-to-all-start = ((bf16[32,12,2048]{2,1,0:T(8,128)(2,1)}), bf16[32,12,2048]{2,1,0:T(8,128)(2,1)}, u32[]{:S(2)}, u32[]{:S(2)}) async-start(bf16[32,12,2048]{2,1,0:T(8,128)(2,1)} %reshape.110), calls=%async_computation | async-start | bytes 4194304 | tf_op jit(solution)/shard_map/all_to_all | solution.py:28
  26.9 28.3 %copy-start.19 = (bf16[1,192,2]{1,2,0:T(2,128)(2,1)S(1)}, bf16[1,192,2]{1,2,0:T(2,128)(2,1)}, u32[]{:S(2)}) copy-start(bf16[1,192,2]{1,2,0:T(2,128)(2,1)} %param.10) | copy-start | bytes 2308
  50.4 34.8 %all-to-all-start.2 = ((bf16[32,12,2048]{2,1,0:T(8,128)(2,1)}), bf16[32,12,2048]{2,1,0:T(8,128)(2,1)}, u32[]{:S(2)}, u32[]{:S(2)}) async-start(bf16[32,12,2048]{2,1,0:T(8,128)(2,1)} %reshape.115), calls=%async_computation.2 | async-start | bytes 4194304 | tf_op jit(solution)/shard_map/all_to_all | solution.py:28
  85.3 36.4 %all-to-all-start.1 = ((bf16[32,12,2176]{2,1,0:T(8,128)(2,1)}), bf16[32,12,2176]{2,1,0:T(8,128)(2,1)}, u32[]{:S(2)}, u32[]{:S(2)}) async-start(bf16[32,12,2176]{2,1,0:T(8,128)(2,1)} %reshape.112), calls=%async_computation.1 | async-start | bytes 4456448 | tf_op jit(solution)/shard_map/all_to_all | solution.py:28
  104.0 4.9 %copy-start.2 = (bf16[384,2048]{1,0:T(8,128)(2,1)S(1)}, bf16[384,2048]{1,0:T(8,128)(2,1)}, u32[]{:S(2)}) copy-start(bf16[384,2048]{1,0:T(8,128)(2,1)} %reshape.116) | copy-start | bytes 4718596
  104.0 4.9 %copy-start.22 = (bf16[1,1,2048,768]{3,2,1,0:T(8,128)(2,1)S(1)}, bf16[1,1,2048,768]{3,2,1,0:T(8,128)(2,1)}, u32[]{:S(2)}) copy-start(bf16[1,1,2048,768]{3,2,1,0:T(8,128)(2,1)} %param.11) | copy-start | bytes 9437188
  121.6 36.4 %all-to-all-start.3 = ((bf16[32,12,2176]{2,1,0:T(8,128)(2,1)}), bf16[32,12,2176]{2,1,0:T(8,128)(2,1)}, u32[]{:S(2)}, u32[]{:S(2)}) async-start(bf16[32,12,2176]{2,1,0:T(8,128)(2,1)} %reshape.117), calls=%async_computation.3 | async-start | bytes 4456448 | tf_op jit(solution)/shard_map/all_to_all | solution.py:28
  131.3 4.0 %copy-start.1 = (bf16[384,2048]{1,0:T(8,128)(2,1)S(1)}, bf16[384,2048]{1,0:T(8,128)(2,1)}, u32[]{:S(2)}) copy-start(bf16[384,2048]{1,0:T(8,128)(2,1)} %reshape.111) | copy-start | bytes 4718596
  131.3 4.0 %copy-start.25 = (f32[384,768]{1,0:T(8,128)S(1)}, f32[384,768]{1,0:T(8,128)}, u32[]{:S(2)}) copy-start(f32[384,768]{1,0:T(8,128)} %fusion.10) | copy-start | bytes 3538948
  162.7 4.0 %copy-start.24 = (f32[384,768]{1,0:T(8,128)S(1)}, f32[384,768]{1,0:T(8,128)}, u32[]{:S(2)}) copy-start(f32[384,768]{1,0:T(8,128)} %fusion.8) | copy-start | bytes 3538948
  182.8 36.4 %all-to-all-start.4 = ((bf16[32,12,2176]{2,1,0:T(8,128)(2,1)}), bf16[32,12,2176]{2,1,0:T(8,128)(2,1)}, u32[]{:S(2)}, u32[]{:S(2)}) async-start(bf16[32,12,2176]{2,1,0:T(8,128)(2,1)} %reshape.119), calls=%async_computation.4 | async-start | bytes 4456448 | tf_op jit(solution)/shard_map/all_to_all | solution.py:28
  196.2 6.2 %copy-start.9 = (bf16[384,2176]{1,0:T(8,128)(2,1)S(1)}, bf16[384,2176]{1,0:T(8,128)(2,1)}, u32[]{:S(2)}) copy-start(bf16[384,2176]{1,0:T(8,128)(2,1)} %reshape.113) | copy-start | bytes 5013508
  196.3 6.2 %copy-start.16 = (bf16[384,768]{1,0:T(8,128)(2,1)S(1)}, bf16[384,768]{1,0:T(8,128)(2,1)}, u32[]{:S(2)}) copy-start(bf16[384,768]{1,0:T(8,128)(2,1)} %copy-done.15) | copy-start | bytes 1769476
  219.1 36.4 %all-to-all-start.5 = ((bf16[32,12,2176]{2,1,0:T(8,128)(2,1)}), bf16[32,12,2176]{2,1,0:T(8,128)(2,1)}, u32[]{:S(2)}, u32[]{:S(2)}) async-start(bf16[32,12,2176]{2,1,0:T(8,128)(2,1)} %reshape.121), calls=%async_computation.5 | async-start | bytes 4456448 | tf_op jit(solution)/shard_map/all_to_all | solution.py:28
  224.0 6.2 %copy-start.4 = (bf16[384,2048]{1,0:T(8,128)(2,1)S(1)}, bf16[384,2048]{1,0:T(8,128)(2,1)}, u32[]{:S(2)}) copy-start(bf16[384,2048]{1,0:T(8,128)(2,1)} %reshape.116) | copy-start | bytes 4718596
  224.0 6.2 %copy-start.17 = (bf16[384,768]{1,0:T(8,128)(2,1)S(1)}, bf16[384,768]{1,0:T(8,128)(2,1)}, u32[]{:S(2)}) copy-start(bf16[384,768]{1,0:T(8,128)(2,1)} %get-tuple-element.7) | copy-start | bytes 1769476
  224.0 12.7 %slice-start = ((s8[6291456]{0:T(1024)(128)(4,1)}), s8[4194304]{0:T(1024)(128)(4,1)S(1)}, s32[]{:S(2)}) async-start(s8[6291456]{0:T(1024)(128)(4,1)} %bitcast.112), calls=%async_computation.6 | async-start | bytes 8388608
  230.2 6.5 %slice-start.1 = ((s8[6291456]{0:T(1024)(128)(4,1)}), s8[2097152]{0:T(1024)(128)(4,1)S(1)}, s32[]{:S(2)}) async-start(s8[6291456]{0:T(1024)(128)(4,1)} %bitcast.112), calls=%async_computation.7 | async-start | bytes 4194304
  230.2 6.5 %copy-start.7 = (bf16[384,2176]{1,0:T(8,128)(2,1)S(1)}, bf16[384,2176]{1,0:T(8,128)(2,1)}, u32[]{:S(2)}) copy-start(bf16[384,2176]{1,0:T(8,128)(2,1)} %reshape.118) | copy-start | bytes 5013508
  230.2 6.5 %copy-start.14 = (bf16[384,768]{1,0:T(8,128)(2,1)S(1)}, bf16[384,768]{1,0:T(8,128)(2,1)}, u32[]{:S(2)}) copy-start(bf16[384,768]{1,0:T(8,128)(2,1)} %copy-done.13) | copy-start | bytes 1769476
  259.2 5.0 %copy-start.5 = (bf16[384,2048]{1,0:T(8,128)(2,1)S(1)}, bf16[384,2048]{1,0:T(8,128)(2,1)}, u32[]{:S(2)}) copy-start(bf16[384,2048]{1,0:T(8,128)(2,1)} %reshape.116) | copy-start | bytes 4718596
  259.2 5.0 %copy-start.11 = (bf16[384,768]{1,0:T(8,128)(2,1)S(1)}, bf16[384,768]{1,0:T(8,128)(2,1)}, u32[]{:S(2)}) copy-start(bf16[384,768]{1,0:T(8,128)(2,1)} %copy-done.10) | copy-start | bytes 1769476
  263.0 20.5 %collective-permute-start = (bf16[192,2048]{1,0:T(8,128)(2,1)}, bf16[192,2048]{1,0:T(8,128)(2,1)}, u32[]{:S(2)}, u32[]{:S(2)}) collective-permute-start(bf16[192,2048]{1,0:T(8,128)(2,1)} %fusion.42), channel_id=1, source_target_pairs={{32,0},{64,32},{96,64},{33,1},{65,33},{97,65},{34,2},{66,34},{98,6... | collective-permute-start | bytes 2359304 | tf_op jit(solution)/shard_map/ppermute | solution.py:10
  (11 other events, 27.2 us)

commit v3 on v1

--- a/solution.py
+++ b/solution.py
@@ -74,6 +74,11 @@
     expert_out = jnp.dot(act_rows, down_mat, preferred_element_type=jnp.float32).astype(
         jnp.bfloat16
     )
+    pre_gate, pre_up, act_rows, expert_out = lax.optimization_barrier(
+        (pre_gate, pre_up, act_rows, expert_out)
+    )
+    sigmoid_g = jax.nn.sigmoid(pre_gate)
+    silu_g = pre_gate * sigmoid_g
     prob_part = jnp.sum(
         grad_rows.astype(jnp.float32) * expert_out.astype(jnp.float32), axis=1
     ).astype(jnp.bfloat16)

time: 204 us -> 198 us (0.971)
  waiting for transfers between devices: 115 us -> 106 us
  other arithmetic: 9.55 us -> 13.4 us
    all_to_all x3, waiting for transfers between devices: 106 us -> 96.6 us  [exchange(): lax.all_to_all(parted, 'expert', split_axis=0, concat_axis=0, tiled=True)]
    reduce_sum x0 -> x1, other arithmetic: none -> 3.88 us  [per_device(): jnp.sum(grad_rows.astype(jnp.float32) * expert_out.astype(jnp.float32), a...]
  transfers between devices with their start and end apart: 4 -> 4, of which waited for: 4 -> 4; matrix products, arithmetic and copies ran while one was open for 16% -> 21% of each run, Pallas kernels for 0% -> 0%
where the time goes in v3:
time: 198 us; the launch traced here: 197 us
  waiting for transfers between devices  106 us (54%)
  matrix products  55.1 us (28%)
  starting transfers between devices  18.9 us (10%)
  other arithmetic  13.4 us (7%)
  local copies, waits for them, and re-layouts  2.84 us (1%)
    all_to_all x3, waiting for transfers between devices, exchange(): lax.all_to_all(parted, 'expert', split_axis=0, concat_axis=0, tiled=True)  96.6 us
    dot_general x4, matrix products, contract_rows(): lax.dot_general(left, right, (((0,), (0,)), ((), ())), preferred_element_...  21.7 us
    all_to_all x3, starting transfers between devices, exchange(): lax.all_to_all(parted, 'expert', split_axis=0, concat_axis=0, tiled=True)  17.6 us
    dot_general x3, matrix products, contract_cols(): lax.dot_general(left, right, (((1,), (1,)), ((), ())), preferred_element_...  11 us
    ppermute x1, waiting for transfers between devices, shifted(): return lax.ppermute(block, axis, route)  9.42 us
    dot_general x1, matrix products, per_device(): pre_up = jnp.dot(rows_in, up_mat, preferred_element_type=jnp.float32)  6.88 us
    dot_general x1, matrix products, per_device(): pre_gate = jnp.dot(rows_in, gate_mat, preferred_element_type=jnp.float32)  5.58 us
    dot_general x1, matrix products, per_device(): jnp.dot(act_rows, down_mat, preferred_element_type=jnp.float32)  3.97 us
  transfers between devices with their start and end apart: 4, of which 4 were waited for; matrix products, arithmetic and copies ran while one was open for 21% of the time, Pallas kernels for 0%

profile of v3, /device:TPU:0, one launch (start us, length us, event | category | flops | bytes accessed | tf_op | source)
XLA Modules:
  0.0 197.2 jit_solution(8238803921465709697)
XLA Ops:
  4.2 3.8 %convolution_convert_fusion.5 = bf16[768,2048]{1,0:T(8,128)(2,1)} fusion(pred[768,192]{0,1:T(8,128)(4,1)S(1)} %fusion.23, bf16[1,192,2048]{2,1,0:T(8,128)(2,1)} %param.7), kind=kOutput, calls=%fused_computation.10 | convolution fusion | flops 605552640 | bytes 4079616 | tf_op jit(solution)/shard_map/dot_general | solution.py:57
  8.1 7.7 %all-to-all-start = ((bf16[32,24,2048]{2,1,0:T(8,128)(2,1)}), bf16[32,24,2048]{2,1,0:T(8,128)(2,1)}, u32[]{:S(2)}, u32[]{:S(2)}) async-start(bf16[32,24,2048]{2,1,0:T(8,128)(2,1)} %bitcast.78), calls=%async_computation | async-start | bytes 6291456 | tf_op jit(solution)/shard_map/all_to_all | solution.py:28
  16.2 2.2 %convolution_convert_fusion.4 = bf16[768,2048]{1,0:T(8,128)(2,1)S(1)} fusion(pred[768,192]{0,1:T(8,128)(4,1)S(1)} %fusion.23, bf16[1,192,2048]{2,1,0:T(8,128)(2,1)} %param.8), kind=kOutput, calls=%fused_computation.9 | convolution fusion | flops 605552640 | bytes 4079616 | tf_op jit(solution)/shard_map/dot_general | solution.py:58
  18.4 2.0 %pad_maximum_fusion = bf16[768,2176]{1,0:T(8,128)(2,1)} fusion(bf16[768,128]{1,0:T(8,128)(2,1)S(1)} %broadcast_select_fusion.1, bf16[768,2048]{1,0:T(8,128)(2,1)S(1)} %convolution_convert_fusion.4), kind=kLoop, calls=%fused_computation.11 | loop fusion | flops 6684672 | bytes 6684672 | tf_op jit(solution)/shard_map/concatenate | solution.py:62
  20.4 37.4 %all-to-all-done = bf16[32,24,2048]{2,1,0:T(8,128)(2,1)} async-done(((bf16[32,24,2048]{2,1,0:T(8,128)(2,1)}), bf16[32,24,2048]{2,1,0:T(8,128)(2,1)}, u32[]{:S(2)}, u32[]{:S(2)}) %all-to-all-start) | async-done | bytes 3145760 | tf_op jit(solution)/shard_map/all_to_all | solution.py:28
  57.8 5.0 %all-to-all-start.1 = ((bf16[32,24,2176]{2,1,0:T(8,128)(2,1)}), bf16[32,24,2176]{2,1,0:T(8,128)(2,1)}, u32[]{:S(2)}, u32[]{:S(2)}) async-start(bf16[32,24,2176]{2,1,0:T(8,128)(2,1)} %bitcast.76), calls=%async_computation.1 | async-start | bytes 6684672 | tf_op jit(solution)/shard_map/all_to_all | solution.py:28
  62.8 5.6 %fusion.9 = f32[768,768]{1,0:T(8,128)S(1)} fusion(bf16[768,2048]{1,0:T(8,128)(2,1)} %bitcast.4, bf16[1,1,2048,768]{3,2,1,0:T(8,128)(2,1)} %param.11), kind=kOutput, calls=%fused_computation.20 | convolution fusion | flops 2415919104 | bytes 8650752 | tf_op jit(solution)/shard_map/dot_general | solution.py:69
  68.4 6.9 %multiply_convert_fusion.2 = (bf16[768,768]{1,0:T(8,128)(2,1)S(1)}, f32[768,768]{1,0:T(8,128)}) fusion(f32[768,768]{1,0:T(8,128)S(1)} %fusion.9, bf16[768,2048]{1,0:T(8,128)(2,1)} %bitcast.4, bf16[1,1,2048,768]{3,2,1,0:T(8,128)(2,1)S(1)} %copy-done.5), kind=kOutput, calls=%fused_computation.33 | convolution fusion | flops 2419458048 | bytes 12189696 | tf_op jit(solution)/shard_map/dot_general | solution.py:70
  75.3 4.0 %convolution_convert_fusion.3 = bf16[768,2048]{1,0:T(8,128)(2,1)} fusion(bf16[768,768]{1,0:T(8,128)(2,1)S(1)} %get-tuple-element.11, bf16[1,1,768,2048]{3,2,1,0:T(8,128)(2,1)S(1)} %copy-done), kind=kOutput, calls=%fused_computation.8 | convolution fusion | flops 2417491968 | bytes 7471104 | tf_op jit(solution)/shard_map/dot_general | solution.py:74
  79.3 27.5 %all-to-all-done.1 = bf16[32,24,2176]{2,1,0:T(8,128)(2,1)} async-done(((bf16[32,24,2176]{2,1,0:T(8,128)(2,1)}), bf16[32,24,2176]{2,1,0:T(8,128)(2,1)}, u32[]{:S(2)}, u32[]{:S(2)}) %all-to-all-start.1) | async-done | bytes 3342368 | tf_op jit(solution)/shard_map/all_to_all | solution.py:28
  106.8 1.1 convert_reduce_fusion.1
  107.9 3.9 %fusion.1 = bf16[768]{0:T(1024)(128)(2,1)S(1)} fusion(bf16[768,2048]{1,0:T(8,128)(2,1)} %convolution_convert_fusion.3, bf16[768,2176]{1,0:T(8,128)(2,1)} %bitcast.8), kind=kLoop, calls=%fused_computation.3 | loop fusion | flops 6290688 | bytes 6292992 | tf_op jit(solution)/shard_map/reduce_sum | solution.py:82
  112.1 5.3 %multiply_convert_fusion = (bf16[768,768]{1,0:T(8,128)(2,1)S(1)}, bf16[768,768]{1,0:T(8,128)(2,1)S(1)}) fusion(f32[768,768]{1,0:T(8,128)S(1)} %copy-done.10, f32[768,768]{1,0:T(8,128)S(1)} %copy-done.13, bf16[1,1,768,2048]{3,2,1,0:T(8,128)(2,1)S(1)} %copy-done, f32[768]{0:T(1024)S(1)} %convert_reduce_fusion.1, bf16[768,2176]{1,0:T(8,128)(2,1)} %bitcast.8), kind=kOutput, calls=%fused_computation.30 | convolution fusion | flops 2428305408 | bytes 13372416 | tf_op jit(solution)/shard_map/dot_general | solution.py:20
  117.5 2.6 %fusion.7 = f32[768,2048]{1,0:T(8,128)S(1)} fusion(bf16[768,768]{1,0:T(8,128)(2,1)S(1)} %get-tuple-element.14, bf16[1,1,2048,768]{3,2,1,0:T(8,128)(2,1)S(1)} %copy-done.4), kind=kOutput, calls=%fused_computation.18 | convolution fusion | flops 2415919104 | bytes 10616832 | tf_op jit(solution)/shard_map/dot_general | solution.py:20
  120.2 3.1 %add_convert_fusion = bf16[768,2048]{1,0:T(8,128)(2,1)S(1)} fusion(f32[768,2048]{1,0:T(8,128)S(1)} %fusion.7, bf16[768,768]{1,0:T(8,128)(2,1)S(1)} %get-tuple-element.13, bf16[1,1,2048,768]{3,2,1,0:T(8,128)(2,1)S(1)} %copy-done.6), kind=kOutput, calls=%fused_computation.4 | convolution fusion | flops 2419064832 | bytes 13762560 | tf_op jit(solution)/shard_map/dot_general | solution.py:20
  123.3 2.1 %pad_maximum_fusion.1 = bf16[768,2176]{1,0:T(8,128)(2,1)} fusion(bf16[768,128]{1,0:T(8,128)(2,1)S(1)} %broadcast_select_fusion, bf16[768,2048]{1,0:T(8,128)(2,1)S(1)} %add_convert_fusion), kind=kLoop, calls=%fused_computation.12 | loop fusion | flops 6684672 | bytes 6684672 | tf_op jit(solution)/shard_map/concatenate | solution.py:97
  125.3 5.0 %all-to-all-start.2 = ((bf16[32,24,2176]{2,1,0:T(8,128)(2,1)}), bf16[32,24,2176]{2,1,0:T(8,128)(2,1)}, u32[]{:S(2)}, u32[]{:S(2)}) async-start(bf16[32,24,2176]{2,1,0:T(8,128)(2,1)} %bitcast.77), calls=%async_computation.2 | async-start | bytes 6684672 | tf_op jit(solution)/shard_map/all_to_all | solution.py:28
  130.3 6.3 %fusion.15 = bf16[1,1,2048,768]{3,2,1,0:T(8,128)(2,1)} fusion(bf16[768,2048]{1,0:T(8,128)(2,1)} %bitcast.4, bf16[768,768]{1,0:T(8,128)(2,1)S(1)} %copy-done.15), kind=kOutput, calls=%fused_computation.26 | convolution fusion | flops 2417491968 | bytes 7471104 | tf_op jit(solution)/shard_map/dot_general | solution.py:14
  136.7 6.2 %fusion.16 = bf16[1,1,768,2048]{3,2,1,0:T(8,128)(2,1)} fusion(bf16[768,768]{1,0:T(8,128)(2,1)S(1)} %copy-done.12, f32[768]{0:T(1024)S(1)} %convert_reduce_fusion.1, bf16[768,2176]{1,0:T(8,128)(2,1)} %bitcast.8), kind=kOutput, calls=%fused_computation.27 | convolution fusion | flops 2422210560 | bytes 7474176 | tf_op jit(solution)/shard_map/dot_general | solution.py:14
  142.8 31.7 %all-to-all-done.2 = bf16[32,24,2176]{2,1,0:T(8,128)(2,1)} async-done(((bf16[32,24,2176]{2,1,0:T(8,128)(2,1)}), bf16[32,24,2176]{2,1,0:T(8,128)(2,1)}, u32[]{:S(2)}, u32[]{:S(2)}) %all-to-all-start.2) | async-done | bytes 3342368 | tf_op jit(solution)/shard_map/all_to_all | solution.py:28
  174.5 2.8 %fusion.20 = bf16[192,2048]{1,0:T(8,128)(2,1)S(1)} fusion(pred[768,192]{0,1:T(8,128)(4,1)S(1)} %fusion.23, bf16[768,2176]{1,0:T(8,128)(2,1)} %bitcast.16, bf16[1,192,2048]{2,1,0:T(8,128)(2,1)S(1)} %copy-done.2), kind=kOutput, calls=%fused_computation.29 | convolution fusion | flops 605159424 | bytes 4866048 | tf_op jit(solution)/shard_map/dot_general | solution.py:14
  177.3 1.3 collective-permute-start
  178.6 6.4 %fusion.14 = bf16[1,1,2048,768]{3,2,1,0:T(8,128)(2,1)} fusion(bf16[768,2048]{1,0:T(8,128)(2,1)} %bitcast.4, bf16[768,768]{1,0:T(8,128)(2,1)S(1)} %copy-done.8), kind=kOutput, calls=%fused_computation.25 | convolution fusion | flops 2417491968 | bytes 7471104 | tf_op jit(solution)/shard_map/dot_general | solution.py:14
  186.9 9.4 %collective-permute-done = bf16[192,2048]{1,0:T(8,128)(2,1)S(1)} collective-permute-done((bf16[192,2048]{1,0:T(8,128)(2,1)S(1)}, bf16[192,2048]{1,0:T(8,128)(2,1)S(1)}, u32[]{:S(2)}, u32[]{:S(2)}) %collective-permute-start) | collective-permute-done | bytes 786464 | tf_op jit(solution)/shard_map/ppermute | solution.py:10
  (52 shorter events, 7.2 us)
Async XLA Ops:
  0.6 74.7 %copy-start = (bf16[1,1,768,2048]{3,2,1,0:T(8,128)(2,1)S(1)}, bf16[1,1,768,2048]{3,2,1,0:T(8,128)(2,1)}, u32[]{:S(2)}) copy-start(bf16[1,1,768,2048]{3,2,1,0:T(8,128)(2,1)} %param.13) | copy-start | bytes 9437188
  8.1 7.7 %copy-start.3 = (bf16[1,192,2]{1,2,0:T(2,128)(2,1)S(1)}, bf16[1,192,2]{1,2,0:T(2,128)(2,1)}, u32[]{:S(2)}) copy-start(bf16[1,192,2]{1,2,0:T(2,128)(2,1)} %param.10) | copy-start | bytes 2308
  8.1 49.7 %all-to-all-start = ((bf16[32,24,2048]{2,1,0:T(8,128)(2,1)}), bf16[32,24,2048]{2,1,0:T(8,128)(2,1)}, u32[]{:S(2)}, u32[]{:S(2)}) async-start(bf16[32,24,2048]{2,1,0:T(8,128)(2,1)} %bitcast.78), calls=%async_computation | async-start | bytes 6291456 | tf_op jit(solution)/shard_map/all_to_all | solution.py:28
  57.8 49.0 %all-to-all-start.1 = ((bf16[32,24,2176]{2,1,0:T(8,128)(2,1)}), bf16[32,24,2176]{2,1,0:T(8,128)(2,1)}, u32[]{:S(2)}, u32[]{:S(2)}) async-start(bf16[32,24,2176]{2,1,0:T(8,128)(2,1)} %bitcast.76), calls=%async_computation.1 | async-start | bytes 6684672 | tf_op jit(solution)/shard_map/all_to_all | solution.py:28
  62.8 5.6 %copy-start.5 = (bf16[1,1,2048,768]{3,2,1,0:T(8,128)(2,1)S(1)}, bf16[1,1,2048,768]{3,2,1,0:T(8,128)(2,1)}, u32[]{:S(2)}) copy-start(bf16[1,1,2048,768]{3,2,1,0:T(8,128)(2,1)} %param.12) | copy-start | bytes 9437188
  68.4 6.9 %copy-start.9 = (f32[768,768]{1,0:T(8,128)}, f32[768,768]{1,0:T(8,128)S(1)}, u32[]{:S(2)}) copy-start(f32[768,768]{1,0:T(8,128)S(1)} %fusion.9) | copy-start | bytes 7077892
  75.3 4.0 %copy-start.11 = (bf16[768,768]{1,0:T(8,128)(2,1)}, bf16[768,768]{1,0:T(8,128)(2,1)S(1)}, u32[]{:S(2)}) copy-start(bf16[768,768]{1,0:T(8,128)(2,1)S(1)} %get-tuple-element.11) | copy-start | bytes 3538948
  107.9 4.1 %copy-start.10 = (f32[768,768]{1,0:T(8,128)S(1)}, f32[768,768]{1,0:T(8,128)}, u32[]{:S(2)}) copy-start(f32[768,768]{1,0:T(8,128)} %copy-done.9) | copy-start | bytes 7077892
  107.9 4.2 %copy-start.13 = (f32[768,768]{1,0:T(8,128)S(1)}, f32[768,768]{1,0:T(8,128)}, u32[]{:S(2)}) copy-start(f32[768,768]{1,0:T(8,128)} %get-tuple-element.9) | copy-start | bytes 7077892
  112.1 5.3 %copy-start.4 = (bf16[1,1,2048,768]{3,2,1,0:T(8,128)(2,1)S(1)}, bf16[1,1,2048,768]{3,2,1,0:T(8,128)(2,1)}, u32[]{:S(2)}) copy-start(bf16[1,1,2048,768]{3,2,1,0:T(8,128)(2,1)} %param.11) | copy-start | bytes 9437188
  117.4 2.7 %copy-start.7 = (bf16[768,768]{1,0:T(8,128)(2,1)}, bf16[768,768]{1,0:T(8,128)(2,1)S(1)}, u32[]{:S(2)}) copy-start(bf16[768,768]{1,0:T(8,128)(2,1)S(1)} %get-tuple-element.14) | copy-start | bytes 3538948
  117.4 2.7 %copy-start.14 = (bf16[768,768]{1,0:T(8,128)(2,1)}, bf16[768,768]{1,0:T(8,128)(2,1)S(1)}, u32[]{:S(2)}) copy-start(bf16[768,768]{1,0:T(8,128)(2,1)S(1)} %get-tuple-element.13) | copy-start | bytes 3538948
  117.4 2.7 %copy-start.6 = (bf16[1,1,2048,768]{3,2,1,0:T(8,128)(2,1)S(1)}, bf16[1,1,2048,768]{3,2,1,0:T(8,128)(2,1)}, u32[]{:S(2)}) copy-start(bf16[1,1,2048,768]{3,2,1,0:T(8,128)(2,1)} %param.12) | copy-start | bytes 9437188
  125.3 5.0 %copy-start.15 = (bf16[768,768]{1,0:T(8,128)(2,1)S(1)}, bf16[768,768]{1,0:T(8,128)(2,1)}, u32[]{:S(2)}) copy-start(bf16[768,768]{1,0:T(8,128)(2,1)} %copy-done.14) | copy-start | bytes 3538948
  125.3 49.2 %all-to-all-start.2 = ((bf16[32,24,2176]{2,1,0:T(8,128)(2,1)}), bf16[32,24,2176]{2,1,0:T(8,128)(2,1)}, u32[]{:S(2)}, u32[]{:S(2)}) async-start(bf16[32,24,2176]{2,1,0:T(8,128)(2,1)} %bitcast.77), calls=%async_computation.2 | async-start | bytes 6684672 | tf_op jit(solution)/shard_map/all_to_all | solution.py:28
  130.3 6.3 %copy-start.12 = (bf16[768,768]{1,0:T(8,128)(2,1)S(1)}, bf16[768,768]{1,0:T(8,128)(2,1)}, u32[]{:S(2)}) copy-start(bf16[768,768]{1,0:T(8,128)(2,1)} %copy-done.11) | copy-start | bytes 3538948
  136.7 37.9 %copy-start.2 = (bf16[1,192,2048]{2,1,0:T(8,128)(2,1)S(1)}, bf16[1,192,2048]{2,1,0:T(8,128)(2,1)}, u32[]{:S(2)}) copy-start(bf16[1,192,2048]{2,1,0:T(8,128)(2,1)} %param.8) | copy-start | bytes 2359300
  174.5 4.1 %copy-start.8 = (bf16[768,768]{1,0:T(8,128)(2,1)S(1)}, bf16[768,768]{1,0:T(8,128)(2,1)}, u32[]{:S(2)}) copy-start(bf16[768,768]{1,0:T(8,128)(2,1)} %copy-done.7) | copy-start | bytes 3538948
  177.3 19.1 %collective-permute-start = (bf16[192,2048]{1,0:T(8,128)(2,1)S(1)}, bf16[192,2048]{1,0:T(8,128)(2,1)S(1)}, u32[]{:S(2)}, u32[]{:S(2)}) collective-permute-start(bf16[192,2048]{1,0:T(8,128)(2,1)S(1)} %fusion.20), channel_id=1, source_target_pairs={{32,0},{64,32},{96,64},{33,1},{65,33},{97,65},{34,2},{66,34},{98,6... | collective-permute-start | bytes 2359304 | tf_op jit(solution)/shard_map/ppermute | solution.py:10
  178.6 18.6 %copy-start.1 = (bf16[1,1,768,2048]{3,2,1,0:T(8,128)(2,1)S(1)}, bf16[1,1,768,2048]{3,2,1,0:T(8,128)(2,1)}, u32[]{:S(2)}) copy-start(bf16[1,1,768,2048]{3,2,1,0:T(8,128)(2,1)} %param.13) | copy-start | bytes 9437188

commit v4 on v0

--- a/solution.py
+++ b/solution.py
@@ -29,16 +29,24 @@
     return moved.reshape(block.shape)
 
 
+def lane_block(values, width, lane):
+    lanes = jnp.arange(width, dtype=jnp.int32)[None, :]
+    return jnp.where(lanes == lane, values.astype(jnp.float32)[:, None], 0.0)
+
+
 def per_device(hidden_in, out_grad, routes, mixing, w_gate, w_up, w_down):
     tokens_in = hidden_in[0]
     grads_in = out_grad[0]
     groups = lax.axis_size("expert")
     tok_rows = tokens_in.shape[0]
+    model_width = tokens_in.shape[1]
+    side = 128
     capacity = 4 * tok_rows // groups
     slot_total = groups * capacity
     gate_mat = w_gate[0, 0]
     up_mat = w_up[0, 0]
     down_mat = w_down[0, 0]
+    hidden_units = gate_mat.shape[1]
 
     chosen = routes[0].reshape(-1)
     onehot = (chosen[:, None] == jnp.arange(groups, dtype=jnp.int32)[None, :]).astype(jnp.int32)
@@ -51,12 +59,18 @@
         jnp.where(hit, mixing[0][None, :, :].astype(jnp.float32), 0.0), axis=(1, 2)
     ).astype(jnp.bfloat16)
 
-    send_rows = jnp.dot(pick, tokens_in, preferred_element_type=jnp.float32).astype(jnp.bfloat16)
-    send_grads = jnp.dot(pick, grads_in, preferred_element_type=jnp.float32).astype(jnp.bfloat16)
-
-    rows_in = exchange(send_rows, groups)
-    weight_in = exchange(slot_weight, groups)
-    grad_rows = exchange(send_grads, groups)
+    both = jnp.concatenate(
+        [tokens_in, grads_in, jnp.zeros((tok_rows, side), jnp.bfloat16)], axis=1
+    )
+    send_width = 2 * model_width + side
+    send = (
+        jnp.dot(pick, both, preferred_element_type=jnp.float32)
+        + lane_block(slot_weight, send_width, 2 * model_width)
+    ).astype(jnp.bfloat16)
+    recv = exchange(send, groups)
+    rows_in = recv[:, :model_width]
+    grad_rows = recv[:, model_width:2 * model_width]
+    weight_in = recv[:, 2 * model_width]
 
     pre_gate = jnp.dot(rows_in, gate_mat, preferred_element_type=jnp.float32)
     pre_up = jnp.dot(rows_in, up_mat, preferred_element_type=jnp.float32)
@@ -77,12 +91,18 @@
         jnp.bfloat16
     )
     up_pre = (act_grad * silu_g).astype(jnp.bfloat16)
-    in_grad = (contract_cols(gate_pre, gate_mat) + contract_cols(up_pre, up_mat)).astype(
-        jnp.bfloat16
-    )
+    pad_rows = jnp.zeros((side, hidden_units), jnp.bfloat16)
+    gate_ext = jnp.concatenate([gate_mat, pad_rows], axis=0)
+    up_ext = jnp.concatenate([up_mat, pad_rows], axis=0)
+    back_width = model_width + side
+    in_grad_ext = (
+        (contract_cols(gate_pre, gate_ext) + contract_cols(up_pre, up_ext))
+        + lane_block(prob_part, back_width, model_width)
+    ).astype(jnp.bfloat16)
 
-    back_grad = exchange(in_grad, groups)
-    back_prob = exchange(prob_part, groups)
+    back_ext = exchange(in_grad_ext, groups)
+    back_grad = back_ext[:, :model_width]
+    back_prob = back_ext[:, model_width]
 
     grad_down = contract_rows(act_rows, scaled).astype(jnp.bfloat16)
     grad_gate = contract_rows(rows_in, gate_pre).astype(jnp.bfloat16)

time: 220 us -> 201 us (0.914)
  blocking collectives: 10.7 us -> 0 us
  starting transfers between devices: 22.8 us -> 14.1 us
  waiting for transfers between devices: 113 us -> 121 us
  other arithmetic: 9.76 us -> 5.79 us
  local copies, waits for them, and re-layouts: 5.88 us -> 3.57 us
    all_to_all x1 -> x0, blocking collectives: 10.7 us -> none  [exchange(): lax.all_to_all(parted, 'expert', split_axis=0, concat_axis=0, tiled=True)]
    all_to_all x4 -> x2, starting transfers between devices: 21 us -> 12.8 us  [exchange(): lax.all_to_all(parted, 'expert', split_axis=0, concat_axis=0, tiled=True)]
    convert_element_type x4 -> x2, other arithmetic: 6.81 us -> 0.01 us  [lane_block(): return jnp.where(lanes == lane, values.astype(jnp.float32)[:, None], 0.0)]
    all_to_all x4 -> x2, waiting for transfers between devices: 105 us -> 111 us  [exchange(): lax.all_to_all(parted, 'expert', split_axis=0, concat_axis=0, tiled=True)]
    dot_general x4, matrix products: 19.8 us -> 22 us  [contract_rows(): lax.dot_general(left, right, (((0,), (0,)), ((), ())), preferred_element_...]
    dot_general x2 -> x1, matrix products: 7.67 us -> 6.15 us  [per_device(): jnp.dot(pick, both, preferred_element_type=jnp.float32)]
  transfers between devices with their start and end apart: 5 -> 3, of which waited for: 5 -> 3; matrix products, arithmetic and copies ran while one was open for 17% -> 10% of each run, Pallas kernels for 0% -> 0%
where the time goes in v4:
time: 201 us
  waiting for transfers between devices  121 us (60%)
  matrix products  55.5 us (28%)
  starting transfers between devices  14.1 us (7%)
  other arithmetic  5.79 us (3%)
  local copies, waits for them, and re-layouts  3.57 us (2%)
    all_to_all x2, waiting for transfers between devices, exchange(): lax.all_to_all(parted, 'expert', split_axis=0, concat_axis=0, tiled=True)  111 us
    dot_general x4, matrix products, contract_rows(): lax.dot_general(left, right, (((0,), (0,)), ((), ())), preferred_element_...  22 us
    all_to_all x2, starting transfers between devices, exchange(): lax.all_to_all(parted, 'expert', split_axis=0, concat_axis=0, tiled=True)  12.8 us
    dot_general x3, matrix products, contract_cols(): lax.dot_general(left, right, (((1,), (1,)), ((), ())), preferred_element_...  12.1 us
    ppermute x1, waiting for transfers between devices, shifted(): return lax.ppermute(block, axis, route)  9.56 us
    dot_general x1, matrix products, per_device(): jnp.dot(pick, both, preferred_element_type=jnp.float32)  6.15 us
    dot_general x1, matrix products, per_device(): pre_gate = jnp.dot(rows_in, gate_mat, preferred_element_type=jnp.float32)  5.45 us
    dot_general x1, matrix products, per_device(): pre_up = jnp.dot(rows_in, up_mat, preferred_element_type=jnp.float32)  5.19 us
  transfers between devices with their start and end apart: 3, of which 3 were waited for; matrix products, arithmetic and copies ran while one was open for 10% of the time, Pallas kernels for 0%

profile of v4, /device:TPU:0, one launch (start us, length us, event | category | flops | bytes accessed | tf_op | source)
XLA Modules:
  0.0 200.7 jit_solution(14182100624785905271)
XLA Ops:
  0.6 0.9 copy.33
  1.9 0.9 reduce-window.6
  5.2 6.1 %add_convert_fusion = bf16[768,4224]{1,0:T(8,128)(2,1)} fusion(pred[768,192]{0,1:T(8,128)(4,1)S(1)} %fusion.32, f32[768]{0:T(1024)S(1)} %convert_element_type.166, pred[4224]{0:T(1024)(128)(4,1)S(1)} %iota_compare_fusion.3, bf16[192,2048]{1,0:T(8,128)(2,1)} %bitcast.69, bf16[192,2048]{1,0:T(8,128)(2,1)} %bitcast.68, bf16[4224]{0:T(1024)(128)(2,1)S(1)} %pad.4.clone), kind=kOutput, calls=%fused_computation | convolution fusion | flops 1260306432 | bytes 8224128 | tf_op jit(solution)/shard_map/dot_general | solution.py:67
  11.3 7.7 %all-to-all-start = ((bf16[32,24,4224]{2,1,0:T(8,128)(2,1)}), bf16[32,24,4224]{2,1,0:T(8,128)(2,1)}, u32[]{:S(2)}, u32[]{:S(2)}) async-start(bf16[32,24,4224]{2,1,0:T(8,128)(2,1)} %bitcast.61), calls=%async_computation | async-start | bytes 12976128 | tf_op jit(solution)/shard_map/all_to_all | solution.py:28
  19.1 80.1 %all-to-all-done = bf16[32,24,4224]{2,1,0:T(8,128)(2,1)} async-done(((bf16[32,24,4224]{2,1,0:T(8,128)(2,1)}), bf16[32,24,4224]{2,1,0:T(8,128)(2,1)}, u32[]{:S(2)}, u32[]{:S(2)}) %all-to-all-start) | async-done | bytes 6488096 | tf_op jit(solution)/shard_map/all_to_all | solution.py:28
  99.2 1.1 convert_reduce_fusion.1
  100.2 5.4 %fusion.22 = f32[768,768]{1,0:T(8,128)S(1)} fusion(bf16[768,4224]{1,0:T(8,128)(2,1)} %bitcast.6, bf16[1,1,2048,768]{3,2,1,0:T(8,128)(2,1)} %param.11), kind=kOutput, calls=%fused_computation.30 | convolution fusion | flops 2415919104 | bytes 8650752 | tf_op jit(solution)/shard_map/dot_general | solution.py:75
  105.7 4.7 %fusion.8 = f32[768,768]{1,0:T(8,128)S(1)} fusion(bf16[1,1,768,2048]{3,2,1,0:T(8,128)(2,1)S(1)} %copy-done, f32[768]{0:T(1024)S(1)} %convert_reduce_fusion.1, bf16[768,4224]{1,0:T(8,128)(2,1)} %bitcast.6), kind=kOutput, calls=%fused_computation.16 | convolution fusion | flops 2420637696 | bytes 8653824 | tf_op jit(solution)/shard_map/dot_general | solution.py:20
  110.4 5.2 %multiply_convert_fusion = (bf16[768,768]{1,0:T(8,128)(2,1)S(1)}, bf16[768,768]{1,0:T(8,128)(2,1)S(1)}, bf16[768,768]{1,0:T(8,128)(2,1)S(1)}) fusion(f32[768,768]{1,0:T(8,128)S(1)} %fusion.22, f32[768,768]{1,0:T(8,128)S(1)} %fusion.8, bf16[1,1,2048,768]{3,2,1,0:T(8,128)(2,1)S(1)} %copy-done.2, bf16[768,4224]{1,0:T(8,128)(2,1)} %bitcast.6), kind=kOutput, calls=%fused_computation.23 | convolution fusion | flops 2424766464 | bytes 14548992 | tf_op jit(solution)/shard_map/dot_general | solution.py:76
  115.6 1.0 copy-done.5
  116.6 4.7 %fusion.1 = bf16[768]{0:T(1024)(128)(2,1)S(1)} fusion(bf16[768,4224]{1,0:T(8,128)(2,1)} %bitcast.6, bf16[768,768]{1,0:T(8,128)(2,1)S(1)} %get-tuple-element.5, bf16[1,1,768,2048]{3,2,1,0:T(8,128)(2,1)S(1)} %copy-done), kind=kOutput, calls=%fused_computation.5 | convolution fusion | flops 2423782656 | bytes 7472640 | tf_op jit(solution)/shard_map/dot_general | solution.py:80
  121.3 2.9 %fusion.3 = f32[768,2176]{1,0:T(8,128)S(1)} fusion(bf16[768,768]{1,0:T(8,128)(2,1)S(1)} %get-tuple-element.6, bf16[2048,768]{1,0:T(8,128)(2,1)S(1)} %bitcast.66), kind=kOutput, calls=%fused_computation.11 | convolution fusion | flops 2566914048 | bytes 11010048 | tf_op jit(solution)/shard_map/dot_general | solution.py:20
  124.2 4.5 %add_convert_fusion.1 = bf16[768,2176]{1,0:T(8,128)(2,1)} fusion(f32[768,2176]{1,0:T(8,128)S(1)} %fusion.3, bf16[768,768]{1,0:T(8,128)(2,1)S(1)} %get-tuple-element.7, f32[768]{0:T(1024)S(1)} %convert_element_type.165, bf16[2048,768]{1,0:T(8,128)(2,1)S(1)} %bitcast.67, pred[2176]{0:T(1024)(128)(4,1)S(1)} %iota_compare_fusion.4), kind=kOutput, calls=%fused_computation.3 | convolution fusion | flops 2573598720 | bytes 14357632 | tf_op jit(solution)/shard_map/dot_general | solution.py:20
  128.7 5.0 %all-to-all-start.1 = ((bf16[32,24,2176]{2,1,0:T(8,128)(2,1)}), bf16[32,24,2176]{2,1,0:T(8,128)(2,1)}, u32[]{:S(2)}, u32[]{:S(2)}) async-start(bf16[32,24,2176]{2,1,0:T(8,128)(2,1)} %bitcast.62), calls=%async_computation.1 | async-start | bytes 6684672 | tf_op jit(solution)/shard_map/all_to_all | solution.py:28
  133.8 6.7 %fusion.11 = bf16[1,1,2048,768]{3,2,1,0:T(8,128)(2,1)} fusion(bf16[768,768]{1,0:T(8,128)(2,1)} %copy-done.7, bf16[768,4224]{1,0:T(8,128)(2,1)} %bitcast.6), kind=kOutput, calls=%fused_computation.19 | convolution fusion | flops 2417491968 | bytes 7471104 | tf_op jit(solution)/shard_map/dot_general | solution.py:14
  140.5 6.1 %fusion.12 = bf16[1,1,768,2048]{3,2,1,0:T(8,128)(2,1)} fusion(bf16[768,768]{1,0:T(8,128)(2,1)S(1)} %copy-done.6, f32[768]{0:T(1024)S(1)} %convert_reduce_fusion.1, bf16[768,4224]{1,0:T(8,128)(2,1)} %bitcast.6), kind=kOutput, calls=%fused_computation.20 | convolution fusion | flops 2422210560 | bytes 7474176 | tf_op jit(solution)/shard_map/dot_general | solution.py:14
  146.6 31.2 %all-to-all-done.1 = bf16[32,24,2176]{2,1,0:T(8,128)(2,1)} async-done(((bf16[32,24,2176]{2,1,0:T(8,128)(2,1)}), bf16[32,24,2176]{2,1,0:T(8,128)(2,1)}, u32[]{:S(2)}, u32[]{:S(2)}) %all-to-all-start.1) | async-done | bytes 3342368 | tf_op jit(solution)/shard_map/all_to_all | solution.py:28
  177.8 3.0 %fusion.16 = bf16[192,2048]{1,0:T(8,128)(2,1)S(1)} fusion(pred[768,192]{0,1:T(8,128)(4,1)S(1)} %fusion.32, bf16[768,2176]{1,0:T(8,128)(2,1)} %bitcast.14, bf16[1,192,2048]{2,1,0:T(8,128)(2,1)} %param.8), kind=kOutput, calls=%fused_computation.22 | convolution fusion | flops 605159424 | bytes 4866048 | tf_op jit(solution)/shard_map/dot_general | solution.py:14
  180.7 1.3 collective-permute-start
  182.0 6.3 %fusion.10 = bf16[1,1,2048,768]{3,2,1,0:T(8,128)(2,1)} fusion(bf16[768,768]{1,0:T(8,128)(2,1)S(1)} %copy-done.4, bf16[768,4224]{1,0:T(8,128)(2,1)} %bitcast.6), kind=kOutput, calls=%fused_computation.18 | convolution fusion | flops 2417491968 | bytes 7471104 | tf_op jit(solution)/shard_map/dot_general | solution.py:14
  188.3 1.1 convert_reduce_fusion
  189.4 0.8 select_reduce_fusion
  190.2 9.6 %collective-permute-done = bf16[192,2048]{1,0:T(8,128)(2,1)S(1)} collective-permute-done((bf16[192,2048]{1,0:T(8,128)(2,1)S(1)}, bf16[192,2048]{1,0:T(8,128)(2,1)S(1)}, u32[]{:S(2)}, u32[]{:S(2)}) %collective-permute-start) | collective-permute-done | bytes 786464 | tf_op jit(solution)/shard_map/ppermute | solution.py:10
  199.8 0.9 copy.40
  (33 shorter events, 2.7 us)
Async XLA Ops:
  0.6 105.0 %copy-start = (bf16[1,1,768,2048]{3,2,1,0:T(8,128)(2,1)S(1)}, bf16[1,1,768,2048]{3,2,1,0:T(8,128)(2,1)}, u32[]{:S(2)}) copy-start(bf16[1,1,768,2048]{3,2,1,0:T(8,128)(2,1)} %param.13) | copy-start | bytes 9437188
  11.3 87.8 %all-to-all-start = ((bf16[32,24,4224]{2,1,0:T(8,128)(2,1)}), bf16[32,24,4224]{2,1,0:T(8,128)(2,1)}, u32[]{:S(2)}, u32[]{:S(2)}) async-start(bf16[32,24,4224]{2,1,0:T(8,128)(2,1)} %bitcast.61), calls=%async_computation | async-start | bytes 12976128 | tf_op jit(solution)/shard_map/all_to_all | solution.py:28
  105.7 4.7 %copy-start.2 = (bf16[1,1,2048,768]{3,2,1,0:T(8,128)(2,1)S(1)}, bf16[1,1,2048,768]{3,2,1,0:T(8,128)(2,1)}, u32[]{:S(2)}) copy-start(bf16[1,1,2048,768]{3,2,1,0:T(8,128)(2,1)} %param.12) | copy-start | bytes 9437188
  115.6 1.0 copy-start.5
  115.6 5.7 %copy-start.3 = (bf16[768,768]{1,0:T(8,128)(2,1)}, bf16[768,768]{1,0:T(8,128)(2,1)S(1)}, u32[]{:S(2)}) copy-start(bf16[768,768]{1,0:T(8,128)(2,1)S(1)} %get-tuple-element.6) | copy-start | bytes 3538948
  115.6 8.6 %copy-start.7 = (bf16[768,768]{1,0:T(8,128)(2,1)}, bf16[768,768]{1,0:T(8,128)(2,1)S(1)}, u32[]{:S(2)}) copy-start(bf16[768,768]{1,0:T(8,128)(2,1)S(1)} %get-tuple-element.7) | copy-start | bytes 3538948
  116.6 4.7 %copy-start.1 = (bf16[1,1,2048,768]{3,2,1,0:T(8,128)(2,1)S(1)}, bf16[1,1,2048,768]{3,2,1,0:T(8,128)(2,1)}, u32[]{:S(2)}) copy-start(bf16[1,1,2048,768]{3,2,1,0:T(8,128)(2,1)} %param.11) | copy-start | bytes 9437188
  128.7 49.0 %all-to-all-start.1 = ((bf16[32,24,2176]{2,1,0:T(8,128)(2,1)}), bf16[32,24,2176]{2,1,0:T(8,128)(2,1)}, u32[]{:S(2)}, u32[]{:S(2)}) async-start(bf16[32,24,2176]{2,1,0:T(8,128)(2,1)} %bitcast.62), calls=%async_computation.1 | async-start | bytes 6684672 | tf_op jit(solution)/shard_map/all_to_all | solution.py:28
  133.8 6.7 %copy-start.6 = (bf16[768,768]{1,0:T(8,128)(2,1)S(1)}, bf16[768,768]{1,0:T(8,128)(2,1)}, u32[]{:S(2)}) copy-start(bf16[768,768]{1,0:T(8,128)(2,1)} %copy-done.5) | copy-start | bytes 3538948
  177.8 4.3 %copy-start.4 = (bf16[768,768]{1,0:T(8,128)(2,1)S(1)}, bf16[768,768]{1,0:T(8,128)(2,1)}, u32[]{:S(2)}) copy-start(bf16[768,768]{1,0:T(8,128)(2,1)} %copy-done.3) | copy-start | bytes 3538948
  180.7 19.0 %collective-permute-start = (bf16[192,2048]{1,0:T(8,128)(2,1)S(1)}, bf16[192,2048]{1,0:T(8,128)(2,1)S(1)}, u32[]{:S(2)}, u32[]{:S(2)}) collective-permute-start(bf16[192,2048]{1,0:T(8,128)(2,1)S(1)} %fusion.16), channel_id=1, source_target_pairs={{32,0},{64,32},{96,64},{33,1},{65,33},{97,65},{34,2},{66,34},{98,6... | collective-permute-start | bytes 2359304 | tf_op jit(solution)/shard_map/ppermute | solution.py:10

commit v5 on v3

--- a/solution.py
+++ b/solution.py
@@ -94,9 +94,8 @@
         jnp.bfloat16
     )
 
-    back_ext = exchange(jnp.concatenate([in_grad, side_block(prob_part)], axis=1), groups)
-    back_grad = back_ext[:, :model_width]
-    back_prob = back_ext[:, model_width]
+    back_grad = exchange(in_grad, groups)
+    back_prob = exchange(prob_part, groups)
 
     grad_down = contract_rows(act_rows, scaled).astype(jnp.bfloat16)
     grad_gate = contract_rows(rows_in, gate_pre).astype(jnp.bfloat16)

time: 198 us -> 201 us (1.015)
  starting transfers between devices: 18.9 us -> 22.9 us
  other arithmetic: 13.4 us -> 10 us
  matrix products: 55.1 us -> 58.5 us
  waiting for transfers between devices: 106 us -> 103 us
    all_to_all x3 -> x4, waiting for transfers between devices: 96.6 us -> 89.5 us  [exchange(): lax.all_to_all(parted, 'expert', split_axis=0, concat_axis=0, tiled=True)]
    ppermute x1, waiting for transfers between devices: 9.42 us -> 13.4 us  [shifted(): return lax.ppermute(block, axis, route)]
    all_to_all x3 -> x4, starting transfers between devices: 17.6 us -> 21.6 us  [exchange(): lax.all_to_all(parted, 'expert', split_axis=0, concat_axis=0, tiled=True)]
    dot_general x3, matrix products: 11 us -> 13.3 us  [contract_cols(): lax.dot_general(left, right, (((1,), (1,)), ((), ())), preferred_element_...]
    concatenate x1 -> x0, other arithmetic: 2.08 us -> none  [per_device(): jnp.concatenate([in_grad, side_block(prob_part)], axis=1)]
  transfers between devices with their start and end apart: 4 -> 5, of which waited for: 4 -> 4; matrix products, arithmetic and copies ran while one was open for 21% -> 25% of each run, Pallas kernels for 0% -> 0%
where the time goes in v5:
time: 201 us; the launch traced here: 200 us
  waiting for transfers between devices  103 us (51%)
  matrix products  58.5 us (29%)
  starting transfers between devices  22.9 us (11%)
  other arithmetic  10 us (5%)
  local copies, waits for them, and re-layouts  4.65 us (2%)
    all_to_all x4, waiting for transfers between devices, exchange(): lax.all_to_all(parted, 'expert', split_axis=0, concat_axis=0, tiled=True)  89.5 us
    dot_general x4, matrix products, contract_rows(): lax.dot_general(left, right, (((0,), (0,)), ((), ())), preferred_element_...  22.9 us
    all_to_all x4, starting transfers between devices, exchange(): lax.all_to_all(parted, 'expert', split_axis=0, concat_axis=0, tiled=True)  21.6 us
    ppermute x1, waiting for transfers between devices, shifted(): return lax.ppermute(block, axis, route)  13.4 us
    dot_general x3, matrix products, contract_cols(): lax.dot_general(left, right, (((1,), (1,)), ((), ())), preferred_element_...  13.3 us
    dot_general x1, matrix products, per_device(): pre_up = jnp.dot(rows_in, up_mat, preferred_element_type=jnp.float32)  6.88 us
    dot_general x1, matrix products, per_device(): pre_gate = jnp.dot(rows_in, gate_mat, preferred_element_type=jnp.float32)  5.58 us
  transfers between devices with their start and end apart: 5, of which 4 were waited for; matrix products, arithmetic and copies ran while one was open for 25% of the time, Pallas kernels for 0%

profile of v5, /device:TPU:0, one launch (start us, length us, event | category | flops | bytes accessed | tf_op | source)
XLA Modules:
  0.0 199.9 jit_solution(16598826598224084266)
XLA Ops:
  4.2 3.8 %convolution_convert_fusion.5 = bf16[768,2048]{1,0:T(8,128)(2,1)} fusion(pred[768,192]{0,1:T(8,128)(4,1)S(1)} %fusion.16, bf16[1,192,2048]{2,1,0:T(8,128)(2,1)} %param.7), kind=kOutput, calls=%fused_computation.10 | convolution fusion | flops 605552640 | bytes 4079616 | tf_op jit(solution)/shard_map/dot_general | solution.py:57
  8.1 7.7 %all-to-all-start = ((bf16[32,24,2048]{2,1,0:T(8,128)(2,1)}), bf16[32,24,2048]{2,1,0:T(8,128)(2,1)}, u32[]{:S(2)}, u32[]{:S(2)}) async-start(bf16[32,24,2048]{2,1,0:T(8,128)(2,1)} %bitcast.78), calls=%async_computation | async-start | bytes 6291456 | tf_op jit(solution)/shard_map/all_to_all | solution.py:28
  16.2 2.2 %convolution_convert_fusion.4 = bf16[768,2048]{1,0:T(8,128)(2,1)S(1)} fusion(pred[768,192]{0,1:T(8,128)(4,1)S(1)} %fusion.16, bf16[1,192,2048]{2,1,0:T(8,128)(2,1)} %param.8), kind=kOutput, calls=%fused_computation.9 | convolution fusion | flops 605552640 | bytes 4079616 | tf_op jit(solution)/shard_map/dot_general | solution.py:58
  18.3 2.0 %pad_maximum_fusion = bf16[768,2176]{1,0:T(8,128)(2,1)} fusion(bf16[768,128]{1,0:T(8,128)(2,1)S(1)} %broadcast_select_fusion, bf16[768,2048]{1,0:T(8,128)(2,1)S(1)} %convolution_convert_fusion.4), kind=kLoop, calls=%fused_computation.11 | loop fusion | flops 6684672 | bytes 6684672 | tf_op jit(solution)/shard_map/concatenate | solution.py:62
  20.4 37.4 %all-to-all-done = bf16[32,24,2048]{2,1,0:T(8,128)(2,1)} async-done(((bf16[32,24,2048]{2,1,0:T(8,128)(2,1)}), bf16[32,24,2048]{2,1,0:T(8,128)(2,1)}, u32[]{:S(2)}, u32[]{:S(2)}) %all-to-all-start) | async-done | bytes 3145760 | tf_op jit(solution)/shard_map/all_to_all | solution.py:28
  57.8 5.0 %all-to-all-start.1 = ((bf16[32,24,2176]{2,1,0:T(8,128)(2,1)}), bf16[32,24,2176]{2,1,0:T(8,128)(2,1)}, u32[]{:S(2)}, u32[]{:S(2)}) async-start(bf16[32,24,2176]{2,1,0:T(8,128)(2,1)} %bitcast.77), calls=%async_computation.1 | async-start | bytes 6684672 | tf_op jit(solution)/shard_map/all_to_all | solution.py:28
  62.8 5.6 %fusion.7 = f32[768,768]{1,0:T(8,128)S(1)} fusion(bf16[768,2048]{1,0:T(8,128)(2,1)} %bitcast.4, bf16[1,1,2048,768]{3,2,1,0:T(8,128)(2,1)} %param.11), kind=kOutput, calls=%fused_computation.17 | convolution fusion | flops 2415919104 | bytes 8650752 | tf_op jit(solution)/shard_map/dot_general | solution.py:69
  68.4 6.9 %multiply_convert_fusion.2 = (bf16[768,768]{1,0:T(8,128)(2,1)S(1)}, f32[768,768]{1,0:T(8,128)}) fusion(f32[768,768]{1,0:T(8,128)S(1)} %fusion.7, bf16[768,2048]{1,0:T(8,128)(2,1)} %bitcast.4, bf16[1,1,2048,768]{3,2,1,0:T(8,128)(2,1)S(1)} %copy-done.3), kind=kOutput, calls=%fused_computation.30 | convolution fusion | flops 2419458048 | bytes 12189696 | tf_op jit(solution)/shard_map/dot_general | solution.py:70
  75.3 4.0 %convolution_convert_fusion.3 = bf16[768,2048]{1,0:T(8,128)(2,1)} fusion(bf16[768,768]{1,0:T(8,128)(2,1)S(1)} %get-tuple-element.11, bf16[1,1,768,2048]{3,2,1,0:T(8,128)(2,1)S(1)} %copy-done), kind=kOutput, calls=%fused_computation.8 | convolution fusion | flops 2417491968 | bytes 7471104 | tf_op jit(solution)/shard_map/dot_general | solution.py:74
  79.3 27.6 %all-to-all-done.1 = bf16[32,24,2176]{2,1,0:T(8,128)(2,1)} async-done(((bf16[32,24,2176]{2,1,0:T(8,128)(2,1)}), bf16[32,24,2176]{2,1,0:T(8,128)(2,1)}, u32[]{:S(2)}, u32[]{:S(2)}) %all-to-all-start.1) | async-done | bytes 3342368 | tf_op jit(solution)/shard_map/all_to_all | solution.py:28
  107.9 6.6 %multiply_convert_fusion = (bf16[768,768]{1,0:T(8,128)(2,1)S(1)}, bf16[768,768]{1,0:T(8,128)(2,1)S(1)}) fusion(f32[768,768]{1,0:T(8,128)} %copy-done.7, f32[768,768]{1,0:T(8,128)} %get-tuple-element.9, bf16[1,1,768,2048]{3,2,1,0:T(8,128)(2,1)S(1)} %copy-done, f32[768]{0:T(1024)S(1)} %convert_reduce_fusion, bf16[768,2176]{1,0:T(8,128)(2,1)} %bitcast.8), kind=kOutput, calls=%fused_computation.27 | convolution fusion | flops 2428305408 | bytes 13372416 | tf_op jit(solution)/shard_map/dot_general | solution.py:20
  114.6 2.6 %fusion.5 = f32[768,2048]{1,0:T(8,128)S(1)} fusion(bf16[768,768]{1,0:T(8,128)(2,1)S(1)} %get-tuple-element.14, bf16[1,1,2048,768]{3,2,1,0:T(8,128)(2,1)S(1)} %copy-done.2), kind=kOutput, calls=%fused_computation.15 | convolution fusion | flops 2415919104 | bytes 10616832 | tf_op jit(solution)/shard_map/dot_general | solution.py:20
  117.3 4.0 %add_convert_fusion = bf16[768,2048]{1,0:T(8,128)(2,1)} fusion(f32[768,2048]{1,0:T(8,128)S(1)} %fusion.5, bf16[768,768]{1,0:T(8,128)(2,1)S(1)} %get-tuple-element.13, bf16[1,1,2048,768]{3,2,1,0:T(8,128)(2,1)S(1)} %copy-done.4), kind=kOutput, calls=%fused_computation.4 | convolution fusion | flops 2419064832 | bytes 13762560 | tf_op jit(solution)/shard_map/dot_general | solution.py:20
  121.3 5.1 %all-to-all-start.2 = ((bf16[32,24,2048]{2,1,0:T(8,128)(2,1)}), bf16[32,24,2048]{2,1,0:T(8,128)(2,1)}, u32[]{:S(2)}, u32[]{:S(2)}) async-start(bf16[32,24,2048]{2,1,0:T(8,128)(2,1)} %bitcast.79), calls=%async_computation.2 | async-start | bytes 6291456 | tf_op jit(solution)/shard_map/all_to_all | solution.py:28
  126.3 3.7 %fusion.1 = bf16[768]{0:T(1024)(128)(2,1)S(1)} fusion(bf16[768,2048]{1,0:T(8,128)(2,1)} %convolution_convert_fusion.3, bf16[768,2176]{1,0:T(8,128)(2,1)} %bitcast.8), kind=kLoop, calls=%fused_computation.3 | loop fusion | flops 6290688 | bytes 6292992 | tf_op jit(solution)/shard_map/reduce_sum | solution.py:82
  130.8 6.7 %fusion.13 = bf16[1,1,2048,768]{3,2,1,0:T(8,128)(2,1)} fusion(bf16[768,2048]{1,0:T(8,128)(2,1)} %bitcast.4, bf16[768,768]{1,0:T(8,128)(2,1)} %copy-done.10), kind=kOutput, calls=%fused_computation.23 | convolution fusion | flops 2417491968 | bytes 7471104 | tf_op jit(solution)/shard_map/dot_general | solution.py:14
  137.4 6.1 %fusion.14 = bf16[1,1,768,2048]{3,2,1,0:T(8,128)(2,1)} fusion(bf16[768,768]{1,0:T(8,128)(2,1)S(1)} %copy-done.9, f32[768]{0:T(1024)S(1)} %convert_reduce_fusion, bf16[768,2176]{1,0:T(8,128)(2,1)} %bitcast.8), kind=kOutput, calls=%fused_computation.24 | convolution fusion | flops 2422210560 | bytes 7474176 | tf_op jit(solution)/shard_map/dot_general | solution.py:14
  143.5 24.6 %all-to-all-done.2 = bf16[32,24,2048]{2,1,0:T(8,128)(2,1)} async-done(((bf16[32,24,2048]{2,1,0:T(8,128)(2,1)}), bf16[32,24,2048]{2,1,0:T(8,128)(2,1)}, u32[]{:S(2)}, u32[]{:S(2)}) %all-to-all-start.2) | async-done | bytes 3145760 | tf_op jit(solution)/shard_map/all_to_all | solution.py:28
  168.1 3.8 %all-to-all-start.3 = ((bf16[32,1,24]{2,1,0:T(2,128)(2,1)}), bf16[32,1,24]{2,1,0:T(2,128)(2,1)S(1)}, u32[]{:S(2)}, u32[]{:S(2)}) async-start(bf16[32,1,24]{2,1,0:T(2,128)(2,1)} %convert_element_type.123), calls=%async_computation.3 | async-start | bytes 32768 | tf_op jit(solution)/shard_map/all_to_all | solution.py:28
  172.0 3.8 %fusion.15 = bf16[192,2048]{1,0:T(8,128)(2,1)} fusion(pred[768,192]{0,1:T(8,128)(4,1)S(1)} %fusion.16, bf16[768,2048]{1,0:T(8,128)(2,1)} %bitcast.16, bf16[1,192,2048]{2,1,0:T(8,128)(2,1)} %param.8), kind=kOutput, calls=%fused_computation.26 | convolution fusion | flops 605159424 | bytes 4866048 | tf_op jit(solution)/shard_map/dot_general | solution.py:14
  175.8 1.3 collective-permute-start
  177.1 6.2 %fusion.12 = bf16[1,1,2048,768]{3,2,1,0:T(8,128)(2,1)} fusion(bf16[768,2048]{1,0:T(8,128)(2,1)} %bitcast.4, bf16[768,768]{1,0:T(8,128)(2,1)S(1)} %copy-done.6), kind=kOutput, calls=%fused_computation.22 | convolution fusion | flops 2417491968 | bytes 7471104 | tf_op jit(solution)/shard_map/dot_general | solution.py:14
  184.4 13.4 %collective-permute-done = bf16[192,2048]{1,0:T(8,128)(2,1)} collective-permute-done((bf16[192,2048]{1,0:T(8,128)(2,1)}, bf16[192,2048]{1,0:T(8,128)(2,1)}, u32[]{:S(2)}, u32[]{:S(2)}) %collective-permute-start) | collective-permute-done | bytes 786464 | tf_op jit(solution)/shard_map/ppermute | solution.py:10
  197.8 2.1 %copy.42 = bf16[1,192,2048]{2,1,0:T(8,128)(2,1)} copy(bf16[1,192,2048]{2,1,0:T(8,128)(2,1)} %bitcast.17) | data formatting | bytes 1572864
  (44 shorter events, 6.8 us)
Async XLA Ops:
  0.6 74.7 %copy-start = (bf16[1,1,768,2048]{3,2,1,0:T(8,128)(2,1)S(1)}, bf16[1,1,768,2048]{3,2,1,0:T(8,128)(2,1)}, u32[]{:S(2)}) copy-start(bf16[1,1,768,2048]{3,2,1,0:T(8,128)(2,1)} %param.13) | copy-start | bytes 9437188
  8.1 7.7 %copy-start.1 = (bf16[1,192,2]{1,2,0:T(2,128)(2,1)S(1)}, bf16[1,192,2]{1,2,0:T(2,128)(2,1)}, u32[]{:S(2)}) copy-start(bf16[1,192,2]{1,2,0:T(2,128)(2,1)} %param.10) | copy-start | bytes 2308
  8.1 49.7 %all-to-all-start = ((bf16[32,24,2048]{2,1,0:T(8,128)(2,1)}), bf16[32,24,2048]{2,1,0:T(8,128)(2,1)}, u32[]{:S(2)}, u32[]{:S(2)}) async-start(bf16[32,24,2048]{2,1,0:T(8,128)(2,1)} %bitcast.78), calls=%async_computation | async-start | bytes 6291456 | tf_op jit(solution)/shard_map/all_to_all | solution.py:28
  57.8 49.0 %all-to-all-start.1 = ((bf16[32,24,2176]{2,1,0:T(8,128)(2,1)}), bf16[32,24,2176]{2,1,0:T(8,128)(2,1)}, u32[]{:S(2)}, u32[]{:S(2)}) async-start(bf16[32,24,2176]{2,1,0:T(8,128)(2,1)} %bitcast.77), calls=%async_computation.1 | async-start | bytes 6684672 | tf_op jit(solution)/shard_map/all_to_all | solution.py:28
  62.8 5.6 %copy-start.3 = (bf16[1,1,2048,768]{3,2,1,0:T(8,128)(2,1)S(1)}, bf16[1,1,2048,768]{3,2,1,0:T(8,128)(2,1)}, u32[]{:S(2)}) copy-start(bf16[1,1,2048,768]{3,2,1,0:T(8,128)(2,1)} %param.12) | copy-start | bytes 9437188
  68.4 6.9 %copy-start.7 = (f32[768,768]{1,0:T(8,128)}, f32[768,768]{1,0:T(8,128)S(1)}, u32[]{:S(2)}) copy-start(f32[768,768]{1,0:T(8,128)S(1)} %fusion.7) | copy-start | bytes 7077892
  75.3 4.0 %copy-start.8 = (bf16[768,768]{1,0:T(8,128)(2,1)}, bf16[768,768]{1,0:T(8,128)(2,1)S(1)}, u32[]{:S(2)}) copy-start(bf16[768,768]{1,0:T(8,128)(2,1)S(1)} %get-tuple-element.11) | copy-start | bytes 3538948
  107.9 6.7 %copy-start.2 = (bf16[1,1,2048,768]{3,2,1,0:T(8,128)(2,1)S(1)}, bf16[1,1,2048,768]{3,2,1,0:T(8,128)(2,1)}, u32[]{:S(2)}) copy-start(bf16[1,1,2048,768]{3,2,1,0:T(8,128)(2,1)} %param.11) | copy-start | bytes 9437188
  114.5 2.7 %copy-start.5 = (bf16[768,768]{1,0:T(8,128)(2,1)}, bf16[768,768]{1,0:T(8,128)(2,1)S(1)}, u32[]{:S(2)}) copy-start(bf16[768,768]{1,0:T(8,128)(2,1)S(1)} %get-tuple-element.14) | copy-start | bytes 3538948
  114.5 2.7 %copy-start.10 = (bf16[768,768]{1,0:T(8,128)(2,1)}, bf16[768,768]{1,0:T(8,128)(2,1)S(1)}, u32[]{:S(2)}) copy-start(bf16[768,768]{1,0:T(8,128)(2,1)S(1)} %get-tuple-element.13) | copy-start | bytes 3538948
  114.6 2.7 %copy-start.4 = (bf16[1,1,2048,768]{3,2,1,0:T(8,128)(2,1)S(1)}, bf16[1,1,2048,768]{3,2,1,0:T(8,128)(2,1)}, u32[]{:S(2)}) copy-start(bf16[1,1,2048,768]{3,2,1,0:T(8,128)(2,1)} %param.12) | copy-start | bytes 9437188
  121.3 46.8 %all-to-all-start.2 = ((bf16[32,24,2048]{2,1,0:T(8,128)(2,1)}), bf16[32,24,2048]{2,1,0:T(8,128)(2,1)}, u32[]{:S(2)}, u32[]{:S(2)}) async-start(bf16[32,24,2048]{2,1,0:T(8,128)(2,1)} %bitcast.79), calls=%async_computation.2 | async-start | bytes 6291456 | tf_op jit(solution)/shard_map/all_to_all | solution.py:28
  130.8 6.7 %copy-start.9 = (bf16[768,768]{1,0:T(8,128)(2,1)S(1)}, bf16[768,768]{1,0:T(8,128)(2,1)}, u32[]{:S(2)}) copy-start(bf16[768,768]{1,0:T(8,128)(2,1)} %copy-done.8) | copy-start | bytes 3538948
  168.1 15.2 %all-to-all-start.3 = ((bf16[32,1,24]{2,1,0:T(2,128)(2,1)}), bf16[32,1,24]{2,1,0:T(2,128)(2,1)S(1)}, u32[]{:S(2)}, u32[]{:S(2)}) async-start(bf16[32,1,24]{2,1,0:T(2,128)(2,1)} %convert_element_type.123), calls=%async_computation.3 | async-start | bytes 32768 | tf_op jit(solution)/shard_map/all_to_all | solution.py:28
  172.0 5.1 %copy-start.6 = (bf16[768,768]{1,0:T(8,128)(2,1)S(1)}, bf16[768,768]{1,0:T(8,128)(2,1)}, u32[]{:S(2)}) copy-start(bf16[768,768]{1,0:T(8,128)(2,1)} %copy-done.5) | copy-start | bytes 3538948
  175.8 22.0 %collective-permute-start = (bf16[192,2048]{1,0:T(8,128)(2,1)}, bf16[192,2048]{1,0:T(8,128)(2,1)}, u32[]{:S(2)}, u32[]{:S(2)}) collective-permute-start(bf16[192,2048]{1,0:T(8,128)(2,1)} %fusion.15), channel_id=1, source_target_pairs={{32,0},{64,32},{96,64},{33,1},{65,33},{97,65},{34,2},{66,34},{98,6... | collective-permute-start | bytes 2359304 | tf_op jit(solution)/shard_map/ppermute | solution.py:10

commit v6 on v5

--- a/solution.py
+++ b/solution.py
@@ -34,7 +34,7 @@
     return jnp.where(lanes == 0, values[:, None], jnp.zeros((), values.dtype))
 
 
-def per_device(hidden_in, out_grad, routes, mixing, w_gate, w_up, w_down):
+def device_body(hidden_in, out_grad, routes, mixing, w_gate, w_up, w_down):
     tokens_in = hidden_in[0]
     grads_in = out_grad[0]
     groups = lax.axis_size("expert")
@@ -101,13 +101,18 @@
     grad_gate = contract_rows(rows_in, gate_pre).astype(jnp.bfloat16)
     grad_up = contract_rows(rows_in, up_pre).astype(jnp.bfloat16)
 
-    input_grad = (
-        grads_in.astype(jnp.float32) + contract_rows(pick, back_grad)
-    ).astype(jnp.bfloat16)
+    half = tok_rows // 2 if tok_rows % 16 == 0 else tok_rows
+    handed_parts = []
+    for lo in range(0, tok_rows, half):
+        part = (
+            grads_in[lo:lo + half].astype(jnp.float32)
+            + contract_rows(pick[:, lo:lo + half], back_grad)
+        ).astype(jnp.bfloat16)
+        handed_parts.append(shifted(part, "section", -1))
+    handed = jnp.concatenate(handed_parts, axis=0)
     prob_grad = jnp.sum(
         jnp.where(hit, back_prob.astype(jnp.float32)[:, None, None], 0.0), axis=0
     ).astype(jnp.bfloat16)
-    handed = shifted(input_grad, "section", -1)
     return (
         grad_gate[None, None],
         grad_up[None, None],
@@ -128,7 +133,7 @@
         P("section", "expert", None, None),
     )
     return jax.shard_map(
-        per_device,
+        device_body,
         mesh=mesh,
         in_specs=placed,
         out_specs=(

time: 201 us -> 204 us (1.015)
  waiting for transfers between devices: 103 us -> 99.6 us
  other arithmetic: 10 us -> 13.3 us
  matrix products: 58.5 us -> 61.4 us
    ppermute x1 -> x2, waiting for transfers between devices: 13.4 us -> 10.1 us  [shifted(): return lax.ppermute(block, axis, route)]
    dot_general x4 -> x5, matrix products: 22.9 us -> 25.7 us  [contract_rows(): lax.dot_general(left, right, (((0,), (0,)), ((), ())), preferred_element_...]
    unnamed x24 -> x27, local copies, waits for them, and re-layouts: 3.15 us -> 1.07 us
  transfers between devices with their start and end apart: 5 -> 6, of which waited for: 4 -> 5; matrix products, arithmetic and copies ran while one was open for 25% -> 27% of each run, Pallas kernels for 0% -> 0%
where the time goes in v6:
time: 204 us; the launch traced here: 203 us
  waiting for transfers between devices  99.6 us (49%)
  matrix products  61.4 us (30%)
  starting transfers between devices  24.8 us (12%)
  other arithmetic  13.3 us (7%)
  local copies, waits for them, and re-layouts  3.17 us (2%)
    all_to_all x4, waiting for transfers between devices, exchange(): lax.all_to_all(parted, 'expert', split_axis=0, concat_axis=0, tiled=True)  89.5 us
    dot_general x5, matrix products, contract_rows(): lax.dot_general(left, right, (((0,), (0,)), ((), ())), preferred_element_...  25.7 us
    all_to_all x4, starting transfers between devices, exchange(): lax.all_to_all(parted, 'expert', split_axis=0, concat_axis=0, tiled=True)  22.3 us
    dot_general x3, matrix products, contract_cols(): lax.dot_general(left, right, (((1,), (1,)), ((), ())), preferred_element_...  13.3 us
    ppermute x2, waiting for transfers between devices, shifted(): return lax.ppermute(block, axis, route)  10.1 us
    dot_general x1, matrix products, device_body(): pre_up = jnp.dot(rows_in, up_mat, preferred_element_type=jnp.float32)  6.88 us
    dot_general x1, matrix products, device_body(): pre_gate = jnp.dot(rows_in, gate_mat, preferred_element_type=jnp.float32)  5.58 us
  transfers between devices with their start and end apart: 6, of which 5 were waited for; matrix products, arithmetic and copies ran while one was open for 27% of the time, Pallas kernels for 0%

profile of v6, /device:TPU:0, one launch (start us, length us, event | category | flops | bytes accessed | tf_op | source)
XLA Modules:
  0.0 203.3 jit_solution(9726096731741164959)
XLA Ops:
  4.2 3.8 %convolution_convert_fusion.5 = bf16[768,2048]{1,0:T(8,128)(2,1)} fusion(pred[768,192]{0,1:T(8,128)(4,1)S(1)} %fusion.17, bf16[1,192,2048]{2,1,0:T(8,128)(2,1)} %param.7), kind=kOutput, calls=%fused_computation.10 | convolution fusion | flops 605552640 | bytes 4079616 | tf_op jit(solution)/shard_map/dot_general | solution.py:57
  8.1 7.7 %all-to-all-start = ((bf16[32,24,2048]{2,1,0:T(8,128)(2,1)}), bf16[32,24,2048]{2,1,0:T(8,128)(2,1)}, u32[]{:S(2)}, u32[]{:S(2)}) async-start(bf16[32,24,2048]{2,1,0:T(8,128)(2,1)} %bitcast.84), calls=%async_computation | async-start | bytes 6291456 | tf_op jit(solution)/shard_map/all_to_all | solution.py:28
  16.2 2.2 %convolution_convert_fusion.4 = bf16[768,2048]{1,0:T(8,128)(2,1)S(1)} fusion(pred[768,192]{0,1:T(8,128)(4,1)S(1)} %fusion.17, bf16[1,192,2048]{2,1,0:T(8,128)(2,1)} %param.8), kind=kOutput, calls=%fused_computation.9 | convolution fusion | flops 605552640 | bytes 4079616 | tf_op jit(solution)/shard_map/dot_general | solution.py:58
  18.4 2.0 %pad_maximum_fusion = bf16[768,2176]{1,0:T(8,128)(2,1)} fusion(bf16[768,128]{1,0:T(8,128)(2,1)S(1)} %broadcast_select_fusion, bf16[768,2048]{1,0:T(8,128)(2,1)S(1)} %convolution_convert_fusion.4), kind=kLoop, calls=%fused_computation.11 | loop fusion | flops 6684672 | bytes 6684672 | tf_op jit(solution)/shard_map/concatenate | solution.py:62
  20.4 37.4 %all-to-all-done = bf16[32,24,2048]{2,1,0:T(8,128)(2,1)} async-done(((bf16[32,24,2048]{2,1,0:T(8,128)(2,1)}), bf16[32,24,2048]{2,1,0:T(8,128)(2,1)}, u32[]{:S(2)}, u32[]{:S(2)}) %all-to-all-start) | async-done | bytes 3145760 | tf_op jit(solution)/shard_map/all_to_all | solution.py:28
  57.8 5.0 %all-to-all-start.1 = ((bf16[32,24,2176]{2,1,0:T(8,128)(2,1)}), bf16[32,24,2176]{2,1,0:T(8,128)(2,1)}, u32[]{:S(2)}, u32[]{:S(2)}) async-start(bf16[32,24,2176]{2,1,0:T(8,128)(2,1)} %bitcast.83), calls=%async_computation.1 | async-start | bytes 6684672 | tf_op jit(solution)/shard_map/all_to_all | solution.py:28
  62.8 5.6 %fusion.7 = f32[768,768]{1,0:T(8,128)S(1)} fusion(bf16[768,2048]{1,0:T(8,128)(2,1)} %bitcast.4, bf16[1,1,2048,768]{3,2,1,0:T(8,128)(2,1)} %param.11), kind=kOutput, calls=%fused_computation.17 | convolution fusion | flops 2415919104 | bytes 8650752 | tf_op jit(solution)/shard_map/dot_general | solution.py:69
  68.4 6.9 %multiply_convert_fusion.2 = (bf16[768,768]{1,0:T(8,128)(2,1)S(1)}, f32[768,768]{1,0:T(8,128)}) fusion(f32[768,768]{1,0:T(8,128)S(1)} %fusion.7, bf16[768,2048]{1,0:T(8,128)(2,1)} %bitcast.4, bf16[1,1,2048,768]{3,2,1,0:T(8,128)(2,1)S(1)} %copy-done.5), kind=kOutput, calls=%fused_computation.30 | convolution fusion | flops 2419458048 | bytes 12189696 | tf_op jit(solution)/shard_map/dot_general | solution.py:70
  75.3 4.0 %convolution_convert_fusion.3 = bf16[768,2048]{1,0:T(8,128)(2,1)} fusion(bf16[768,768]{1,0:T(8,128)(2,1)S(1)} %get-tuple-element.11, bf16[1,1,768,2048]{3,2,1,0:T(8,128)(2,1)S(1)} %copy-done), kind=kOutput, calls=%fused_computation.8 | convolution fusion | flops 2417491968 | bytes 7471104 | tf_op jit(solution)/shard_map/dot_general | solution.py:74
  79.3 27.6 %all-to-all-done.1 = bf16[32,24,2176]{2,1,0:T(8,128)(2,1)} async-done(((bf16[32,24,2176]{2,1,0:T(8,128)(2,1)}), bf16[32,24,2176]{2,1,0:T(8,128)(2,1)}, u32[]{:S(2)}, u32[]{:S(2)}) %all-to-all-start.1) | async-done | bytes 3342368 | tf_op jit(solution)/shard_map/all_to_all | solution.py:28
  107.9 6.6 %multiply_convert_fusion = (bf16[768,768]{1,0:T(8,128)(2,1)S(1)}, bf16[768,768]{1,0:T(8,128)(2,1)S(1)}) fusion(f32[768,768]{1,0:T(8,128)} %copy-done.9, f32[768,768]{1,0:T(8,128)} %get-tuple-element.9, bf16[1,1,768,2048]{3,2,1,0:T(8,128)(2,1)S(1)} %copy-done, f32[768]{0:T(1024)S(1)} %convert_reduce_fusion, bf16[768,2176]{1,0:T(8,128)(2,1)} %bitcast.8), kind=kOutput, calls=%fused_computation.27 | convolution fusion | flops 2428305408 | bytes 13372416 | tf_op jit(solution)/shard_map/dot_general | solution.py:20
  114.6 2.6 %fusion.5 = f32[768,2048]{1,0:T(8,128)S(1)} fusion(bf16[768,768]{1,0:T(8,128)(2,1)S(1)} %get-tuple-element.14, bf16[1,1,2048,768]{3,2,1,0:T(8,128)(2,1)S(1)} %copy-done.4), kind=kOutput, calls=%fused_computation.15 | convolution fusion | flops 2415919104 | bytes 10616832 | tf_op jit(solution)/shard_map/dot_general | solution.py:20
  117.3 4.0 %add_convert_fusion = bf16[768,2048]{1,0:T(8,128)(2,1)} fusion(f32[768,2048]{1,0:T(8,128)S(1)} %fusion.5, bf16[768,768]{1,0:T(8,128)(2,1)S(1)} %get-tuple-element.13, bf16[1,1,2048,768]{3,2,1,0:T(8,128)(2,1)S(1)} %copy-done.6), kind=kOutput, calls=%fused_computation.4 | convolution fusion | flops 2419064832 | bytes 13762560 | tf_op jit(solution)/shard_map/dot_general | solution.py:20
  121.3 5.0 %all-to-all-start.2 = ((bf16[32,24,2048]{2,1,0:T(8,128)(2,1)}), bf16[32,24,2048]{2,1,0:T(8,128)(2,1)}, u32[]{:S(2)}, u32[]{:S(2)}) async-start(bf16[32,24,2048]{2,1,0:T(8,128)(2,1)} %bitcast.85), calls=%async_computation.2 | async-start | bytes 6291456 | tf_op jit(solution)/shard_map/all_to_all | solution.py:28
  126.3 3.7 %fusion.1 = bf16[768]{0:T(1024)(128)(2,1)S(1)} fusion(bf16[768,2048]{1,0:T(8,128)(2,1)} %convolution_convert_fusion.3, bf16[768,2176]{1,0:T(8,128)(2,1)} %bitcast.8), kind=kLoop, calls=%fused_computation.3 | loop fusion | flops 6290688 | bytes 6292992 | tf_op jit(solution)/shard_map/reduce_sum | solution.py:82
  130.8 6.7 %fusion.13 = bf16[1,1,2048,768]{3,2,1,0:T(8,128)(2,1)} fusion(bf16[768,2048]{1,0:T(8,128)(2,1)} %bitcast.4, bf16[768,768]{1,0:T(8,128)(2,1)} %copy-done.12), kind=kOutput, calls=%fused_computation.23 | convolution fusion | flops 2417491968 | bytes 7471104 | tf_op jit(solution)/shard_map/dot_general | solution.py:14
  137.4 6.1 %fusion.14 = bf16[1,1,768,2048]{3,2,1,0:T(8,128)(2,1)} fusion(bf16[768,768]{1,0:T(8,128)(2,1)S(1)} %copy-done.11, f32[768]{0:T(1024)S(1)} %convert_reduce_fusion, bf16[768,2176]{1,0:T(8,128)(2,1)} %bitcast.8), kind=kOutput, calls=%fused_computation.24 | convolution fusion | flops 2422210560 | bytes 7474176 | tf_op jit(solution)/shard_map/dot_general | solution.py:14
  143.5 24.6 %all-to-all-done.2 = bf16[32,24,2048]{2,1,0:T(8,128)(2,1)} async-done(((bf16[32,24,2048]{2,1,0:T(8,128)(2,1)}), bf16[32,24,2048]{2,1,0:T(8,128)(2,1)}, u32[]{:S(2)}, u32[]{:S(2)}) %all-to-all-start.2) | async-done | bytes 3145760 | tf_op jit(solution)/shard_map/all_to_all | solution.py:28
  168.1 4.5 %all-to-all-start.3 = ((bf16[32,1,24]{2,1,0:T(2,128)(2,1)}), bf16[32,1,24]{2,1,0:T(2,128)(2,1)}, u32[]{:S(2)}, u32[]{:S(2)}) async-start(bf16[32,1,24]{2,1,0:T(2,128)(2,1)} %convert_element_type.141), calls=%async_computation.3 | async-start | bytes 32768 | tf_op jit(solution)/shard_map/all_to_all | solution.py:28
  172.7 3.5 %fusion.16 = bf16[96,2048]{1,0:T(8,128)(2,1)} fusion(bf16[768,2048]{1,0:T(8,128)(2,1)} %bitcast.17, bf16[1,192,2048]{2,1,0:T(8,128)(2,1)} %param.8, pred[768,192]{0,1:T(8,128)(4,1)S(1)} %fusion.17), kind=kOutput, calls=%fused_computation.32 | convolution fusion | flops 302579712 | bytes 4005888 | tf_op jit(solution)/shard_map/dot_general | solution.py:14
  176.1 3.3 %fusion.15 = bf16[96,2048]{1,0:T(8,128)(2,1)} fusion(bf16[768,2048]{1,0:T(8,128)(2,1)} %bitcast.17, bf16[1,192,2048]{2,1,0:T(8,128)(2,1)S(1)} %copy-done.1, pred[768,192]{0,1:T(8,128)(4,1)S(1)} %fusion.17), kind=kOutput, calls=%fused_computation.31 | convolution fusion | flops 302579712 | bytes 4005888 | tf_op jit(solution)/shard_map/dot_general | solution.py:14
  182.0 6.2 %fusion.12 = bf16[1,1,2048,768]{3,2,1,0:T(8,128)(2,1)} fusion(bf16[768,2048]{1,0:T(8,128)(2,1)} %bitcast.4, bf16[768,768]{1,0:T(8,128)(2,1)S(1)} %copy-done.8), kind=kOutput, calls=%fused_computation.22 | convolution fusion | flops 2417491968 | bytes 7471104 | tf_op jit(solution)/shard_map/dot_general | solution.py:14
  191.2 2.3 %collective-permute-done = bf16[96,2048]{1,0:T(8,128)(2,1)S(1)} collective-permute-done((bf16[96,2048]{1,0:T(8,128)(2,1)}, bf16[96,2048]{1,0:T(8,128)(2,1)S(1)}, u32[]{:S(2)}, u32[]{:S(2)}) %collective-permute-start) | collective-permute-done | bytes 393248 | tf_op jit(solution)/shard_map/ppermute | solution.py:10
  193.5 7.8 %collective-permute-done.1 = bf16[96,2048]{1,0:T(8,128)(2,1)} collective-permute-done((bf16[96,2048]{1,0:T(8,128)(2,1)}, bf16[96,2048]{1,0:T(8,128)(2,1)}, u32[]{:S(2)}, u32[]{:S(2)}) %collective-permute-start.1) | collective-permute-done | bytes 393248 | tf_op jit(solution)/shard_map/ppermute | solution.py:10
  (51 shorter events, 13.3 us)
Async XLA Ops:
  0.6 74.7 %copy-start = (bf16[1,1,768,2048]{3,2,1,0:T(8,128)(2,1)S(1)}, bf16[1,1,768,2048]{3,2,1,0:T(8,128)(2,1)}, u32[]{:S(2)}) copy-start(bf16[1,1,768,2048]{3,2,1,0:T(8,128)(2,1)} %param.13) | copy-start | bytes 9437188
  4.1 11.7 %copy-start.2 = (s32[192,2]{0,1:T(2,128)}, s32[192,2]{0,1:T(2,128)S(1)}, u32[]{:S(2)}) copy-start(s32[192,2]{0,1:T(2,128)S(1)} %add_bitcast_fusion.1) | copy-start | bytes 4612
  8.1 7.7 %copy-start.3 = (bf16[1,192,2]{1,2,0:T(2,128)(2,1)S(1)}, bf16[1,192,2]{1,2,0:T(2,128)(2,1)}, u32[]{:S(2)}) copy-start(bf16[1,192,2]{1,2,0:T(2,128)(2,1)} %param.10) | copy-start | bytes 2308
  8.1 49.7 %all-to-all-start = ((bf16[32,24,2048]{2,1,0:T(8,128)(2,1)}), bf16[32,24,2048]{2,1,0:T(8,128)(2,1)}, u32[]{:S(2)}, u32[]{:S(2)}) async-start(bf16[32,24,2048]{2,1,0:T(8,128)(2,1)} %bitcast.84), calls=%async_computation | async-start | bytes 6291456 | tf_op jit(solution)/shard_map/all_to_all | solution.py:28
  57.8 49.0 %all-to-all-start.1 = ((bf16[32,24,2176]{2,1,0:T(8,128)(2,1)}), bf16[32,24,2176]{2,1,0:T(8,128)(2,1)}, u32[]{:S(2)}, u32[]{:S(2)}) async-start(bf16[32,24,2176]{2,1,0:T(8,128)(2,1)} %bitcast.83), calls=%async_computation.1 | async-start | bytes 6684672 | tf_op jit(solution)/shard_map/all_to_all | solution.py:28
  62.8 5.6 %copy-start.5 = (bf16[1,1,2048,768]{3,2,1,0:T(8,128)(2,1)S(1)}, bf16[1,1,2048,768]{3,2,1,0:T(8,128)(2,1)}, u32[]{:S(2)}) copy-start(bf16[1,1,2048,768]{3,2,1,0:T(8,128)(2,1)} %param.12) | copy-start | bytes 9437188
  68.4 6.9 %copy-start.9 = (f32[768,768]{1,0:T(8,128)}, f32[768,768]{1,0:T(8,128)S(1)}, u32[]{:S(2)}) copy-start(f32[768,768]{1,0:T(8,128)S(1)} %fusion.7) | copy-start | bytes 7077892
  75.3 4.0 %copy-start.10 = (bf16[768,768]{1,0:T(8,128)(2,1)}, bf16[768,768]{1,0:T(8,128)(2,1)S(1)}, u32[]{:S(2)}) copy-start(bf16[768,768]{1,0:T(8,128)(2,1)S(1)} %get-tuple-element.11) | copy-start | bytes 3538948
  107.9 6.7 %copy-start.4 = (bf16[1,1,2048,768]{3,2,1,0:T(8,128)(2,1)S(1)}, bf16[1,1,2048,768]{3,2,1,0:T(8,128)(2,1)}, u32[]{:S(2)}) copy-start(bf16[1,1,2048,768]{3,2,1,0:T(8,128)(2,1)} %param.11) | copy-start | bytes 9437188
  114.5 2.7 %copy-start.7 = (bf16[768,768]{1,0:T(8,128)(2,1)}, bf16[768,768]{1,0:T(8,128)(2,1)S(1)}, u32[]{:S(2)}) copy-start(bf16[768,768]{1,0:T(8,128)(2,1)S(1)} %get-tuple-element.14) | copy-start | bytes 3538948
  114.5 2.7 %copy-start.12 = (bf16[768,768]{1,0:T(8,128)(2,1)}, bf16[768,768]{1,0:T(8,128)(2,1)S(1)}, u32[]{:S(2)}) copy-start(bf16[768,768]{1,0:T(8,128)(2,1)S(1)} %get-tuple-element.13) | copy-start | bytes 3538948
  114.6 2.7 %copy-start.6 = (bf16[1,1,2048,768]{3,2,1,0:T(8,128)(2,1)S(1)}, bf16[1,1,2048,768]{3,2,1,0:T(8,128)(2,1)}, u32[]{:S(2)}) copy-start(bf16[1,1,2048,768]{3,2,1,0:T(8,128)(2,1)} %param.12) | copy-start | bytes 9437188
  121.3 46.8 %all-to-all-start.2 = ((bf16[32,24,2048]{2,1,0:T(8,128)(2,1)}), bf16[32,24,2048]{2,1,0:T(8,128)(2,1)}, u32[]{:S(2)}, u32[]{:S(2)}) async-start(bf16[32,24,2048]{2,1,0:T(8,128)(2,1)} %bitcast.85), calls=%async_computation.2 | async-start | bytes 6291456 | tf_op jit(solution)/shard_map/all_to_all | solution.py:28
  130.8 6.7 %copy-start.11 = (bf16[768,768]{1,0:T(8,128)(2,1)S(1)}, bf16[768,768]{1,0:T(8,128)(2,1)}, u32[]{:S(2)}) copy-start(bf16[768,768]{1,0:T(8,128)(2,1)} %copy-done.10) | copy-start | bytes 3538948
  168.1 20.2 %all-to-all-start.3 = ((bf16[32,1,24]{2,1,0:T(2,128)(2,1)}), bf16[32,1,24]{2,1,0:T(2,128)(2,1)}, u32[]{:S(2)}, u32[]{:S(2)}) async-start(bf16[32,1,24]{2,1,0:T(2,128)(2,1)} %convert_element_type.141), calls=%async_computation.3 | async-start | bytes 32768 | tf_op jit(solution)/shard_map/all_to_all | solution.py:28
  172.7 3.5 %copy-start.1 = (bf16[1,192,2048]{2,1,0:T(8,128)(2,1)S(1)}, bf16[1,192,2048]{2,1,0:T(8,128)(2,1)}, u32[]{:S(2)}) copy-start(bf16[1,192,2048]{2,1,0:T(8,128)(2,1)} %param.8) | copy-start | bytes 2359300
  172.7 9.3 %copy-start.8 = (bf16[768,768]{1,0:T(8,128)(2,1)S(1)}, bf16[768,768]{1,0:T(8,128)(2,1)}, u32[]{:S(2)}) copy-start(bf16[768,768]{1,0:T(8,128)(2,1)} %copy-done.7) | copy-start | bytes 3538948
  179.4 14.1 %collective-permute-start = (bf16[96,2048]{1,0:T(8,128)(2,1)}, bf16[96,2048]{1,0:T(8,128)(2,1)S(1)}, u32[]{:S(2)}, u32[]{:S(2)}) collective-permute-start(bf16[96,2048]{1,0:T(8,128)(2,1)} %fusion.15), channel_id=1, source_target_pairs={{32,0},{64,32},{96,64},{33,1},{65,33},{97,65},{34,2},{66,34},{98,6... | collective-permute-start | bytes 1179656 | tf_op jit(solution)/shard_map/ppermute | solution.py:10
  180.7 20.6 %collective-permute-start.1 = (bf16[96,2048]{1,0:T(8,128)(2,1)}, bf16[96,2048]{1,0:T(8,128)(2,1)}, u32[]{:S(2)}, u32[]{:S(2)}) collective-permute-start(bf16[96,2048]{1,0:T(8,128)(2,1)} %fusion.16), channel_id=1, source_target_pairs={{32,0},{64,32},{96,64},{33,1},{65,33},{97,65},{34,2},{66,34},{98,6... | collective-permute-start | bytes 1179656 | tf_op jit(solution)/shard_map/ppermute | solution.py:10

commit v7 on v5

--- a/solution.py
+++ b/solution.py
@@ -34,7 +34,7 @@
     return jnp.where(lanes == 0, values[:, None], jnp.zeros((), values.dtype))
 
 
-def per_device(hidden_in, out_grad, routes, mixing, w_gate, w_up, w_down):
+def device_body(hidden_in, out_grad, routes, mixing, w_gate, w_up, w_down):
     tokens_in = hidden_in[0]
     grads_in = out_grad[0]
     groups = lax.axis_size("expert")
@@ -90,9 +90,9 @@
         jnp.bfloat16
     )
     up_pre = (act_grad * silu_g).astype(jnp.bfloat16)
-    in_grad = (contract_cols(gate_pre, gate_mat) + contract_cols(up_pre, up_mat)).astype(
-        jnp.bfloat16
-    )
+    in_grad = contract_cols(
+        jnp.concatenate([gate_pre, up_pre], axis=1), jnp.concatenate([gate_mat, up_mat], axis=1)
+    ).astype(jnp.bfloat16)
 
     back_grad = exchange(in_grad, groups)
     back_prob = exchange(prob_part, groups)
@@ -128,7 +128,7 @@
         P("section", "expert", None, None),
     )
     return jax.shard_map(
-        per_device,
+        device_body,
         mesh=mesh,
         in_specs=placed,
         out_specs=(

time: 201 us -> 201 us (level)
  waiting for transfers between devices: 103 us -> 85.5 us
  local copies, waits for them, and re-layouts: 4.65 us -> 17.8 us
  other arithmetic: 10 us -> 13 us
    all_to_all x4, waiting for transfers between devices: 89.5 us -> 72.3 us  [exchange(): lax.all_to_all(parted, 'expert', split_axis=0, concat_axis=0, tiled=True)]
    optimization_barrier x0 -> x2, local copies, waits for them, and re-layouts: none -> 6.08 us  [device_body(): lax.optimization_barrier((pre_gate, pre_up, act_rows, expert_out))]
    dot_general x0 -> x2, local copies, waits for them, and re-layouts: none -> 6.08 us  [the longest x1 3.04 us: device_body(): pre_up = jnp.dot(rows_in, up_mat, preferred_element_type=jnp.float32)]
    convert_element_type x2 -> x3, other arithmetic: 0.06 us -> 3.09 us  [the longest x1 3.03 us: device_body(): act_rows = (silu_g * pre_up).astype(jnp.bfloat16)]
    unnamed x24 -> x20, local copies, waits for them, and re-layouts: 3.15 us -> 4.13 us
    dot_general x3 -> x2, matrix products: 13.3 us -> 13.4 us  [contract_cols(): lax.dot_general(left, right, (((1,), (1,)), ((), ())), preferred_element_...]
  transfers between devices with their start and end apart: 5 -> 5, of which waited for: 4 -> 4; matrix products, arithmetic and copies ran while one was open for 25% -> 33% of each run, Pallas kernels for 0% -> 0%
where the time goes in v7:
time: 201 us; the launch traced here: 200 us
  waiting for transfers between devices  85.5 us (43%)
  matrix products  59.8 us (30%)
  starting transfers between devices  22.9 us (11%)
  local copies, waits for them, and re-layouts  17.8 us (9%)
  other arithmetic  13 us (6%)
    all_to_all x4, waiting for transfers between devices, exchange(): lax.all_to_all(parted, 'expert', split_axis=0, concat_axis=0, tiled=True)  72.3 us
    dot_general x4, matrix products, contract_rows(): lax.dot_general(left, right, (((0,), (0,)), ((), ())), preferred_element_...  22.8 us
    all_to_all x4, starting transfers between devices, exchange(): lax.all_to_all(parted, 'expert', split_axis=0, concat_axis=0, tiled=True)  21.3 us
    dot_general x2, matrix products, contract_cols(): lax.dot_general(left, right, (((1,), (1,)), ((), ())), preferred_element_...  13.4 us
    ppermute x1, waiting for transfers between devices, shifted(): return lax.ppermute(block, axis, route)  13.2 us
    dot_general x1, matrix products, device_body(): pre_gate = jnp.dot(rows_in, gate_mat, preferred_element_type=jnp.float32)  6.85 us
    dot_general x1, matrix products, device_body(): pre_up = jnp.dot(rows_in, up_mat, preferred_element_type=jnp.float32)  6.84 us
    optimization_barrier x2, local copies, waits for them, and re-layouts, device_body(): lax.optimization_barrier((pre_gate, pre_up, act_rows, expert_out))  6.08 us
  transfers between devices with their start and end apart: 5, of which 4 were waited for; matrix products, arithmetic and copies ran while one was open for 33% of the time, Pallas kernels for 0%

profile of v7, /device:TPU:0, one launch (start us, length us, event | category | flops | bytes accessed | tf_op | source)
XLA Modules:
  0.0 200.0 jit_solution(6174079215093132739)
XLA Ops:
  4.2 3.8 %convolution_convert_fusion.5 = bf16[768,2048]{1,0:T(8,128)(2,1)} fusion(pred[768,192]{0,1:T(8,128)(4,1)S(1)} %fusion.19, bf16[1,192,2048]{2,1,0:T(8,128)(2,1)} %param.7), kind=kOutput, calls=%fused_computation.13 | convolution fusion | flops 605552640 | bytes 4079616 | tf_op jit(solution)/shard_map/dot_general | solution.py:57
  8.1 7.7 %all-to-all-start = ((bf16[32,24,2048]{2,1,0:T(8,128)(2,1)}), bf16[32,24,2048]{2,1,0:T(8,128)(2,1)}, u32[]{:S(2)}, u32[]{:S(2)}) async-start(bf16[32,24,2048]{2,1,0:T(8,128)(2,1)} %bitcast.70), calls=%async_computation | async-start | bytes 6291456 | tf_op jit(solution)/shard_map/all_to_all | solution.py:28
  20.4 37.4 %all-to-all-done = bf16[32,24,2048]{2,1,0:T(8,128)(2,1)} async-done(((bf16[32,24,2048]{2,1,0:T(8,128)(2,1)}), bf16[32,24,2048]{2,1,0:T(8,128)(2,1)}, u32[]{:S(2)}, u32[]{:S(2)}) %all-to-all-start) | async-done | bytes 3145760 | tf_op jit(solution)/shard_map/all_to_all | solution.py:28
  57.8 5.0 %all-to-all-start.1 = ((bf16[32,24,2176]{2,1,0:T(8,128)(2,1)}), bf16[32,24,2176]{2,1,0:T(8,128)(2,1)}, u32[]{:S(2)}, u32[]{:S(2)}) async-start(bf16[32,24,2176]{2,1,0:T(8,128)(2,1)} %bitcast.69), calls=%async_computation.1 | async-start | bytes 6684672 | tf_op jit(solution)/shard_map/all_to_all | solution.py:28
  62.8 6.8 %fusion.30 = f32[768,768]{1,0:T(8,128)} fusion(bf16[768,2048]{1,0:T(8,128)(2,1)} %bitcast.4, bf16[1,1,2048,768]{3,2,1,0:T(8,128)(2,1)} %param.11), kind=kOutput, calls=%fused_computation.55 | convolution fusion | flops 2415919104 | bytes 8650752 | tf_op jit(solution)/shard_map/dot_general | solution.py:69
  69.6 3.0 %copy.67 = f32[768,768]{0,1:T(8,128)} copy(f32[768,768]{1,0:T(8,128)} %fusion.30) | data formatting | bytes 4718592 | tf_op jit(solution)/shard_map/dot_general | solution.py:69
  72.7 6.8 %fusion.28 = f32[768,768]{1,0:T(8,128)} fusion(bf16[768,2048]{1,0:T(8,128)(2,1)} %bitcast.4, bf16[1,1,2048,768]{3,2,1,0:T(8,128)(2,1)} %param.12), kind=kOutput, calls=%fused_computation.53 | convolution fusion | flops 2415919104 | bytes 8650752 | tf_op jit(solution)/shard_map/dot_general | solution.py:70
  79.5 3.0 %copy.68 = f32[768,768]{0,1:T(8,128)} copy(f32[768,768]{1,0:T(8,128)} %fusion.28) | data formatting | bytes 4718592 | tf_op jit(solution)/shard_map/dot_general | solution.py:70
  82.5 3.0 %multiply_convert_fusion.2 = bf16[768,768]{0,1:T(8,128)(2,1)S(1)} fusion(f32[768,768]{0,1:T(8,128)} %copy.68, f32[768,768]{0,1:T(8,128)} %copy.67), kind=kLoop, calls=%fused_computation.30 | loop fusion | flops 3538944 | bytes 5898240 | tf_op jit(solution)/shard_map/convert_element_type | solution.py:73
  86.7 4.0 %convolution_convert_fusion.3 = bf16[768,2048]{1,0:T(8,128)(2,1)} fusion(bf16[768,768]{0,1:T(8,128)(2,1)S(1)} %multiply_convert_fusion.2, bf16[1,1,768,2048]{3,2,1,0:T(8,128)(2,1)S(1)} %copy-done), kind=kOutput, calls=%fused_computation.11 | convolution fusion | flops 2417491968 | bytes 7471104 | tf_op jit(solution)/shard_map/dot_general | solution.py:74
  90.7 3.0 %copy.69 = f32[768,768]{0,1:T(8,128)} copy(f32[768,768]{1,0:T(8,128)} %fusion.28) | data formatting | bytes 4718592 | tf_op jit(solution)/shard_map/optimization_barrier | solution.py:77
  93.7 3.0 %copy.70 = f32[768,768]{0,1:T(8,128)} copy(f32[768,768]{1,0:T(8,128)} %fusion.30) | data formatting | bytes 4718592 | tf_op jit(solution)/shard_map/optimization_barrier | solution.py:77
  96.7 10.1 %all-to-all-done.1 = bf16[32,24,2176]{2,1,0:T(8,128)(2,1)} async-done(((bf16[32,24,2176]{2,1,0:T(8,128)(2,1)}), bf16[32,24,2176]{2,1,0:T(8,128)(2,1)}, u32[]{:S(2)}, u32[]{:S(2)}) %all-to-all-start.1) | async-done | bytes 3342368 | tf_op jit(solution)/shard_map/all_to_all | solution.py:28
  107.9 6.7 %multiply_convert_fusion = (bf16[768,768]{0,1:T(8,128)(2,1)S(1)}, bf16[768,768]{0,1:T(8,128)(2,1)S(1)}) fusion(f32[768,768]{0,1:T(8,128)} %copy.70, f32[768,768]{0,1:T(8,128)} %copy.69, bf16[1,1,768,2048]{3,2,1,0:T(8,128)(2,1)S(1)} %copy-done, f32[768]{0:T(1024)S(1)} %convert_reduce_fusion, bf16[768,2176]{1,0:T(8,128)(2,1)} %bitcast.8), kind=kOutput, calls=%fused_computation.27 | convolution fusion | flops 2428305408 | bytes 13372416 | tf_op jit(solution)/shard_map/dot_general | solution.py:20
  114.6 6.7 %fusion.6 = bf16[768,2048]{1,0:T(8,128)(2,1)} fusion(bf16[2048,768]{1,0:T(8,128)(2,1)S(1)} %bitcast.75, bf16[2048,768]{1,0:T(8,128)(2,1)S(1)} %bitcast.74, bf16[768,768]{0,1:T(8,128)(2,1)S(1)} %get-tuple-element.13, bf16[768,768]{0,1:T(8,128)(2,1)S(1)} %get-tuple-element.14), kind=kOutput, calls=%fused_computation.14 | convolution fusion | flops 4850712576 | bytes 11796480 | tf_op jit(solution)/shard_map/dot_general | solution.py:20
  121.3 4.8 %all-to-all-start.2 = ((bf16[32,24,2048]{2,1,0:T(8,128)(2,1)}), bf16[32,24,2048]{2,1,0:T(8,128)(2,1)}, u32[]{:S(2)}, u32[]{:S(2)}) async-start(bf16[32,24,2048]{2,1,0:T(8,128)(2,1)} %bitcast.71), calls=%async_computation.2 | async-start | bytes 6291456 | tf_op jit(solution)/shard_map/all_to_all | solution.py:28
  126.2 3.7 %fusion.1 = bf16[768]{0:T(1024)(128)(2,1)S(1)} fusion(bf16[768,2048]{1,0:T(8,128)(2,1)} %convolution_convert_fusion.3, bf16[768,2176]{1,0:T(8,128)(2,1)} %bitcast.8), kind=kLoop, calls=%fused_computation.3 | loop fusion | flops 6290688 | bytes 6292992 | tf_op jit(solution)/shard_map/reduce_sum | solution.py:82
  130.6 6.7 %fusion.12 = bf16[1,1,2048,768]{3,2,1,0:T(8,128)(2,1)} fusion(bf16[768,2048]{1,0:T(8,128)(2,1)} %bitcast.4, bf16[768,768]{0,1:T(8,128)(2,1)} %copy-done.8), kind=kOutput, calls=%fused_computation.19 | convolution fusion | flops 2417491968 | bytes 7471104 | tf_op jit(solution)/shard_map/dot_general | solution.py:14
  137.3 6.0 %fusion.14 = bf16[1,1,768,2048]{3,2,1,0:T(8,128)(2,1)} fusion(bf16[768,768]{0,1:T(8,128)(2,1)S(1)} %copy-done.2, f32[768]{0:T(1024)S(1)} %convert_reduce_fusion, bf16[768,2176]{1,0:T(8,128)(2,1)} %bitcast.8), kind=kOutput, calls=%fused_computation.21 | convolution fusion | flops 2422210560 | bytes 7474176 | tf_op jit(solution)/shard_map/dot_general | solution.py:14
  143.3 24.9 %all-to-all-done.2 = bf16[32,24,2048]{2,1,0:T(8,128)(2,1)} async-done(((bf16[32,24,2048]{2,1,0:T(8,128)(2,1)}), bf16[32,24,2048]{2,1,0:T(8,128)(2,1)}, u32[]{:S(2)}, u32[]{:S(2)}) %all-to-all-start.2) | async-done | bytes 3145760 | tf_op jit(solution)/shard_map/all_to_all | solution.py:28
  168.2 3.8 %all-to-all-start.3 = ((bf16[32,1,24]{2,1,0:T(2,128)(2,1)}), bf16[32,1,24]{2,1,0:T(2,128)(2,1)S(1)}, u32[]{:S(2)}, u32[]{:S(2)}) async-start(bf16[32,1,24]{2,1,0:T(2,128)(2,1)} %convert_element_type.123), calls=%async_computation.3 | async-start | bytes 32768 | tf_op jit(solution)/shard_map/all_to_all | solution.py:28
  172.0 3.8 %fusion.15 = bf16[192,2048]{1,0:T(8,128)(2,1)} fusion(pred[768,192]{0,1:T(8,128)(4,1)S(1)} %fusion.19, bf16[768,2048]{1,0:T(8,128)(2,1)} %bitcast.16, bf16[1,192,2048]{2,1,0:T(8,128)(2,1)} %param.8), kind=kOutput, calls=%fused_computation.23 | convolution fusion | flops 605159424 | bytes 4866048 | tf_op jit(solution)/shard_map/dot_general | solution.py:14
  177.4 6.2 %fusion.13 = bf16[1,1,2048,768]{3,2,1,0:T(8,128)(2,1)} fusion(bf16[768,2048]{1,0:T(8,128)(2,1)} %bitcast.4, bf16[768,768]{0,1:T(8,128)(2,1)S(1)} %copy-done.7), kind=kOutput, calls=%fused_computation.20 | convolution fusion | flops 2417491968 | bytes 7471104 | tf_op jit(solution)/shard_map/dot_general | solution.py:14
  184.7 13.2 %collective-permute-done = bf16[192,2048]{1,0:T(8,128)(2,1)} collective-permute-done((bf16[192,2048]{1,0:T(8,128)(2,1)}, bf16[192,2048]{1,0:T(8,128)(2,1)}, u32[]{:S(2)}, u32[]{:S(2)}) %collective-permute-start) | collective-permute-done | bytes 786464 | tf_op jit(solution)/shard_map/ppermute | solution.py:10
  (44 shorter events, 15.6 us)
Async XLA Ops:
  0.6 86.0 %copy-start = (bf16[1,1,768,2048]{3,2,1,0:T(8,128)(2,1)S(1)}, bf16[1,1,768,2048]{3,2,1,0:T(8,128)(2,1)}, u32[]{:S(2)}) copy-start(bf16[1,1,768,2048]{3,2,1,0:T(8,128)(2,1)} %param.13) | copy-start | bytes 9437188
  8.1 7.7 %copy-start.3 = (bf16[1,192,2]{1,2,0:T(2,128)(2,1)S(1)}, bf16[1,192,2]{1,2,0:T(2,128)(2,1)}, u32[]{:S(2)}) copy-start(bf16[1,192,2]{1,2,0:T(2,128)(2,1)} %param.10) | copy-start | bytes 2308
  8.1 49.7 %all-to-all-start = ((bf16[32,24,2048]{2,1,0:T(8,128)(2,1)}), bf16[32,24,2048]{2,1,0:T(8,128)(2,1)}, u32[]{:S(2)}, u32[]{:S(2)}) async-start(bf16[32,24,2048]{2,1,0:T(8,128)(2,1)} %bitcast.70), calls=%async_computation | async-start | bytes 6291456 | tf_op jit(solution)/shard_map/all_to_all | solution.py:28
  57.8 49.0 %all-to-all-start.1 = ((bf16[32,24,2176]{2,1,0:T(8,128)(2,1)}), bf16[32,24,2176]{2,1,0:T(8,128)(2,1)}, u32[]{:S(2)}, u32[]{:S(2)}) async-start(bf16[32,24,2176]{2,1,0:T(8,128)(2,1)} %bitcast.69), calls=%async_computation.1 | async-start | bytes 6684672 | tf_op jit(solution)/shard_map/all_to_all | solution.py:28
  85.6 1.1 copy-start.1
  107.9 6.7 %copy-start.4 = (bf16[1,1,2048,768]{3,2,1,0:T(8,128)(2,1)S(1)}, bf16[1,1,2048,768]{3,2,1,0:T(8,128)(2,1)}, u32[]{:S(2)}) copy-start(bf16[1,1,2048,768]{3,2,1,0:T(8,128)(2,1)} %param.11) | copy-start | bytes 9437188
  107.9 6.7 %copy-start.5 = (bf16[1,1,2048,768]{3,2,1,0:T(8,128)(2,1)S(1)}, bf16[1,1,2048,768]{3,2,1,0:T(8,128)(2,1)}, u32[]{:S(2)}) copy-start(bf16[1,1,2048,768]{3,2,1,0:T(8,128)(2,1)} %param.12) | copy-start | bytes 9437188
  114.6 6.7 %copy-start.6 = (bf16[768,768]{0,1:T(8,128)(2,1)}, bf16[768,768]{0,1:T(8,128)(2,1)S(1)}, u32[]{:S(2)}) copy-start(bf16[768,768]{0,1:T(8,128)(2,1)S(1)} %get-tuple-element.13) | copy-start | bytes 3538948
  114.6 6.7 %copy-start.8 = (bf16[768,768]{0,1:T(8,128)(2,1)}, bf16[768,768]{0,1:T(8,128)(2,1)S(1)}, u32[]{:S(2)}) copy-start(bf16[768,768]{0,1:T(8,128)(2,1)S(1)} %get-tuple-element.14) | copy-start | bytes 3538948
  121.3 46.8 %all-to-all-start.2 = ((bf16[32,24,2048]{2,1,0:T(8,128)(2,1)}), bf16[32,24,2048]{2,1,0:T(8,128)(2,1)}, u32[]{:S(2)}, u32[]{:S(2)}) async-start(bf16[32,24,2048]{2,1,0:T(8,128)(2,1)} %bitcast.71), calls=%async_computation.2 | async-start | bytes 6291456 | tf_op jit(solution)/shard_map/all_to_all | solution.py:28
  130.6 6.7 %copy-start.2 = (bf16[768,768]{0,1:T(8,128)(2,1)S(1)}, bf16[768,768]{0,1:T(8,128)(2,1)}, u32[]{:S(2)}) copy-start(bf16[768,768]{0,1:T(8,128)(2,1)} %copy-done.1) | copy-start | bytes 3538948
  168.2 15.5 %all-to-all-start.3 = ((bf16[32,1,24]{2,1,0:T(2,128)(2,1)}), bf16[32,1,24]{2,1,0:T(2,128)(2,1)S(1)}, u32[]{:S(2)}, u32[]{:S(2)}) async-start(bf16[32,1,24]{2,1,0:T(2,128)(2,1)} %convert_element_type.123), calls=%async_computation.3 | async-start | bytes 32768 | tf_op jit(solution)/shard_map/all_to_all | solution.py:28
  172.0 5.4 %copy-start.7 = (bf16[768,768]{0,1:T(8,128)(2,1)S(1)}, bf16[768,768]{0,1:T(8,128)(2,1)}, u32[]{:S(2)}) copy-start(bf16[768,768]{0,1:T(8,128)(2,1)} %copy-done.6) | copy-start | bytes 3538948
  175.9 22.0 %collective-permute-start = (bf16[192,2048]{1,0:T(8,128)(2,1)}, bf16[192,2048]{1,0:T(8,128)(2,1)}, u32[]{:S(2)}, u32[]{:S(2)}) collective-permute-start(bf16[192,2048]{1,0:T(8,128)(2,1)} %fusion.15), channel_id=1, source_target_pairs={{32,0},{64,32},{96,64},{33,1},{65,33},{97,65},{34,2},{66,34},{98,6... | collective-permute-start | bytes 2359304 | tf_op jit(solution)/shard_map/ppermute | solution.py:10

commit v8 on v5

--- a/solution.py
+++ b/solution.py
@@ -34,7 +34,7 @@
     return jnp.where(lanes == 0, values[:, None], jnp.zeros((), values.dtype))
 
 
-def per_device(hidden_in, out_grad, routes, mixing, w_gate, w_up, w_down):
+def device_body(hidden_in, out_grad, routes, mixing, w_gate, w_up, w_down):
     tokens_in = hidden_in[0]
     grads_in = out_grad[0]
     groups = lax.axis_size("expert")
@@ -74,10 +74,9 @@
     expert_out = jnp.dot(act_rows, down_mat, preferred_element_type=jnp.float32).astype(
         jnp.bfloat16
     )
-    pre_gate, pre_up, act_rows, expert_out = lax.optimization_barrier(
-        (pre_gate, pre_up, act_rows, expert_out)
+    pre_gate, pre_up, sigmoid_g, act_rows, expert_out = lax.optimization_barrier(
+        (pre_gate, pre_up, sigmoid_g, act_rows, expert_out)
     )
-    sigmoid_g = jax.nn.sigmoid(pre_gate)
     silu_g = pre_gate * sigmoid_g
     prob_part = jnp.sum(
         grad_rows.astype(jnp.float32) * expert_out.astype(jnp.float32), axis=1
@@ -128,7 +127,7 @@
         P("section", "expert", None, None),
     )
     return jax.shard_map(
-        per_device,
+        device_body,
         mesh=mesh,
         in_specs=placed,
         out_specs=(

time: 201 us -> 202 us (level)
  no operation moved by 1% of the time
where the time goes in v8:
time: 202 us; the launch traced here: 201 us
  waiting for transfers between devices  102 us (50%)
  matrix products  60.5 us (30%)
  starting transfers between devices  22.8 us (11%)
  other arithmetic  10 us (5%)
  local copies, waits for them, and re-layouts  4.58 us (2%)
    all_to_all x4, waiting for transfers between devices, exchange(): lax.all_to_all(parted, 'expert', split_axis=0, concat_axis=0, tiled=True)  88.9 us
    dot_general x4, matrix products, contract_rows(): lax.dot_general(left, right, (((0,), (0,)), ((), ())), preferred_element_...  22.8 us
    all_to_all x4, starting transfers between devices, exchange(): lax.all_to_all(parted, 'expert', split_axis=0, concat_axis=0, tiled=True)  21.6 us
    dot_general x3, matrix products, contract_cols(): lax.dot_general(left, right, (((1,), (1,)), ((), ())), preferred_element_...  14.6 us
    ppermute x1, waiting for transfers between devices, shifted(): return lax.ppermute(block, axis, route)  13.4 us
    dot_general x1, matrix products, device_body(): pre_up = jnp.dot(rows_in, up_mat, preferred_element_type=jnp.float32)  7.68 us
    dot_general x1, matrix products, device_body(): pre_gate = jnp.dot(rows_in, gate_mat, preferred_element_type=jnp.float32)  5.44 us
  transfers between devices with their start and end apart: 5, of which 4 were waited for; matrix products, arithmetic and copies ran while one was open for 25% of the time, Pallas kernels for 0%

profile of v8, /device:TPU:0, one launch (start us, length us, event | category | flops | bytes accessed | tf_op | source)
XLA Modules:
  0.0 201.1 jit_solution(13429604510320990385)
XLA Ops:
  4.2 3.8 %convolution_convert_fusion.5 = bf16[768,2048]{1,0:T(8,128)(2,1)} fusion(pred[768,192]{0,1:T(8,128)(4,1)S(1)} %fusion.16, bf16[1,192,2048]{2,1,0:T(8,128)(2,1)} %param.7), kind=kOutput, calls=%fused_computation.10 | convolution fusion | flops 605552640 | bytes 4079616 | tf_op jit(solution)/shard_map/dot_general | solution.py:57
  8.1 7.7 %all-to-all-start = ((bf16[32,24,2048]{2,1,0:T(8,128)(2,1)}), bf16[32,24,2048]{2,1,0:T(8,128)(2,1)}, u32[]{:S(2)}, u32[]{:S(2)}) async-start(bf16[32,24,2048]{2,1,0:T(8,128)(2,1)} %bitcast.78), calls=%async_computation | async-start | bytes 6291456 | tf_op jit(solution)/shard_map/all_to_all | solution.py:28
  16.2 2.2 %convolution_convert_fusion.4 = bf16[768,2048]{1,0:T(8,128)(2,1)S(1)} fusion(pred[768,192]{0,1:T(8,128)(4,1)S(1)} %fusion.16, bf16[1,192,2048]{2,1,0:T(8,128)(2,1)} %param.8), kind=kOutput, calls=%fused_computation.9 | convolution fusion | flops 605552640 | bytes 4079616 | tf_op jit(solution)/shard_map/dot_general | solution.py:58
  18.3 2.0 %pad_maximum_fusion = bf16[768,2176]{1,0:T(8,128)(2,1)} fusion(bf16[768,128]{1,0:T(8,128)(2,1)S(1)} %broadcast_select_fusion, bf16[768,2048]{1,0:T(8,128)(2,1)S(1)} %convolution_convert_fusion.4), kind=kLoop, calls=%fused_computation.11 | loop fusion | flops 6684672 | bytes 6684672 | tf_op jit(solution)/shard_map/concatenate | solution.py:62
  20.4 37.4 %all-to-all-done = bf16[32,24,2048]{2,1,0:T(8,128)(2,1)} async-done(((bf16[32,24,2048]{2,1,0:T(8,128)(2,1)}), bf16[32,24,2048]{2,1,0:T(8,128)(2,1)}, u32[]{:S(2)}, u32[]{:S(2)}) %all-to-all-start) | async-done | bytes 3145760 | tf_op jit(solution)/shard_map/all_to_all | solution.py:28
  57.8 5.0 %all-to-all-start.1 = ((bf16[32,24,2176]{2,1,0:T(8,128)(2,1)}), bf16[32,24,2176]{2,1,0:T(8,128)(2,1)}, u32[]{:S(2)}, u32[]{:S(2)}) async-start(bf16[32,24,2176]{2,1,0:T(8,128)(2,1)} %bitcast.77), calls=%async_computation.1 | async-start | bytes 6684672 | tf_op jit(solution)/shard_map/all_to_all | solution.py:28
  62.8 5.4 %fusion.7 = f32[768,768]{1,0:T(8,128)S(1)} fusion(bf16[768,2048]{1,0:T(8,128)(2,1)} %bitcast.4, bf16[1,1,2048,768]{3,2,1,0:T(8,128)(2,1)} %param.11), kind=kOutput, calls=%fused_computation.17 | convolution fusion | flops 2415919104 | bytes 8650752 | tf_op jit(solution)/shard_map/dot_general | solution.py:69
  68.3 7.7 %multiply_convert_fusion.2 = (bf16[768,768]{1,0:T(8,128)(2,1)S(1)}, f32[768,768]{1,0:T(8,128)}, f32[768,768]{1,0:T(8,128)}) fusion(f32[768,768]{1,0:T(8,128)S(1)} %fusion.7, bf16[768,2048]{1,0:T(8,128)(2,1)} %bitcast.4, bf16[1,1,2048,768]{3,2,1,0:T(8,128)(2,1)S(1)} %copy-done), kind=kOutput, calls=%fused_computation.29 | convolution fusion | flops 2419458048 | bytes 14548992 | tf_op jit(solution)/shard_map/dot_general | solution.py:70
  75.9 4.0 %convolution_convert_fusion.3 = bf16[768,2048]{1,0:T(8,128)(2,1)} fusion(bf16[768,768]{1,0:T(8,128)(2,1)S(1)} %get-tuple-element.13, bf16[1,1,768,2048]{3,2,1,0:T(8,128)(2,1)S(1)} %copy-done.2), kind=kOutput, calls=%fused_computation.8 | convolution fusion | flops 2417491968 | bytes 7471104 | tf_op jit(solution)/shard_map/dot_general | solution.py:74
  79.9 26.9 %all-to-all-done.1 = bf16[32,24,2176]{2,1,0:T(8,128)(2,1)} async-done(((bf16[32,24,2176]{2,1,0:T(8,128)(2,1)}), bf16[32,24,2176]{2,1,0:T(8,128)(2,1)}, u32[]{:S(2)}, u32[]{:S(2)}) %all-to-all-start.1) | async-done | bytes 3342368 | tf_op jit(solution)/shard_map/all_to_all | solution.py:28
  107.9 7.9 %multiply_convert_fusion = (bf16[768,768]{1,0:T(8,128)(2,1)S(1)}, bf16[768,768]{1,0:T(8,128)(2,1)S(1)}) fusion(f32[768,768]{1,0:T(8,128)} %copy-done.4, f32[768,768]{1,0:T(8,128)} %get-tuple-element.11, f32[768,768]{1,0:T(8,128)} %get-tuple-element.10, bf16[1,1,768,2048]{3,2,1,0:T(8,128)(2,1)} %param.13, f32[768]{0:T(1024)S(1)} %convert_reduce_fusion, ...), kind=kOutput, calls=%fused_computation.27 | convolution fusion | flops 2426535936 | bytes 15731712 | tf_op jit(solution)/shard_map/dot_general | solution.py:20
  115.8 2.6 %fusion.5 = f32[768,2048]{1,0:T(8,128)S(1)} fusion(bf16[768,768]{1,0:T(8,128)(2,1)S(1)} %get-tuple-element.16, bf16[1,1,2048,768]{3,2,1,0:T(8,128)(2,1)S(1)} %copy-done.3), kind=kOutput, calls=%fused_computation.15 | convolution fusion | flops 2415919104 | bytes 10616832 | tf_op jit(solution)/shard_map/dot_general | solution.py:20
  118.5 4.0 %add_convert_fusion = bf16[768,2048]{1,0:T(8,128)(2,1)} fusion(f32[768,2048]{1,0:T(8,128)S(1)} %fusion.5, bf16[768,768]{1,0:T(8,128)(2,1)S(1)} %get-tuple-element.15, bf16[1,1,2048,768]{3,2,1,0:T(8,128)(2,1)S(1)} %copy-done), kind=kOutput, calls=%fused_computation.4 | convolution fusion | flops 2419064832 | bytes 13762560 | tf_op jit(solution)/shard_map/dot_general | solution.py:20
  122.5 5.0 %all-to-all-start.2 = ((bf16[32,24,2048]{2,1,0:T(8,128)(2,1)}), bf16[32,24,2048]{2,1,0:T(8,128)(2,1)}, u32[]{:S(2)}, u32[]{:S(2)}) async-start(bf16[32,24,2048]{2,1,0:T(8,128)(2,1)} %bitcast.79), calls=%async_computation.2 | async-start | bytes 6291456 | tf_op jit(solution)/shard_map/all_to_all | solution.py:28
  127.6 3.7 %fusion.1 = bf16[768]{0:T(1024)(128)(2,1)S(1)} fusion(bf16[768,2048]{1,0:T(8,128)(2,1)} %convolution_convert_fusion.3, bf16[768,2176]{1,0:T(8,128)(2,1)} %bitcast.8), kind=kLoop, calls=%fused_computation.3 | loop fusion | flops 6290688 | bytes 6292992 | tf_op jit(solution)/shard_map/reduce_sum | solution.py:81
  132.0 6.7 %fusion.13 = bf16[1,1,2048,768]{3,2,1,0:T(8,128)(2,1)} fusion(bf16[768,2048]{1,0:T(8,128)(2,1)} %bitcast.4, bf16[768,768]{1,0:T(8,128)(2,1)} %copy-done.7), kind=kOutput, calls=%fused_computation.23 | convolution fusion | flops 2417491968 | bytes 7471104 | tf_op jit(solution)/shard_map/dot_general | solution.py:14
  138.7 6.1 %fusion.14 = bf16[1,1,768,2048]{3,2,1,0:T(8,128)(2,1)} fusion(bf16[768,768]{1,0:T(8,128)(2,1)S(1)} %copy-done.9, f32[768]{0:T(1024)S(1)} %convert_reduce_fusion, bf16[768,2176]{1,0:T(8,128)(2,1)} %bitcast.8), kind=kOutput, calls=%fused_computation.24 | convolution fusion | flops 2422210560 | bytes 7474176 | tf_op jit(solution)/shard_map/dot_general | solution.py:14
  144.8 24.6 %all-to-all-done.2 = bf16[32,24,2048]{2,1,0:T(8,128)(2,1)} async-done(((bf16[32,24,2048]{2,1,0:T(8,128)(2,1)}), bf16[32,24,2048]{2,1,0:T(8,128)(2,1)}, u32[]{:S(2)}, u32[]{:S(2)}) %all-to-all-start.2) | async-done | bytes 3145760 | tf_op jit(solution)/shard_map/all_to_all | solution.py:28
  169.3 3.8 %all-to-all-start.3 = ((bf16[32,1,24]{2,1,0:T(2,128)(2,1)}), bf16[32,1,24]{2,1,0:T(2,128)(2,1)S(1)}, u32[]{:S(2)}, u32[]{:S(2)}) async-start(bf16[32,1,24]{2,1,0:T(2,128)(2,1)} %convert_element_type.123), calls=%async_computation.3 | async-start | bytes 32768 | tf_op jit(solution)/shard_map/all_to_all | solution.py:28
  173.2 3.8 %fusion.15 = bf16[192,2048]{1,0:T(8,128)(2,1)} fusion(pred[768,192]{0,1:T(8,128)(4,1)S(1)} %fusion.16, bf16[768,2048]{1,0:T(8,128)(2,1)} %bitcast.16, bf16[1,192,2048]{2,1,0:T(8,128)(2,1)} %param.8), kind=kOutput, calls=%fused_computation.26 | convolution fusion | flops 605159424 | bytes 4866048 | tf_op jit(solution)/shard_map/dot_general | solution.py:14
  177.1 1.3 collective-permute-start
  178.3 6.2 %fusion.12 = bf16[1,1,2048,768]{3,2,1,0:T(8,128)(2,1)} fusion(bf16[768,2048]{1,0:T(8,128)(2,1)} %bitcast.4, bf16[768,768]{1,0:T(8,128)(2,1)S(1)} %copy-done.6), kind=kOutput, calls=%fused_computation.22 | convolution fusion | flops 2417491968 | bytes 7471104 | tf_op jit(solution)/shard_map/dot_general | solution.py:14
  185.6 13.4 %collective-permute-done = bf16[192,2048]{1,0:T(8,128)(2,1)} collective-permute-done((bf16[192,2048]{1,0:T(8,128)(2,1)}, bf16[192,2048]{1,0:T(8,128)(2,1)}, u32[]{:S(2)}, u32[]{:S(2)}) %collective-permute-start) | collective-permute-done | bytes 786464 | tf_op jit(solution)/shard_map/ppermute | solution.py:10
  199.0 2.1 %copy.42 = bf16[1,192,2048]{2,1,0:T(8,128)(2,1)} copy(bf16[1,192,2048]{2,1,0:T(8,128)(2,1)} %bitcast.17) | data formatting | bytes 1572864
  (42 shorter events, 6.7 us)
Async XLA Ops:
  0.6 67.6 %copy-start = (bf16[1,1,2048,768]{3,2,1,0:T(8,128)(2,1)S(1)}, bf16[1,1,2048,768]{3,2,1,0:T(8,128)(2,1)}, u32[]{:S(2)}) copy-start(bf16[1,1,2048,768]{3,2,1,0:T(8,128)(2,1)} %param.12) | copy-start | bytes 9437188
  8.1 7.7 %copy-start.1 = (bf16[1,192,2]{1,2,0:T(2,128)(2,1)S(1)}, bf16[1,192,2]{1,2,0:T(2,128)(2,1)}, u32[]{:S(2)}) copy-start(bf16[1,192,2]{1,2,0:T(2,128)(2,1)} %param.10) | copy-start | bytes 2308
  8.1 49.7 %all-to-all-start = ((bf16[32,24,2048]{2,1,0:T(8,128)(2,1)}), bf16[32,24,2048]{2,1,0:T(8,128)(2,1)}, u32[]{:S(2)}, u32[]{:S(2)}) async-start(bf16[32,24,2048]{2,1,0:T(8,128)(2,1)} %bitcast.78), calls=%async_computation | async-start | bytes 6291456 | tf_op jit(solution)/shard_map/all_to_all | solution.py:28
  57.8 49.0 %all-to-all-start.1 = ((bf16[32,24,2176]{2,1,0:T(8,128)(2,1)}), bf16[32,24,2176]{2,1,0:T(8,128)(2,1)}, u32[]{:S(2)}, u32[]{:S(2)}) async-start(bf16[32,24,2176]{2,1,0:T(8,128)(2,1)} %bitcast.77), calls=%async_computation.1 | async-start | bytes 6684672 | tf_op jit(solution)/shard_map/all_to_all | solution.py:28
  68.2 7.7 %copy-start.4 = (f32[768,768]{1,0:T(8,128)}, f32[768,768]{1,0:T(8,128)S(1)}, u32[]{:S(2)}) copy-start(f32[768,768]{1,0:T(8,128)S(1)} %fusion.7) | copy-start | bytes 7077892
  68.2 7.7 %copy-start.2 = (bf16[1,1,768,2048]{3,2,1,0:T(8,128)(2,1)S(1)}, bf16[1,1,768,2048]{3,2,1,0:T(8,128)(2,1)}, u32[]{:S(2)}) copy-start(bf16[1,1,768,2048]{3,2,1,0:T(8,128)(2,1)} %param.13) | copy-start | bytes 9437188
  75.9 4.0 %copy-start.8 = (bf16[768,768]{1,0:T(8,128)(2,1)}, bf16[768,768]{1,0:T(8,128)(2,1)S(1)}, u32[]{:S(2)}) copy-start(bf16[768,768]{1,0:T(8,128)(2,1)S(1)} %get-tuple-element.13) | copy-start | bytes 3538948
  107.9 8.0 %copy-start.3 = (bf16[1,1,2048,768]{3,2,1,0:T(8,128)(2,1)S(1)}, bf16[1,1,2048,768]{3,2,1,0:T(8,128)(2,1)}, u32[]{:S(2)}) copy-start(bf16[1,1,2048,768]{3,2,1,0:T(8,128)(2,1)} %param.11) | copy-start | bytes 9437188
  115.8 2.7 %copy-start.5 = (bf16[768,768]{1,0:T(8,128)(2,1)}, bf16[768,768]{1,0:T(8,128)(2,1)S(1)}, u32[]{:S(2)}) copy-start(bf16[768,768]{1,0:T(8,128)(2,1)S(1)} %get-tuple-element.16) | copy-start | bytes 3538948
  115.8 2.7 %copy-start.7 = (bf16[768,768]{1,0:T(8,128)(2,1)}, bf16[768,768]{1,0:T(8,128)(2,1)S(1)}, u32[]{:S(2)}) copy-start(bf16[768,768]{1,0:T(8,128)(2,1)S(1)} %get-tuple-element.15) | copy-start | bytes 3538948
  122.5 46.8 %all-to-all-start.2 = ((bf16[32,24,2048]{2,1,0:T(8,128)(2,1)}), bf16[32,24,2048]{2,1,0:T(8,128)(2,1)}, u32[]{:S(2)}, u32[]{:S(2)}) async-start(bf16[32,24,2048]{2,1,0:T(8,128)(2,1)} %bitcast.79), calls=%async_computation.2 | async-start | bytes 6291456 | tf_op jit(solution)/shard_map/all_to_all | solution.py:28
  132.0 6.7 %copy-start.9 = (bf16[768,768]{1,0:T(8,128)(2,1)S(1)}, bf16[768,768]{1,0:T(8,128)(2,1)}, u32[]{:S(2)}) copy-start(bf16[768,768]{1,0:T(8,128)(2,1)} %copy-done.8) | copy-start | bytes 3538948
  169.3 15.3 %all-to-all-start.3 = ((bf16[32,1,24]{2,1,0:T(2,128)(2,1)}), bf16[32,1,24]{2,1,0:T(2,128)(2,1)S(1)}, u32[]{:S(2)}, u32[]{:S(2)}) async-start(bf16[32,1,24]{2,1,0:T(2,128)(2,1)} %convert_element_type.123), calls=%async_computation.3 | async-start | bytes 32768 | tf_op jit(solution)/shard_map/all_to_all | solution.py:28
  173.2 5.1 %copy-start.6 = (bf16[768,768]{1,0:T(8,128)(2,1)S(1)}, bf16[768,768]{1,0:T(8,128)(2,1)}, u32[]{:S(2)}) copy-start(bf16[768,768]{1,0:T(8,128)(2,1)} %copy-done.5) | copy-start | bytes 3538948
  177.1 22.0 %collective-permute-start = (bf16[192,2048]{1,0:T(8,128)(2,1)}, bf16[192,2048]{1,0:T(8,128)(2,1)}, u32[]{:S(2)}, u32[]{:S(2)}) collective-permute-start(bf16[192,2048]{1,0:T(8,128)(2,1)} %fusion.15), channel_id=1, source_target_pairs={{32,0},{64,32},{96,64},{33,1},{65,33},{97,65},{34,2},{66,34},{98,6... | collective-permute-start | bytes 2359304 | tf_op jit(solution)/shard_map/ppermute | solution.py:10
